TPU v7x, 32 devices: a whole 2x2x4 slice. The times are simulated.
32 devices in a mesh: elem: 4 (over y, x), grp: 8 (over z, core).
Axes of the slice: x: 2, y: 2, z: 4, core: 2. Of those that a mesh axis runs over, the one named last changes fastest.
Arguments:
- params: bfloat16 [12, 32768], P(None, ('elem', 'grp')), may hold values from -0.796875 to 1
- profiles: bfloat16 [32768, 512], P(('elem', 'grp')), may hold values from 0 to 2
- weights: bfloat16 [32768], P(('elem', 'grp')), may hold values from 0.099609375 to 1
- destinations: int32 [32768], P(('elem', 'grp')), may hold values from 0 to 3, as said below
- table: int32 [1024, 12], replicated, may hold values from 0 to 3
Outputs:
- gram: float32 [4, 1024, 1024], P('elem', 'grp')
- moment: float32 [4, 1024, 512], P('elem', 'grp')
Inputs may be any that keep to these rules, and one draw needn't show every extreme that they name: `destinations`: of the 1024 samples of one device at most 512 name one element. For every index of grp, one element drawn from the seed is named by exactly 512 samples of each of the 4 devices with that index.
All inputs are finite; a program needn't handle non-finite values.
Results may differ from a plain program's by a relative error of at most 0.0039.
Values may be sent and summed in bfloat16 or wider, within the bound.
No kernel may reach another device: no remote copies, remote signals or barrier semaphores. Data moves between devices by JAX's collectives and lax.ppermute only.
A program may use at most 128 MiB of HBM per device.

v0:
```python
import functools

import numpy as np
import jax
import jax.numpy as jnp
from jax import lax
from jax.sharding import PartitionSpec as P
from jax.experimental import pallas as pl
from jax.experimental.pallas import tpu as pltpu

LEVELS = 4
GROUP = 3


def split3(x):
    hi = x.astype(jnp.bfloat16)
    rest = x - hi.astype(jnp.float32)
    mid = rest.astype(jnp.bfloat16)
    lo = (rest - mid.astype(jnp.float32)).astype(jnp.bfloat16)
    return jnp.concatenate([hi, mid, lo], axis=0)


def term_maps(table, rows):
    npar = table.shape[1]
    width = LEVELS ** GROUP
    n_groups = -(-npar // GROUP)
    maps = []
    for start in range(0, n_groups * GROUP, GROUP):
        code = jnp.zeros((table.shape[0],), jnp.int32)
        for j in range(start, start + GROUP):
            code = code * LEVELS + (table[:, j] if j < npar else 0)
        onehot = (code[:, None] == jnp.arange(width, dtype=jnp.int32)[None, :]).astype(jnp.bfloat16)
        maps.append(jnp.concatenate([onehot] * 3, axis=1))
    pick = np.zeros((GROUP, n_groups * width, 3 * LEVELS * rows), np.float32)
    for g in range(n_groups):
        for c in range(width):
            for pos in range(GROUP):
                j = g * GROUP + pos
                degree = (c // LEVELS ** (GROUP - 1 - pos)) % LEVELS
                col = degree * rows + j if j < npar else 0
                for piece in range(3):
                    pick[pos, g * width + c, piece * LEVELS * rows + col] = 1.0
    return jnp.stack(maps), jnp.asarray(pick, jnp.bfloat16)


def gram_kernel(m_ref, pick_ref, oh_ref, ohr_ref, gram_ref, *wt_refs, npar):
    @pl.when(pl.program_id(0) == 0)
    def _():
        gram_ref[...] = jnp.zeros_like(gram_ref)

    coords = m_ref[...].astype(jnp.float32)
    values = [jnp.ones_like(coords), coords]
    for degree in range(1, LEVELS - 1):
        nxt = ((2.0 * degree + 1.0) * coords * values[-1] - degree * values[-2]) / (degree + 1.0)
        values.append(nxt)
    stacked = jnp.concatenate(
        [values[d] * float(np.sqrt(np.float32(2 * d + 1))) for d in range(LEVELS)], axis=0
    )
    pieces = split3(stacked)
    combos = None
    for pos in range(pick_ref.shape[0]):
        factor = jnp.dot(pick_ref[pos], pieces, preferred_element_type=jnp.float32)
        combos = factor if combos is None else combos * factor
    groups = oh_ref.shape[0]
    width = combos.shape[0] // groups
    basis = None
    rows = None
    for g in range(groups):
        piece = split3(combos[g * width:(g + 1) * width])
        factor = jnp.dot(oh_ref[g], piece, preferred_element_type=jnp.float32)
        part = jnp.dot(ohr_ref[g], piece, preferred_element_type=jnp.float32)
        basis = factor if basis is None else basis * factor
        rows = part if rows is None else rows * part
    w = coords[npar:npar + 1]
    low = basis.astype(jnp.bfloat16)
    weighted_rows = (w * rows).astype(jnp.bfloat16)
    gram_ref[...] += lax.dot_general(
        weighted_rows, low, (((1,), (1,)), ((), ())), preferred_element_type=jnp.float32
    )
    if wt_refs:
        wt_refs[0][...] = (w * basis).astype(jnp.bfloat16)


def gram_rows(meta, pick, rhs, rhs_rows, npar, with_weighted, block=256):
    rows, samples = meta.shape
    groups, terms, width3 = rhs.shape
    picked = rhs_rows.shape[1]
    out_specs = [pl.BlockSpec((picked, terms), lambda i: (0, 0))]
    out_shape = [jax.ShapeDtypeStruct((picked, terms), jnp.float32)]
    if with_weighted:
        out_specs.append(pl.BlockSpec((terms, block), lambda i: (0, i)))
        out_shape.append(jax.ShapeDtypeStruct((terms, samples), jnp.bfloat16))
    return pl.pallas_call(
        functools.partial(gram_kernel, npar=npar),
        grid=(samples // block,),
        in_specs=[
            pl.BlockSpec((rows, block), lambda i: (0, i)),
            pl.BlockSpec(pick.shape, lambda i: (0, 0, 0)),
            pl.BlockSpec((groups, terms, width3), lambda i: (0, 0, 0)),
            pl.BlockSpec((groups, picked, width3), lambda i: (0, 0, 0)),
        ],
        out_specs=out_specs,
        out_shape=out_shape,
        compiler_params=pltpu.CompilerParams(
            dimension_semantics=("arbitrary",), vmem_limit_bytes=48 * 1024 * 1024
        ),
    )(meta, pick, rhs, rhs_rows)


def on_device(params, profiles, weights, destinations, table):
    groups = lax.axis_size("elem")
    members = lax.axis_size("grp")
    samples = destinations.shape[0]
    cap = samples // 2
    scale = 1.0 / (members * samples)

    mine = destinations[:, None] == jnp.arange(groups, dtype=jnp.int32)[None, :]
    idx = jnp.arange(samples, dtype=jnp.int32)
    earlier = (idx[:, None] > idx[None, :]).astype(jnp.bfloat16)
    counts = jnp.dot(earlier, mine.astype(jnp.bfloat16), preferred_element_type=jnp.float32)
    slot = jnp.sum(jnp.where(mine, counts, 0.0), axis=1).astype(jnp.int32)
    sel = mine.T[:, None, :] & (slot[None, None, :] == jnp.arange(cap, dtype=jnp.int32)[None, :, None])
    sel = sel.astype(jnp.bfloat16)

    prof_c = jnp.einsum("eis,sq->eiq", sel, profiles, preferred_element_type=jnp.float32).astype(jnp.bfloat16)
    prof_r = lax.all_to_all(prof_c, "elem", 0, 0, tiled=True)
    meta = jnp.concatenate([params, weights[None, :]], axis=0)
    meta_c = jnp.einsum("eis,js->eji", sel, meta, preferred_element_type=jnp.float32).astype(jnp.bfloat16)
    meta_r = lax.all_to_all(meta_c, "elem", 0, 0, tiled=True)

    npar = params.shape[0]
    q = profiles.shape[1]
    terms = table.shape[0]
    slots = groups * cap
    rows = -(-(npar + 1) // 16) * 16
    prof_r = prof_r.reshape(slots, q)
    meta_r = jnp.transpose(meta_r, (1, 0, 2)).reshape(npar + 1, slots)
    meta_r = jnp.pad(meta_r, ((0, rows - npar - 1), (0, 0)))

    me = lax.axis_index("grp")
    core = me % 2
    chip = me // 2
    pairs = members // 2
    own_rows = terms // members
    others = [
        lax.ppermute(meta_r, "grp", [(i, (i + 2 * k) % members) for i in range(members)])
        for k in range(1, pairs)
    ]
    rhs, pick = term_maps(table, rows)
    rhs_rows = lax.dynamic_slice_in_dim(rhs, chip * 2 * own_rows, 2 * own_rows, axis=1)
    gram_own, weighted_t = gram_rows(meta_r, pick, rhs, rhs_rows, npar, True)
    moment_part = jnp.dot(weighted_t, prof_r, preferred_element_type=jnp.float32)
    moment_rows = lax.psum_scatter(moment_part, "grp", scatter_dimension=0, tiled=True) * scale
    (gram_oth,) = gram_rows(jnp.concatenate(others, axis=1), pick, rhs, rhs_rows, npar, False)
    gram_chip = gram_own + gram_oth
    keep = lax.dynamic_slice_in_dim(gram_chip, core * own_rows, own_rows, axis=0)
    send = lax.dynamic_slice_in_dim(gram_chip, (1 - core) * own_rows, own_rows, axis=0)
    recv = lax.ppermute(send, "grp", [(i, i ^ 1) for i in range(members)])
    gram_out = (keep + recv) * scale
    return (gram_out[None], moment_rows[None])


def solution(mesh):
    in_specs = (
        P(None, ("elem", "grp")),
        P(("elem", "grp"), None),
        P(("elem", "grp")),
        P(("elem", "grp")),
        P(),
    )
    out_specs = (P("elem", "grp", None), P("elem", "grp", None))

    return jax.shard_map(on_device, mesh=mesh, in_specs=in_specs, out_specs=out_specs, check_vma=False)
```

profile of v0, /device:TPU:0, one launch (start us, length us, event | category | flops | bytes accessed | tf_op | source)
XLA Modules:
  0.0 112.2 jit_solution(6193782085335576429)
XLA Ops:
  7.2 1.3 %fusion.19 = f32[1024]{0:T(1024)S(1)} fusion(s32[1024]{0:T(1024)} %param.9), kind=kOutput, calls=%fused_computation.16 | convolution fusion | flops 9452544 | bytes 8192 | tf_op jit(solution)/shard_map/dot_general | solution.py:120
  8.5 0.7 iota_compare_fusion.12
  9.5 0.7 broadcast_in_dim.10
  10.2 2.6 %fusion.15 = bf16[4,13,512]{2,1,0:T(8,128)(2,1)} fusion(pred[512,1024]{1,0:T(8,128)(4,1)S(1)} %iota_compare_fusion.2, pred[4,1024]{1,0:T(4,128)(4,1)S(1)} %iota_compare_fusion.12, bf16[1,1024]{1,0:T(2,128)(2,1)S(1)} %broadcast_in_dim.10, bf16[12,1024]{1,0:T(8,128)(2,1)} %param.6), kind=kOutput, calls=%fused_computation.14 | convolution fusion | flops 56702976 | bytes 608256 | tf_op jit(solution)/shard_map/eis,js->eji/dot_general | solution.py:128
  12.8 5.2 %all-to-all-start = ((bf16[4,13,512]{2,1,0:T(8,128)(2,1)}), bf16[4,13,512]{2,1,0:T(8,128)(2,1)S(1)}, u32[]{:S(2)}, u32[]{:S(2)}) async-start(bf16[4,13,512]{2,1,0:T(8,128)(2,1)} %fusion.15), calls=%async_computation | async-start | bytes 131072 | tf_op jit(solution)/shard_map/all_to_all | solution.py:129
  18.0 3.7 %fusion.9 = bf16[4,512,512]{2,1,0:T(8,128)(2,1)} fusion(pred[512,1024]{1,0:T(8,128)(4,1)S(1)} %iota_compare_fusion.2, pred[4,1024]{1,0:T(4,128)(4,1)S(1)} %iota_compare_fusion.12, bf16[1024,512]{1,0:T(8,128)(2,1)S(1)} %copy-done), kind=kOutput, calls=%fused_computation.12 | convolution fusion | flops 2150629376 | bytes 3674112 | tf_op jit(solution)/shard_map/eis,sq->eiq/dot_general | solution.py:125
  21.7 1.1 %all-to-all-done = bf16[4,13,512]{2,1,0:T(8,128)(2,1)S(1)} async-done(((bf16[4,13,512]{2,1,0:T(8,128)(2,1)}), bf16[4,13,512]{2,1,0:T(8,128)(2,1)S(1)}, u32[]{:S(2)}, u32[]{:S(2)}) %all-to-all-start) | async-done | bytes 53280 | tf_op jit(solution)/shard_map/all_to_all | solution.py:129
  22.8 4.5 %all-to-all-start.1 = ((bf16[4,512,512]{2,1,0:T(8,128)(2,1)}), bf16[4,512,512]{2,1,0:T(8,128)(2,1)}, u32[]{:S(2)}, u32[]{:S(2)}) async-start(bf16[4,512,512]{2,1,0:T(8,128)(2,1)} %fusion.9), calls=%async_computation.1 | async-start | bytes 4194304 | tf_op jit(solution)/shard_map/all_to_all | solution.py:126
  30.6 10.9 %shard_map.77 = (f32[256,1024]{1,0:T(8,128)S(1)}, bf16[1024,2048]{1,0:T(8,128)(2,1)}) custom-call(bf16[16,2048]{1,0:T(8,128)(2,1)S(1)} %pad.4.m_ref, bf16[3,256,192]{2,1,0:T(8,128)(2,1)S(1)} %copy-done.3, bf16[4,1024,192]{2,1,0:T(8,128)(2,1)S(1)} %add_convert_fusion.oh_ref, bf16[4,256,192]{2,1,0:T(8,128)(2,1)S(1)} %constant_dynamic-slice_fusion.1.ohr_ref), custom_call_target="tpu_custom_call" | custom-call | tf_op jit(solution)/shard_map/pallas_call | solution.py:93
  41.5 0.8 copy-done.1
  42.3 1.1 copy-done.4
  44.0 7.2 %all-to-all-done.1 = bf16[4,512,512]{2,1,0:T(8,128)(2,1)} async-done(((bf16[4,512,512]{2,1,0:T(8,128)(2,1)}), bf16[4,512,512]{2,1,0:T(8,128)(2,1)}, u32[]{:S(2)}, u32[]{:S(2)}) %all-to-all-start.1) | async-done | bytes 2097184 | tf_op jit(solution)/shard_map/all_to_all | solution.py:126
  51.2 6.6 %fusion.25 = f32[1024,512]{1,0:T(8,128)} fusion(bf16[1024,2048]{1,0:T(8,128)(2,1)} %get-tuple-element.5, bf16[2048,512]{1,0:T(8,128)(2,1)} %bitcast.13), kind=kOutput, calls=%fused_computation.42 | convolution fusion | flops 2147483648 | bytes 8388608 | tf_op jit(solution)/shard_map/dot_general | solution.py:152
  57.8 3.6 %collective-permute-start.2 = (bf16[16,2048]{1,0:T(8,128)(2,1)}, bf16[16,2048]{1,0:T(8,128)(2,1)}, u32[]{:S(2)}, u32[]{:S(2)}) collective-permute-start(bf16[16,2048]{1,0:T(8,128)(2,1)} %copy-done.6), channel_id=1, source_target_pairs={{0,6},{1,7},{2,0},{3,1},{4,2},{5,3},{6,4},{7,5},{8,14},{9,15},{10,... | collective-permute-start | bytes 196616 | tf_op jit(solution)/shard_map/ppermute | solution.py:146
  61.5 1.0 collective-permute-start
  62.5 1.3 %collective-permute-done.2 = bf16[16,2048]{1,0:T(8,128)(2,1)} collective-permute-done((bf16[16,2048]{1,0:T(8,128)(2,1)}, bf16[16,2048]{1,0:T(8,128)(2,1)}, u32[]{:S(2)}, u32[]{:S(2)}) %collective-permute-start.2) | collective-permute-done | bytes 65568 | tf_op jit(solution)/shard_map/ppermute | solution.py:146
  63.8 3.2 %collective-permute-done.1 = bf16[16,2048]{1,0:T(8,128)(2,1)} collective-permute-done((bf16[16,2048]{1,0:T(8,128)(2,1)}, bf16[16,2048]{1,0:T(8,128)(2,1)}, u32[]{:S(2)}, u32[]{:S(2)}) %collective-permute-start.1) | collective-permute-done | bytes 65568 | tf_op jit(solution)/shard_map/ppermute | solution.py:146
  67.0 0.9 collective-permute-done
  67.9 0.9 pad_maximum_fusion.m_ref
  68.8 1.0 copy-done.2
  69.8 30.8 %shard_map.78 = f32[256,1024]{1,0:T(8,128)S(1)} custom-call(bf16[16,6144]{1,0:T(8,128)(2,1)S(1)} %pad_maximum_fusion.m_ref, bf16[3,256,192]{2,1,0:T(8,128)(2,1)S(1)} %copy-done.3, bf16[4,1024,192]{2,1,0:T(8,128)(2,1)S(1)} %add_convert_fusion.oh_ref, bf16[4,256,192]{2,1,0:T(8,128)(2,1)S(1)} %copy-done.2), custom_call_target="tpu_custom_call" | custom-call | tf_op jit(solution)/shard_map/pallas_call | solution.py:93
  100.9 1.9 %collective-permute-done.3 = f32[128,1024]{1,0:T(8,128)S(1)} collective-permute-done((f32[128,1024]{1,0:T(8,128)S(1)}, f32[128,1024]{1,0:T(8,128)S(1)}, u32[]{:S(2)}, u32[]{:S(2)}) %collective-permute-start.3) | collective-permute-done | bytes 524320 | tf_op jit(solution)/shard_map/ppermute | solution.py:158
  102.8 0.9 multiply_bitcast_fusion
  103.7 1.7 %multiply_bitcast_fusion.1 = f32[1,128,512]{2,1,0:T(8,128)} fusion(f32[128,512]{1,0:T(8,128)} %reduce-scatter.2.cloned.1.call-done), kind=kLoop, calls=%fused_computation.27 | loop fusion | flops 65536 | bytes 524288 | tf_op jit(solution)/shard_map/broadcast_in_dim | solution.py:160
  (39 shorter events, 4.4 us)
Async XLA Ops:
  7.2 10.8 %copy-start = (bf16[1024,512]{1,0:T(8,128)(2,1)S(1)}, bf16[1024,512]{1,0:T(8,128)(2,1)}, u32[]{:S(2)}) copy-start(bf16[1024,512]{1,0:T(8,128)(2,1)} %param.7) | copy-start | bytes 3145732
  12.8 10.0 %all-to-all-start = ((bf16[4,13,512]{2,1,0:T(8,128)(2,1)}), bf16[4,13,512]{2,1,0:T(8,128)(2,1)S(1)}, u32[]{:S(2)}, u32[]{:S(2)}) async-start(bf16[4,13,512]{2,1,0:T(8,128)(2,1)} %fusion.15), calls=%async_computation | async-start | bytes 131072 | tf_op jit(solution)/shard_map/all_to_all | solution.py:129
  21.7 5.7 %copy-start.9 = (s32[1024,12]{0,1:T(8,128)S(1)}, s32[1024,12]{0,1:T(8,128)}, u32[]{:S(2)}) copy-start(s32[1024,12]{0,1:T(8,128)} %param.10) | copy-start | bytes 147460
  22.8 4.6 %copy-start.7 = (bf16[4,13,512]{2,1,0:T(8,128)(2,1)}, bf16[4,13,512]{2,1,0:T(8,128)(2,1)S(1)}, u32[]{:S(2)}) copy-start(bf16[4,13,512]{2,1,0:T(8,128)(2,1)S(1)} %all-to-all-done) | copy-start | bytes 159748
  22.8 28.4 %all-to-all-start.1 = ((bf16[4,512,512]{2,1,0:T(8,128)(2,1)}), bf16[4,512,512]{2,1,0:T(8,128)(2,1)}, u32[]{:S(2)}, u32[]{:S(2)}) async-start(bf16[4,512,512]{2,1,0:T(8,128)(2,1)} %fusion.9), calls=%async_computation.1 | async-start | bytes 4194304 | tf_op jit(solution)/shard_map/all_to_all | solution.py:126
  27.3 76.4 %reduce-scatter.2.cloned.1.call-start = ((), (), s32[]{:S(2)}) async-start(), calls=%async_computation.3 | async-start | bytes 2359296 | tf_op jit(solution)/shard_map/reduce_scatter | solution.py:153
  29.5 0.8 copy-start.8
  29.5 1.0 copy-start.3
  41.5 0.8 copy-start.1
  42.3 1.1 copy-start.4
  43.4 0.6 copy-start.6
  57.8 6.0 %collective-permute-start.2 = (bf16[16,2048]{1,0:T(8,128)(2,1)}, bf16[16,2048]{1,0:T(8,128)(2,1)}, u32[]{:S(2)}, u32[]{:S(2)}) collective-permute-start(bf16[16,2048]{1,0:T(8,128)(2,1)} %copy-done.6), channel_id=1, source_target_pairs={{0,6},{1,7},{2,0},{3,1},{4,2},{5,3},{6,4},{7,5},{8,14},{9,15},{10,... | collective-permute-start | bytes 196616 | tf_op jit(solution)/shard_map/ppermute | solution.py:146
  61.5 5.5 %collective-permute-start.1 = (bf16[16,2048]{1,0:T(8,128)(2,1)}, bf16[16,2048]{1,0:T(8,128)(2,1)}, u32[]{:S(2)}, u32[]{:S(2)}) collective-permute-start(bf16[16,2048]{1,0:T(8,128)(2,1)} %copy-done.6), channel_id=1, source_target_pairs={{0,4},{1,5},{2,6},{3,7},{4,0},{5,1},{6,2},{7,3},{8,12},{9,13},{10,... | collective-permute-start | bytes 196616 | tf_op jit(solution)/shard_map/ppermute | solution.py:146
  61.5 6.4 %collective-permute-start = (bf16[16,2048]{1,0:T(8,128)(2,1)}, bf16[16,2048]{1,0:T(8,128)(2,1)}, u32[]{:S(2)}, u32[]{:S(2)}) collective-permute-start(bf16[16,2048]{1,0:T(8,128)(2,1)} %copy-done.6), channel_id=1, source_target_pairs={{0,2},{1,3},{2,4},{3,5},{4,6},{5,7},{6,0},{7,1},{8,10},{9,11},{10,... | collective-permute-start | bytes 196616 | tf_op jit(solution)/shard_map/ppermute | solution.py:146
  68.8 1.0 copy-start.2
  69.8 30.8 %copy-start.5 = (f32[256,1024]{1,0:T(8,128)S(1)}, f32[256,1024]{1,0:T(8,128)}, u32[]{:S(2)}) copy-start(f32[256,1024]{1,0:T(8,128)} %copy-done.4) | copy-start | bytes 3145732
  100.8 2.0 %collective-permute-start.3 = (f32[128,1024]{1,0:T(8,128)S(1)}, f32[128,1024]{1,0:T(8,128)S(1)}, u32[]{:S(2)}, u32[]{:S(2)}) collective-permute-start(f32[128,1024]{1,0:T(8,128)S(1)} %constant_dynamic-slice_fusion), channel_id=1, source_target_pairs={{0,1},{1,0},{2,3},{3,2},{4,5},{5,4},{6,7},{7,6},{8,9},{9,8},{10,11... | collective-permute-start | bytes 1572872 | tf_op jit(solution)/shard_map/ppermute | solution.py:158
Sparse Core Ops, SparseCore 0:
  57.9 36.3 reduce-scatter.1
where the time goes:
time: 113 us; the launch traced here: 112 us
  Pallas kernels  41.7 us (37%)
  waiting for transfers between devices  15.7 us (14%)
  starting transfers between devices  14.4 us (13%)
  between operations  14.3 us (13%)
  matrix products  14.2 us (13%)
  other arithmetic  7.18 us (6%)
  local copies, waits for them, and re-layouts  4.76 us (4%)
    pallas_call x2, Pallas kernels, gram_rows(): pl.pallas_call(functools.partial(gram_kernel, npar=npar), grid=(samples /...  41.7 us
    all_to_all x1, waiting for transfers between devices, on_device(): prof_r = lax.all_to_all(prof_c, 'elem', 0, 0, tiled=True)  7.24 us
    dot_general x1, matrix products, on_device(): jnp.dot(weighted_t, prof_r, preferred_element_type=jnp.float32)  6.55 us
    ppermute x3, waiting for transfers between devices, on_device(): lax.ppermute(meta_r, 'grp', [(i, (i + 2 * k) % members) for i in range(me...  5.37 us
    all_to_all x1, starting transfers between devices, on_device(): meta_r = lax.all_to_all(meta_c, 'elem', 0, 0, tiled=True)  5.19 us
    ppermute x3, starting transfers between devices, on_device(): lax.ppermute(meta_r, 'grp', [(i, (i + 2 * k) % members) for i in range(me...  4.68 us
    all_to_all x1, starting transfers between devices, on_device(): prof_r = lax.all_to_all(prof_c, 'elem', 0, 0, tiled=True)  4.45 us
    unnamed x22, local copies, waits for them, and re-layouts  3.92 us
  transfers between devices with their start and end apart: 7, of which 6 were waited for; matrix products, arithmetic and copies ran while one was open for 7% of the time, Pallas kernels for 37%

commit v1 on v0

--- a/solution.py
+++ b/solution.py
@@ -149,9 +149,13 @@
     rhs, pick = term_maps(table, rows)
     rhs_rows = lax.dynamic_slice_in_dim(rhs, chip * 2 * own_rows, 2 * own_rows, axis=1)
     gram_own, weighted_t = gram_rows(meta_r, pick, rhs, rhs_rows, npar, True)
+    (gram_first,) = gram_rows(others[0], pick, rhs, rhs_rows, npar, False)
+    gram_oth = gram_first
     moment_part = jnp.dot(weighted_t, prof_r, preferred_element_type=jnp.float32)
     moment_rows = lax.psum_scatter(moment_part, "grp", scatter_dimension=0, tiled=True) * scale
-    (gram_oth,) = gram_rows(jnp.concatenate(others, axis=1), pick, rhs, rhs_rows, npar, False)
+    if len(others) > 1:
+        (gram_rest,) = gram_rows(jnp.concatenate(others[1:], axis=1), pick, rhs, rhs_rows, npar, False)
+        gram_oth = gram_oth + gram_rest
     gram_chip = gram_own + gram_oth
     keep = lax.dynamic_slice_in_dim(gram_chip, core * own_rows, own_rows, axis=0)
     send = lax.dynamic_slice_in_dim(gram_chip, (1 - core) * own_rows, own_rows, axis=0)

time: 113 us -> 110 us (0.973)
  waiting for transfers between devices: 15.7 us -> 12.8 us
    ppermute x3, waiting for transfers between devices: 5.37 us -> 2.56 us  [on_device(): lax.ppermute(meta_r, 'grp', [(i, (i + 2 * k) % members) for i in range(me...]
    pallas_call x2 -> x3, Pallas kernels: 41.7 us -> 41.8 us  [gram_rows(): pl.pallas_call(functools.partial(gram_kernel, npar=npar), grid=(samples /...]
  transfers between devices with their start and end apart: 7 -> 7, of which waited for: 6 -> 5; matrix products, arithmetic and copies ran while one was open for 7% -> 8% of each run, Pallas kernels for 37% -> 38%
where the time goes in v1:
time: 110 us
  Pallas kernels  41.8 us (38%)
  starting transfers between devices  14.4 us (13%)
  between operations  14.3 us (13%)
  matrix products  14.2 us (13%)
  waiting for transfers between devices  12.8 us (12%)
  other arithmetic  7.28 us (7%)
  local copies, waits for them, and re-layouts  4.75 us (4%)
    pallas_call x3, Pallas kernels, gram_rows(): pl.pallas_call(functools.partial(gram_kernel, npar=npar), grid=(samples /...  41.8 us
    all_to_all x1, waiting for transfers between devices, on_device(): prof_r = lax.all_to_all(prof_c, 'elem', 0, 0, tiled=True)  7.24 us
    dot_general x1, matrix products, on_device(): jnp.dot(weighted_t, prof_r, preferred_element_type=jnp.float32)  6.55 us
    all_to_all x1, starting transfers between devices, on_device(): meta_r = lax.all_to_all(meta_c, 'elem', 0, 0, tiled=True)  5.19 us
    ppermute x3, starting transfers between devices, on_device(): lax.ppermute(meta_r, 'grp', [(i, (i + 2 * k) % members) for i in range(me...  4.69 us
    all_to_all x1, starting transfers between devices, on_device(): prof_r = lax.all_to_all(prof_c, 'elem', 0, 0, tiled=True)  4.45 us
    unnamed x22, local copies, waits for them, and re-layouts  3.91 us
    dot_general x1, matrix products, on_device(): jnp.einsum('eis,sq->eiq', sel, profiles, preferred_element_type=jnp.float32)  3.7 us
  transfers between devices with their start and end apart: 7, of which 5 were waited for; matrix products, arithmetic and copies ran while one was open for 8% of the time, Pallas kernels for 38%

profile of v1, /device:TPU:0, one launch (start us, length us, event | category | flops | bytes accessed | tf_op | source)
XLA Modules:
  0.0 109.6 jit_solution(14007857034350163866)
XLA Ops:
  7.2 1.3 %fusion.19 = f32[1024]{0:T(1024)S(1)} fusion(s32[1024]{0:T(1024)} %param.9), kind=kOutput, calls=%fused_computation.16 | convolution fusion | flops 9452544 | bytes 8192 | tf_op jit(solution)/shard_map/dot_general | solution.py:120
  8.5 0.7 iota_compare_fusion.12
  9.5 0.7 broadcast_in_dim.10
  10.2 2.6 %fusion.15 = bf16[4,13,512]{2,1,0:T(8,128)(2,1)} fusion(pred[512,1024]{1,0:T(8,128)(4,1)S(1)} %iota_compare_fusion.2, pred[4,1024]{1,0:T(4,128)(4,1)S(1)} %iota_compare_fusion.12, bf16[1,1024]{1,0:T(2,128)(2,1)S(1)} %broadcast_in_dim.10, bf16[12,1024]{1,0:T(8,128)(2,1)} %param.6), kind=kOutput, calls=%fused_computation.14 | convolution fusion | flops 56702976 | bytes 608256 | tf_op jit(solution)/shard_map/eis,js->eji/dot_general | solution.py:128
  12.8 5.2 %all-to-all-start = ((bf16[4,13,512]{2,1,0:T(8,128)(2,1)}), bf16[4,13,512]{2,1,0:T(8,128)(2,1)S(1)}, u32[]{:S(2)}, u32[]{:S(2)}) async-start(bf16[4,13,512]{2,1,0:T(8,128)(2,1)} %fusion.15), calls=%async_computation | async-start | bytes 131072 | tf_op jit(solution)/shard_map/all_to_all | solution.py:129
  18.0 3.7 %fusion.9 = bf16[4,512,512]{2,1,0:T(8,128)(2,1)} fusion(pred[512,1024]{1,0:T(8,128)(4,1)S(1)} %iota_compare_fusion.2, pred[4,1024]{1,0:T(4,128)(4,1)S(1)} %iota_compare_fusion.12, bf16[1024,512]{1,0:T(8,128)(2,1)S(1)} %copy-done), kind=kOutput, calls=%fused_computation.12 | convolution fusion | flops 2150629376 | bytes 3674112 | tf_op jit(solution)/shard_map/eis,sq->eiq/dot_general | solution.py:125
  21.7 1.1 %all-to-all-done = bf16[4,13,512]{2,1,0:T(8,128)(2,1)S(1)} async-done(((bf16[4,13,512]{2,1,0:T(8,128)(2,1)}), bf16[4,13,512]{2,1,0:T(8,128)(2,1)S(1)}, u32[]{:S(2)}, u32[]{:S(2)}) %all-to-all-start) | async-done | bytes 53280 | tf_op jit(solution)/shard_map/all_to_all | solution.py:129
  22.8 4.5 %all-to-all-start.1 = ((bf16[4,512,512]{2,1,0:T(8,128)(2,1)}), bf16[4,512,512]{2,1,0:T(8,128)(2,1)}, u32[]{:S(2)}, u32[]{:S(2)}) async-start(bf16[4,512,512]{2,1,0:T(8,128)(2,1)} %fusion.9), calls=%async_computation.1 | async-start | bytes 4194304 | tf_op jit(solution)/shard_map/all_to_all | solution.py:126
  30.6 10.9 %shard_map.77 = (f32[256,1024]{1,0:T(8,128)S(1)}, bf16[1024,2048]{1,0:T(8,128)(2,1)}) custom-call(bf16[16,2048]{1,0:T(8,128)(2,1)S(1)} %pad.4.m_ref, bf16[3,256,192]{2,1,0:T(8,128)(2,1)S(1)} %copy-done.3, bf16[4,1024,192]{2,1,0:T(8,128)(2,1)S(1)} %add_convert_fusion.oh_ref, bf16[4,256,192]{2,1,0:T(8,128)(2,1)S(1)} %constant_dynamic-slice_fusion.1.ohr_ref), custom_call_target="tpu_custom_call" | custom-call | tf_op jit(solution)/shard_map/pallas_call | solution.py:93
  41.5 0.8 copy-done.1
  42.3 1.1 copy-done.4
  44.0 7.2 %all-to-all-done.1 = bf16[4,512,512]{2,1,0:T(8,128)(2,1)} async-done(((bf16[4,512,512]{2,1,0:T(8,128)(2,1)}), bf16[4,512,512]{2,1,0:T(8,128)(2,1)}, u32[]{:S(2)}, u32[]{:S(2)}) %all-to-all-start.1) | async-done | bytes 2097184 | tf_op jit(solution)/shard_map/all_to_all | solution.py:126
  51.2 6.5 %fusion.25 = f32[1024,512]{1,0:T(8,128)} fusion(bf16[1024,2048]{1,0:T(8,128)(2,1)} %get-tuple-element.5, bf16[2048,512]{1,0:T(8,128)(2,1)} %bitcast.13), kind=kOutput, calls=%fused_computation.43 | convolution fusion | flops 2147483648 | bytes 8388608 | tf_op jit(solution)/shard_map/dot_general | solution.py:154
  57.8 2.7 %collective-permute-start.1 = (bf16[16,2048]{1,0:T(8,128)(2,1)}, bf16[16,2048]{1,0:T(8,128)(2,1)}, u32[]{:S(2)}, u32[]{:S(2)}) collective-permute-start(bf16[16,2048]{1,0:T(8,128)(2,1)} %copy-done.6), channel_id=1, source_target_pairs={{0,4},{1,5},{2,6},{3,7},{4,0},{5,1},{6,2},{7,3},{8,12},{9,13},{10,... | collective-permute-start | bytes 196616 | tf_op jit(solution)/shard_map/ppermute | solution.py:146
  60.5 1.3 %collective-permute-start.2 = (bf16[16,2048]{1,0:T(8,128)(2,1)}, bf16[16,2048]{1,0:T(8,128)(2,1)}, u32[]{:S(2)}, u32[]{:S(2)}) collective-permute-start(bf16[16,2048]{1,0:T(8,128)(2,1)} %copy-done.6), channel_id=1, source_target_pairs={{0,6},{1,7},{2,0},{3,1},{4,2},{5,3},{6,4},{7,5},{8,14},{9,15},{10,... | collective-permute-start | bytes 196616 | tf_op jit(solution)/shard_map/ppermute | solution.py:146
  62.5 1.0 collective-permute-done.1
  63.5 1.5 %collective-permute-done.2 = bf16[16,2048]{1,0:T(8,128)(2,1)} collective-permute-done((bf16[16,2048]{1,0:T(8,128)(2,1)}, bf16[16,2048]{1,0:T(8,128)(2,1)}, u32[]{:S(2)}, u32[]{:S(2)}) %collective-permute-start.2) | collective-permute-done | bytes 65568 | tf_op jit(solution)/shard_map/ppermute | solution.py:146
  65.0 0.9 pad_maximum_fusion.m_ref
  65.9 1.0 copy-done.2
  67.0 20.5 %shard_map.79 = f32[256,1024]{1,0:T(8,128)S(1)} custom-call(bf16[16,4096]{1,0:T(8,128)(2,1)S(1)} %pad_maximum_fusion.m_ref, bf16[3,256,192]{2,1,0:T(8,128)(2,1)S(1)} %copy-done.3, bf16[4,1024,192]{2,1,0:T(8,128)(2,1)S(1)} %add_convert_fusion.oh_ref, bf16[4,256,192]{2,1,0:T(8,128)(2,1)S(1)} %copy-done.2), custom_call_target="tpu_custom_call" | custom-call | tf_op jit(solution)/shard_map/pallas_call | solution.py:93
  87.5 10.3 %shard_map.78 = f32[256,1024]{1,0:T(8,128)S(1)} custom-call(bf16[16,2048]{1,0:T(8,128)(2,1)S(1)} %collective-permute-done.m_ref, bf16[3,256,192]{2,1,0:T(8,128)(2,1)S(1)} %copy-done.3, bf16[4,1024,192]{2,1,0:T(8,128)(2,1)S(1)} %add_convert_fusion.oh_ref, bf16[4,256,192]{2,1,0:T(8,128)(2,1)S(1)} %copy-done.2), custom_call_target="tpu_custom_call" | custom-call | tf_op jit(solution)/shard_map/pallas_call | solution.py:93
  98.3 1.9 %collective-permute-done.3 = f32[128,1024]{1,0:T(8,128)S(1)} collective-permute-done((f32[128,1024]{1,0:T(8,128)S(1)}, f32[128,1024]{1,0:T(8,128)S(1)}, u32[]{:S(2)}, u32[]{:S(2)}) %collective-permute-start.3) | collective-permute-done | bytes 524320 | tf_op jit(solution)/shard_map/ppermute | solution.py:162
  100.2 0.9 multiply_bitcast_fusion
  101.1 1.7 %multiply_bitcast_fusion.1 = f32[1,128,512]{2,1,0:T(8,128)} fusion(f32[128,512]{1,0:T(8,128)} %reduce-scatter.2.cloned.1.call-done), kind=kLoop, calls=%fused_computation.28 | loop fusion | flops 65536 | bytes 524288 | tf_op jit(solution)/shard_map/broadcast_in_dim | solution.py:164
  (40 shorter events, 5.2 us)
Async XLA Ops:
  7.2 10.8 %copy-start = (bf16[1024,512]{1,0:T(8,128)(2,1)S(1)}, bf16[1024,512]{1,0:T(8,128)(2,1)}, u32[]{:S(2)}) copy-start(bf16[1024,512]{1,0:T(8,128)(2,1)} %param.7) | copy-start | bytes 3145732
  12.8 10.0 %all-to-all-start = ((bf16[4,13,512]{2,1,0:T(8,128)(2,1)}), bf16[4,13,512]{2,1,0:T(8,128)(2,1)S(1)}, u32[]{:S(2)}, u32[]{:S(2)}) async-start(bf16[4,13,512]{2,1,0:T(8,128)(2,1)} %fusion.15), calls=%async_computation | async-start | bytes 131072 | tf_op jit(solution)/shard_map/all_to_all | solution.py:129
  21.7 5.6 %copy-start.9 = (s32[1024,12]{0,1:T(8,128)S(1)}, s32[1024,12]{0,1:T(8,128)}, u32[]{:S(2)}) copy-start(s32[1024,12]{0,1:T(8,128)} %param.10) | copy-start | bytes 147460
  22.8 4.6 %copy-start.7 = (bf16[4,13,512]{2,1,0:T(8,128)(2,1)}, bf16[4,13,512]{2,1,0:T(8,128)(2,1)S(1)}, u32[]{:S(2)}) copy-start(bf16[4,13,512]{2,1,0:T(8,128)(2,1)S(1)} %all-to-all-done) | copy-start | bytes 159748
  22.8 28.4 %all-to-all-start.1 = ((bf16[4,512,512]{2,1,0:T(8,128)(2,1)}), bf16[4,512,512]{2,1,0:T(8,128)(2,1)}, u32[]{:S(2)}, u32[]{:S(2)}) async-start(bf16[4,512,512]{2,1,0:T(8,128)(2,1)} %fusion.9), calls=%async_computation.1 | async-start | bytes 4194304 | tf_op jit(solution)/shard_map/all_to_all | solution.py:126
  27.3 73.7 %reduce-scatter.2.cloned.1.call-start = ((), (), s32[]{:S(2)}) async-start(), calls=%async_computation.3 | async-start | bytes 2359296 | tf_op jit(solution)/shard_map/reduce_scatter | solution.py:155
  29.5 0.8 copy-start.8
  29.5 1.0 copy-start.3
  41.5 0.8 copy-start.1
  42.3 1.1 copy-start.4
  43.4 0.6 copy-start.6
  57.8 5.7 %collective-permute-start.1 = (bf16[16,2048]{1,0:T(8,128)(2,1)}, bf16[16,2048]{1,0:T(8,128)(2,1)}, u32[]{:S(2)}, u32[]{:S(2)}) collective-permute-start(bf16[16,2048]{1,0:T(8,128)(2,1)} %copy-done.6), channel_id=1, source_target_pairs={{0,4},{1,5},{2,6},{3,7},{4,0},{5,1},{6,2},{7,3},{8,12},{9,13},{10,... | collective-permute-start | bytes 196616 | tf_op jit(solution)/shard_map/ppermute | solution.py:146
  60.5 4.6 %collective-permute-start.2 = (bf16[16,2048]{1,0:T(8,128)(2,1)}, bf16[16,2048]{1,0:T(8,128)(2,1)}, u32[]{:S(2)}, u32[]{:S(2)}) collective-permute-start(bf16[16,2048]{1,0:T(8,128)(2,1)} %copy-done.6), channel_id=1, source_target_pairs={{0,6},{1,7},{2,0},{3,1},{4,2},{5,3},{6,4},{7,5},{8,14},{9,15},{10,... | collective-permute-start | bytes 196616 | tf_op jit(solution)/shard_map/ppermute | solution.py:146
  61.8 25.7 %collective-permute-start = (bf16[16,2048]{1,0:T(8,128)(2,1)}, bf16[16,2048]{1,0:T(8,128)(2,1)S(1)}, u32[]{:S(2)}, u32[]{:S(2)}) collective-permute-start(bf16[16,2048]{1,0:T(8,128)(2,1)} %copy-done.6), channel_id=1, source_target_pairs={{0,2},{1,3},{2,4},{3,5},{4,6},{5,7},{6,0},{7,1},{8,10},{9,11},{10,... | collective-permute-start | bytes 196616 | tf_op jit(solution)/shard_map/ppermute | solution.py:146
  65.9 1.0 copy-start.2
  87.5 10.4 %copy-start.5 = (f32[256,1024]{1,0:T(8,128)S(1)}, f32[256,1024]{1,0:T(8,128)}, u32[]{:S(2)}) copy-start(f32[256,1024]{1,0:T(8,128)} %copy-done.4) | copy-start | bytes 3145732
  98.2 2.0 %collective-permute-start.3 = (f32[128,1024]{1,0:T(8,128)S(1)}, f32[128,1024]{1,0:T(8,128)S(1)}, u32[]{:S(2)}, u32[]{:S(2)}) collective-permute-start(f32[128,1024]{1,0:T(8,128)S(1)} %constant_dynamic-slice_fusion), channel_id=1, source_target_pairs={{0,1},{1,0},{2,3},{3,2},{4,5},{5,4},{6,7},{7,6},{8,9},{9,8},{10,11... | collective-permute-start | bytes 1572872 | tf_op jit(solution)/shard_map/ppermute | solution.py:162
Sparse Core Ops, SparseCore 0:
  57.9 36.4 reduce-scatter.1

commit v2 on v1

--- a/solution.py
+++ b/solution.py
@@ -107,6 +107,28 @@
     )(meta, pick, rhs, rhs_rows)
 
 
+def moment_kernel(w_ref, p_ref, o_ref, *, scale):
+    o_ref[...] = jnp.dot(w_ref[...], p_ref[...], preferred_element_type=jnp.float32) * scale
+
+
+def moment_sums(weighted_t, profiles, scale, block=256):
+    terms, samples = weighted_t.shape
+    q = profiles.shape[1]
+    return pl.pallas_call(
+        functools.partial(moment_kernel, scale=scale),
+        grid=(terms // block,),
+        in_specs=[
+            pl.BlockSpec((block, samples), lambda i: (i, 0)),
+            pl.BlockSpec((samples, q), lambda i: (0, 0)),
+        ],
+        out_specs=pl.BlockSpec((block, q), lambda i: (i, 0)),
+        out_shape=jax.ShapeDtypeStruct((terms, q), jnp.float32),
+        compiler_params=pltpu.CompilerParams(
+            dimension_semantics=("arbitrary",), vmem_limit_bytes=48 * 1024 * 1024
+        ),
+    )(weighted_t, profiles)
+
+
 def on_device(params, profiles, weights, destinations, table):
     groups = lax.axis_size("elem")
     members = lax.axis_size("grp")
@@ -151,8 +173,8 @@
     gram_own, weighted_t = gram_rows(meta_r, pick, rhs, rhs_rows, npar, True)
     (gram_first,) = gram_rows(others[0], pick, rhs, rhs_rows, npar, False)
     gram_oth = gram_first
-    moment_part = jnp.dot(weighted_t, prof_r, preferred_element_type=jnp.float32)
-    moment_rows = lax.psum_scatter(moment_part, "grp", scatter_dimension=0, tiled=True) * scale
+    moment_part = moment_sums(weighted_t, prof_r, scale)
+    moment_rows = lax.psum_scatter(moment_part, "grp", scatter_dimension=0, tiled=True)
     if len(others) > 1:
         (gram_rest,) = gram_rows(jnp.concatenate(others[1:], axis=1), pick, rhs, rhs_rows, npar, False)
         gram_oth = gram_oth + gram_rest

time: 110 us -> 109 us (level)
  matrix products: 14.2 us -> 7.61 us
  Pallas kernels: 41.8 us -> 47.2 us
  other arithmetic: 7.28 us -> 5.61 us
  local copies, waits for them, and re-layouts: 4.75 us -> 6.09 us
    dot_general x1 -> x0, matrix products: 6.55 us -> none  [on_device(): jnp.dot(weighted_t, prof_r, preferred_element_type=jnp.float32)]
    pallas_call x0 -> x1, Pallas kernels: none -> 5.38 us  [moment_sums(): pl.pallas_call(functools.partial(moment_kernel, scale=scale), grid=(terms...]
    broadcast_in_dim x2 -> x1, other arithmetic: 2.53 us -> 0.86 us  [on_device(): return (gram_out[None], moment_rows[None])]
    unnamed x22 -> x24, local copies, waits for them, and re-layouts: 3.91 us -> 5.26 us
  transfers between devices with their start and end apart: 7 -> 7, of which waited for: 5 -> 5; matrix products, arithmetic and copies ran while one was open for 8% -> 8% of each run, Pallas kernels for 38% -> 39%
where the time goes in v2:
time: 109 us; the launch traced here: 108 us
  Pallas kernels  47.2 us (43%)
  starting transfers between devices  14.4 us (13%)
  between operations  14.3 us (13%)
  waiting for transfers between devices  12.8 us (12%)
  matrix products  7.61 us (7%)
  local copies, waits for them, and re-layouts  6.09 us (6%)
  other arithmetic  5.61 us (5%)
    pallas_call x3, Pallas kernels, gram_rows(): pl.pallas_call(functools.partial(gram_kernel, npar=npar), grid=(samples /...  41.8 us
    all_to_all x1, waiting for transfers between devices, on_device(): prof_r = lax.all_to_all(prof_c, 'elem', 0, 0, tiled=True)  7.24 us
    pallas_call x1, Pallas kernels, moment_sums(): pl.pallas_call(functools.partial(moment_kernel, scale=scale), grid=(terms...  5.38 us
    unnamed x24, local copies, waits for them, and re-layouts  5.26 us
    all_to_all x1, starting transfers between devices, on_device(): meta_r = lax.all_to_all(meta_c, 'elem', 0, 0, tiled=True)  5.19 us
    ppermute x3, starting transfers between devices, on_device(): lax.ppermute(meta_r, 'grp', [(i, (i + 2 * k) % members) for i in range(me...  4.68 us
    all_to_all x1, starting transfers between devices, on_device(): prof_r = lax.all_to_all(prof_c, 'elem', 0, 0, tiled=True)  4.45 us
    dot_general x1, matrix products, on_device(): jnp.einsum('eis,sq->eiq', sel, profiles, preferred_element_type=jnp.float32)  3.7 us
  transfers between devices with their start and end apart: 7, of which 5 were waited for; matrix products, arithmetic and copies ran while one was open for 8% of the time, Pallas kernels for 39%

profile of v2, /device:TPU:0, one launch (start us, length us, event | category | flops | bytes accessed | tf_op | source)
XLA Modules:
  0.0 108.1 jit_solution(4253945401763102688)
XLA Ops:
  7.2 1.3 %fusion.19 = f32[1024]{0:T(1024)S(1)} fusion(s32[1024]{0:T(1024)} %param.9), kind=kOutput, calls=%fused_computation.16 | convolution fusion | flops 9452544 | bytes 8192 | tf_op jit(solution)/shard_map/dot_general | solution.py:142
  8.5 0.7 iota_compare_fusion.12
  9.5 0.7 broadcast_in_dim.10
  10.2 2.6 %fusion.15 = bf16[4,13,512]{2,1,0:T(8,128)(2,1)} fusion(pred[512,1024]{1,0:T(8,128)(4,1)S(1)} %iota_compare_fusion.2, pred[4,1024]{1,0:T(4,128)(4,1)S(1)} %iota_compare_fusion.12, bf16[1,1024]{1,0:T(2,128)(2,1)S(1)} %broadcast_in_dim.10, bf16[12,1024]{1,0:T(8,128)(2,1)} %param.6), kind=kOutput, calls=%fused_computation.14 | convolution fusion | flops 56702976 | bytes 608256 | tf_op jit(solution)/shard_map/eis,js->eji/dot_general | solution.py:150
  12.8 5.2 %all-to-all-start = ((bf16[4,13,512]{2,1,0:T(8,128)(2,1)}), bf16[4,13,512]{2,1,0:T(8,128)(2,1)S(1)}, u32[]{:S(2)}, u32[]{:S(2)}) async-start(bf16[4,13,512]{2,1,0:T(8,128)(2,1)} %fusion.15), calls=%async_computation | async-start | bytes 131072 | tf_op jit(solution)/shard_map/all_to_all | solution.py:151
  18.0 3.7 %fusion.9 = bf16[4,512,512]{2,1,0:T(8,128)(2,1)} fusion(pred[512,1024]{1,0:T(8,128)(4,1)S(1)} %iota_compare_fusion.2, pred[4,1024]{1,0:T(4,128)(4,1)S(1)} %iota_compare_fusion.12, bf16[1024,512]{1,0:T(8,128)(2,1)S(1)} %copy-done), kind=kOutput, calls=%fused_computation.12 | convolution fusion | flops 2150629376 | bytes 3674112 | tf_op jit(solution)/shard_map/eis,sq->eiq/dot_general | solution.py:147
  21.7 1.1 %all-to-all-done = bf16[4,13,512]{2,1,0:T(8,128)(2,1)S(1)} async-done(((bf16[4,13,512]{2,1,0:T(8,128)(2,1)}), bf16[4,13,512]{2,1,0:T(8,128)(2,1)S(1)}, u32[]{:S(2)}, u32[]{:S(2)}) %all-to-all-start) | async-done | bytes 53280 | tf_op jit(solution)/shard_map/all_to_all | solution.py:151
  22.8 4.5 %all-to-all-start.1 = ((bf16[4,512,512]{2,1,0:T(8,128)(2,1)}), bf16[4,512,512]{2,1,0:T(8,128)(2,1)}, u32[]{:S(2)}, u32[]{:S(2)}) async-start(bf16[4,512,512]{2,1,0:T(8,128)(2,1)} %fusion.9), calls=%async_computation.1 | async-start | bytes 4194304 | tf_op jit(solution)/shard_map/all_to_all | solution.py:148
  30.6 10.9 %shard_map.77 = (f32[256,1024]{1,0:T(8,128)S(1)}, bf16[1024,2048]{1,0:T(8,128)(2,1)}) custom-call(bf16[16,2048]{1,0:T(8,128)(2,1)S(1)} %pad.4.m_ref, bf16[3,256,192]{2,1,0:T(8,128)(2,1)S(1)} %copy-done.4, bf16[4,1024,192]{2,1,0:T(8,128)(2,1)S(1)} %add_convert_fusion.oh_ref, bf16[4,256,192]{2,1,0:T(8,128)(2,1)S(1)} %constant_dynamic-slice_fusion.1.ohr_ref), custom_call_target="tpu_custom_call" | custom-call | tf_op jit(solution)/shard_map/pallas_call | solution.py:93
  41.5 0.8 copy-done.2
  42.3 1.1 copy-done.5
  44.0 7.2 %all-to-all-done.1 = bf16[4,512,512]{2,1,0:T(8,128)(2,1)} async-done(((bf16[4,512,512]{2,1,0:T(8,128)(2,1)}), bf16[4,512,512]{2,1,0:T(8,128)(2,1)}, u32[]{:S(2)}, u32[]{:S(2)}) %all-to-all-start.1) | async-done | bytes 2097184 | tf_op jit(solution)/shard_map/all_to_all | solution.py:148
  51.2 5.4 %shard_map.80 = f32[1024,512]{1,0:T(8,128)S(1)} custom-call(bf16[1024,2048]{1,0:T(8,128)(2,1)} %get-tuple-element.5.w_ref, bf16[2048,512]{1,0:T(8,128)(2,1)} %bitcast.13.p_ref), custom_call_target="tpu_custom_call" | custom-call | tf_op jit(solution)/shard_map/pallas_call | solution.py:117
  56.6 1.3 %copy-done.1 = f32[1024,512]{1,0:T(8,128)} copy-done((f32[1024,512]{1,0:T(8,128)}, f32[1024,512]{1,0:T(8,128)S(1)}, u32[]{:S(2)}) %copy-start.1) | copy-done | bytes 2097176
  58.0 2.6 %collective-permute-start.1 = (bf16[16,2048]{1,0:T(8,128)(2,1)}, bf16[16,2048]{1,0:T(8,128)(2,1)}, u32[]{:S(2)}, u32[]{:S(2)}) collective-permute-start(bf16[16,2048]{1,0:T(8,128)(2,1)} %copy-done.7), channel_id=1, source_target_pairs={{0,4},{1,5},{2,6},{3,7},{4,0},{5,1},{6,2},{7,3},{8,12},{9,13},{10,... | collective-permute-start | bytes 196616 | tf_op jit(solution)/shard_map/ppermute | solution.py:168
  60.6 1.4 %collective-permute-start.2 = (bf16[16,2048]{1,0:T(8,128)(2,1)}, bf16[16,2048]{1,0:T(8,128)(2,1)}, u32[]{:S(2)}, u32[]{:S(2)}) collective-permute-start(bf16[16,2048]{1,0:T(8,128)(2,1)} %copy-done.7), channel_id=1, source_target_pairs={{0,6},{1,7},{2,0},{3,1},{4,2},{5,3},{6,4},{7,5},{8,14},{9,15},{10,... | collective-permute-start | bytes 196616 | tf_op jit(solution)/shard_map/ppermute | solution.py:168
  62.7 1.0 collective-permute-done.1
  63.6 1.6 %collective-permute-done.2 = bf16[16,2048]{1,0:T(8,128)(2,1)} collective-permute-done((bf16[16,2048]{1,0:T(8,128)(2,1)}, bf16[16,2048]{1,0:T(8,128)(2,1)}, u32[]{:S(2)}, u32[]{:S(2)}) %collective-permute-start.2) | collective-permute-done | bytes 65568 | tf_op jit(solution)/shard_map/ppermute | solution.py:168
  65.2 0.9 pad_maximum_fusion.m_ref
  66.1 1.0 copy-done.3
  67.2 20.5 %shard_map.79 = f32[256,1024]{1,0:T(8,128)S(1)} custom-call(bf16[16,4096]{1,0:T(8,128)(2,1)S(1)} %pad_maximum_fusion.m_ref, bf16[3,256,192]{2,1,0:T(8,128)(2,1)S(1)} %copy-done.4, bf16[4,1024,192]{2,1,0:T(8,128)(2,1)S(1)} %add_convert_fusion.oh_ref, bf16[4,256,192]{2,1,0:T(8,128)(2,1)S(1)} %copy-done.3), custom_call_target="tpu_custom_call" | custom-call | tf_op jit(solution)/shard_map/pallas_call | solution.py:93
  87.7 10.3 %shard_map.78 = f32[256,1024]{1,0:T(8,128)S(1)} custom-call(bf16[16,2048]{1,0:T(8,128)(2,1)S(1)} %collective-permute-done.m_ref, bf16[3,256,192]{2,1,0:T(8,128)(2,1)S(1)} %copy-done.4, bf16[4,1024,192]{2,1,0:T(8,128)(2,1)S(1)} %add_convert_fusion.oh_ref, bf16[4,256,192]{2,1,0:T(8,128)(2,1)S(1)} %copy-done.3), custom_call_target="tpu_custom_call" | custom-call | tf_op jit(solution)/shard_map/pallas_call | solution.py:93
  98.5 1.9 %collective-permute-done.3 = f32[128,1024]{1,0:T(8,128)S(1)} collective-permute-done((f32[128,1024]{1,0:T(8,128)S(1)}, f32[128,1024]{1,0:T(8,128)S(1)}, u32[]{:S(2)}, u32[]{:S(2)}) %collective-permute-start.3) | collective-permute-done | bytes 524320 | tf_op jit(solution)/shard_map/ppermute | solution.py:184
  100.4 0.9 multiply_bitcast_fusion
  (41 shorter events, 5.2 us)
Async XLA Ops:
  7.2 10.8 %copy-start = (bf16[1024,512]{1,0:T(8,128)(2,1)S(1)}, bf16[1024,512]{1,0:T(8,128)(2,1)}, u32[]{:S(2)}) copy-start(bf16[1024,512]{1,0:T(8,128)(2,1)} %param.7) | copy-start | bytes 3145732
  12.8 10.0 %all-to-all-start = ((bf16[4,13,512]{2,1,0:T(8,128)(2,1)}), bf16[4,13,512]{2,1,0:T(8,128)(2,1)S(1)}, u32[]{:S(2)}, u32[]{:S(2)}) async-start(bf16[4,13,512]{2,1,0:T(8,128)(2,1)} %fusion.15), calls=%async_computation | async-start | bytes 131072 | tf_op jit(solution)/shard_map/all_to_all | solution.py:151
  21.7 5.7 %copy-start.10 = (s32[1024,12]{0,1:T(8,128)S(1)}, s32[1024,12]{0,1:T(8,128)}, u32[]{:S(2)}) copy-start(s32[1024,12]{0,1:T(8,128)} %param.10) | copy-start | bytes 147460
  22.8 4.6 %copy-start.8 = (bf16[4,13,512]{2,1,0:T(8,128)(2,1)}, bf16[4,13,512]{2,1,0:T(8,128)(2,1)S(1)}, u32[]{:S(2)}) copy-start(bf16[4,13,512]{2,1,0:T(8,128)(2,1)S(1)} %all-to-all-done) | copy-start | bytes 159748
  22.8 28.4 %all-to-all-start.1 = ((bf16[4,512,512]{2,1,0:T(8,128)(2,1)}), bf16[4,512,512]{2,1,0:T(8,128)(2,1)}, u32[]{:S(2)}, u32[]{:S(2)}) async-start(bf16[4,512,512]{2,1,0:T(8,128)(2,1)} %fusion.9), calls=%async_computation.1 | async-start | bytes 4194304 | tf_op jit(solution)/shard_map/all_to_all | solution.py:148
  27.3 73.9 %reduce-scatter.2.cloned.1.call-start = ((), (), s32[]{:S(2)}) async-start(), calls=%async_computation.3 | async-start | bytes 2359296 | tf_op jit(solution)/shard_map/reduce_scatter | solution.py:177
  29.5 0.8 copy-start.9
  29.5 1.0 copy-start.4
  41.5 0.8 copy-start.2
  42.3 1.1 copy-start.5
  43.4 0.6 copy-start.7
  56.6 1.3 %copy-start.1 = (f32[1024,512]{1,0:T(8,128)}, f32[1024,512]{1,0:T(8,128)S(1)}, u32[]{:S(2)}) copy-start(f32[1024,512]{1,0:T(8,128)S(1)} %shard_map.80) | copy-start | bytes 6291460
  58.0 5.6 %collective-permute-start.1 = (bf16[16,2048]{1,0:T(8,128)(2,1)}, bf16[16,2048]{1,0:T(8,128)(2,1)}, u32[]{:S(2)}, u32[]{:S(2)}) collective-permute-start(bf16[16,2048]{1,0:T(8,128)(2,1)} %copy-done.7), channel_id=1, source_target_pairs={{0,4},{1,5},{2,6},{3,7},{4,0},{5,1},{6,2},{7,3},{8,12},{9,13},{10,... | collective-permute-start | bytes 196616 | tf_op jit(solution)/shard_map/ppermute | solution.py:168
  60.6 4.6 %collective-permute-start.2 = (bf16[16,2048]{1,0:T(8,128)(2,1)}, bf16[16,2048]{1,0:T(8,128)(2,1)}, u32[]{:S(2)}, u32[]{:S(2)}) collective-permute-start(bf16[16,2048]{1,0:T(8,128)(2,1)} %copy-done.7), channel_id=1, source_target_pairs={{0,6},{1,7},{2,0},{3,1},{4,2},{5,3},{6,4},{7,5},{8,14},{9,15},{10,... | collective-permute-start | bytes 196616 | tf_op jit(solution)/shard_map/ppermute | solution.py:168
  62.0 25.7 %collective-permute-start = (bf16[16,2048]{1,0:T(8,128)(2,1)}, bf16[16,2048]{1,0:T(8,128)(2,1)S(1)}, u32[]{:S(2)}, u32[]{:S(2)}) collective-permute-start(bf16[16,2048]{1,0:T(8,128)(2,1)} %copy-done.7), channel_id=1, source_target_pairs={{0,2},{1,3},{2,4},{3,5},{4,6},{5,7},{6,0},{7,1},{8,10},{9,11},{10,... | collective-permute-start | bytes 196616 | tf_op jit(solution)/shard_map/ppermute | solution.py:168
  66.1 1.0 copy-start.3
  87.7 10.4 %copy-start.6 = (f32[256,1024]{1,0:T(8,128)S(1)}, f32[256,1024]{1,0:T(8,128)}, u32[]{:S(2)}) copy-start(f32[256,1024]{1,0:T(8,128)} %copy-done.5) | copy-start | bytes 3145732
  98.4 2.0 %collective-permute-start.3 = (f32[128,1024]{1,0:T(8,128)S(1)}, f32[128,1024]{1,0:T(8,128)S(1)}, u32[]{:S(2)}, u32[]{:S(2)}) collective-permute-start(f32[128,1024]{1,0:T(8,128)S(1)} %constant_dynamic-slice_fusion), channel_id=1, source_target_pairs={{0,1},{1,0},{2,3},{3,2},{4,5},{5,4},{6,7},{7,6},{8,9},{9,8},{10,11... | collective-permute-start | bytes 1572872 | tf_op jit(solution)/shard_map/ppermute | solution.py:184
Sparse Core Ops, SparseCore 0:
  58.1 36.6 reduce-scatter.1

commit v3 on v2

--- a/solution.py
+++ b/solution.py
@@ -171,13 +171,9 @@
     rhs, pick = term_maps(table, rows)
     rhs_rows = lax.dynamic_slice_in_dim(rhs, chip * 2 * own_rows, 2 * own_rows, axis=1)
     gram_own, weighted_t = gram_rows(meta_r, pick, rhs, rhs_rows, npar, True)
-    (gram_first,) = gram_rows(others[0], pick, rhs, rhs_rows, npar, False)
-    gram_oth = gram_first
     moment_part = moment_sums(weighted_t, prof_r, scale)
     moment_rows = lax.psum_scatter(moment_part, "grp", scatter_dimension=0, tiled=True)
-    if len(others) > 1:
-        (gram_rest,) = gram_rows(jnp.concatenate(others[1:], axis=1), pick, rhs, rhs_rows, npar, False)
-        gram_oth = gram_oth + gram_rest
+    (gram_oth,) = gram_rows(jnp.concatenate(others, axis=1), pick, rhs, rhs_rows, npar, False)
     gram_chip = gram_own + gram_oth
     keep = lax.dynamic_slice_in_dim(gram_chip, core * own_rows, own_rows, axis=0)
     send = lax.dynamic_slice_in_dim(gram_chip, (1 - core) * own_rows, own_rows, axis=0)

time: 109 us -> 111 us (1.018)
  waiting for transfers between devices: 12.8 us -> 15.7 us
    ppermute x3, waiting for transfers between devices: 2.56 us -> 5.39 us  [on_device(): lax.ppermute(meta_r, 'grp', [(i, (i + 2 * k) % members) for i in range(me...]
    pallas_call x3 -> x2, Pallas kernels: 41.8 us -> 41.7 us  [gram_rows(): pl.pallas_call(functools.partial(gram_kernel, npar=npar), grid=(samples /...]
  transfers between devices with their start and end apart: 7 -> 7, of which waited for: 5 -> 6; matrix products, arithmetic and copies ran while one was open for 8% -> 8% of each run, Pallas kernels for 39% -> 38%
where the time goes in v3:
time: 111 us
  Pallas kernels  47.1 us (42%)
  waiting for transfers between devices  15.7 us (14%)
  starting transfers between devices  14.4 us (13%)
  between operations  14.3 us (13%)
  matrix products  7.6 us (7%)
  local copies, waits for them, and re-layouts  6.1 us (5%)
  other arithmetic  5.51 us (5%)
    pallas_call x2, Pallas kernels, gram_rows(): pl.pallas_call(functools.partial(gram_kernel, npar=npar), grid=(samples /...  41.7 us
    all_to_all x1, waiting for transfers between devices, on_device(): prof_r = lax.all_to_all(prof_c, 'elem', 0, 0, tiled=True)  7.23 us
    ppermute x3, waiting for transfers between devices, on_device(): lax.ppermute(meta_r, 'grp', [(i, (i + 2 * k) % members) for i in range(me...  5.39 us
    pallas_call x1, Pallas kernels, moment_sums(): pl.pallas_call(functools.partial(moment_kernel, scale=scale), grid=(terms...  5.38 us
    unnamed x24, local copies, waits for them, and re-layouts  5.26 us
    all_to_all x1, starting transfers between devices, on_device(): meta_r = lax.all_to_all(meta_c, 'elem', 0, 0, tiled=True)  5.19 us
    ppermute x3, starting transfers between devices, on_device(): lax.ppermute(meta_r, 'grp', [(i, (i + 2 * k) % members) for i in range(me...  4.67 us
    all_to_all x1, starting transfers between devices, on_device(): prof_r = lax.all_to_all(prof_c, 'elem', 0, 0, tiled=True)  4.45 us
  transfers between devices with their start and end apart: 7, of which 6 were waited for; matrix products, arithmetic and copies ran while one was open for 8% of the time, Pallas kernels for 38%

profile of v3, /device:TPU:0, one launch (start us, length us, event | category | flops | bytes accessed | tf_op | source)
XLA Modules:
  0.0 110.7 jit_solution(16336498284483069015)
XLA Ops:
  7.2 1.3 %fusion.19 = f32[1024]{0:T(1024)S(1)} fusion(s32[1024]{0:T(1024)} %param.9), kind=kOutput, calls=%fused_computation.16 | convolution fusion | flops 9452544 | bytes 8192 | tf_op jit(solution)/shard_map/dot_general | solution.py:142
  8.5 0.7 iota_compare_fusion.12
  9.5 0.7 broadcast_in_dim.10
  10.2 2.6 %fusion.15 = bf16[4,13,512]{2,1,0:T(8,128)(2,1)} fusion(pred[512,1024]{1,0:T(8,128)(4,1)S(1)} %iota_compare_fusion.2, pred[4,1024]{1,0:T(4,128)(4,1)S(1)} %iota_compare_fusion.12, bf16[1,1024]{1,0:T(2,128)(2,1)S(1)} %broadcast_in_dim.10, bf16[12,1024]{1,0:T(8,128)(2,1)} %param.6), kind=kOutput, calls=%fused_computation.14 | convolution fusion | flops 56702976 | bytes 608256 | tf_op jit(solution)/shard_map/eis,js->eji/dot_general | solution.py:150
  12.8 5.2 %all-to-all-start = ((bf16[4,13,512]{2,1,0:T(8,128)(2,1)}), bf16[4,13,512]{2,1,0:T(8,128)(2,1)S(1)}, u32[]{:S(2)}, u32[]{:S(2)}) async-start(bf16[4,13,512]{2,1,0:T(8,128)(2,1)} %fusion.15), calls=%async_computation | async-start | bytes 131072 | tf_op jit(solution)/shard_map/all_to_all | solution.py:151
  18.0 3.7 %fusion.9 = bf16[4,512,512]{2,1,0:T(8,128)(2,1)} fusion(pred[512,1024]{1,0:T(8,128)(4,1)S(1)} %iota_compare_fusion.2, pred[4,1024]{1,0:T(4,128)(4,1)S(1)} %iota_compare_fusion.12, bf16[1024,512]{1,0:T(8,128)(2,1)S(1)} %copy-done), kind=kOutput, calls=%fused_computation.12 | convolution fusion | flops 2150629376 | bytes 3674112 | tf_op jit(solution)/shard_map/eis,sq->eiq/dot_general | solution.py:147
  21.7 1.1 %all-to-all-done = bf16[4,13,512]{2,1,0:T(8,128)(2,1)S(1)} async-done(((bf16[4,13,512]{2,1,0:T(8,128)(2,1)}), bf16[4,13,512]{2,1,0:T(8,128)(2,1)S(1)}, u32[]{:S(2)}, u32[]{:S(2)}) %all-to-all-start) | async-done | bytes 53280 | tf_op jit(solution)/shard_map/all_to_all | solution.py:151
  22.8 4.5 %all-to-all-start.1 = ((bf16[4,512,512]{2,1,0:T(8,128)(2,1)}), bf16[4,512,512]{2,1,0:T(8,128)(2,1)}, u32[]{:S(2)}, u32[]{:S(2)}) async-start(bf16[4,512,512]{2,1,0:T(8,128)(2,1)} %fusion.9), calls=%async_computation.1 | async-start | bytes 4194304 | tf_op jit(solution)/shard_map/all_to_all | solution.py:148
  30.6 10.9 %shard_map.77 = (f32[256,1024]{1,0:T(8,128)S(1)}, bf16[1024,2048]{1,0:T(8,128)(2,1)}) custom-call(bf16[16,2048]{1,0:T(8,128)(2,1)S(1)} %pad.4.m_ref, bf16[3,256,192]{2,1,0:T(8,128)(2,1)S(1)} %copy-done.4, bf16[4,1024,192]{2,1,0:T(8,128)(2,1)S(1)} %add_convert_fusion.oh_ref, bf16[4,256,192]{2,1,0:T(8,128)(2,1)S(1)} %constant_dynamic-slice_fusion.1.ohr_ref), custom_call_target="tpu_custom_call" | custom-call | tf_op jit(solution)/shard_map/pallas_call | solution.py:93
  41.5 0.8 copy-done.2
  42.3 1.1 copy-done.5
  44.0 7.2 %all-to-all-done.1 = bf16[4,512,512]{2,1,0:T(8,128)(2,1)} async-done(((bf16[4,512,512]{2,1,0:T(8,128)(2,1)}), bf16[4,512,512]{2,1,0:T(8,128)(2,1)}, u32[]{:S(2)}, u32[]{:S(2)}) %all-to-all-start.1) | async-done | bytes 2097184 | tf_op jit(solution)/shard_map/all_to_all | solution.py:148
  51.2 5.4 %shard_map.79 = f32[1024,512]{1,0:T(8,128)S(1)} custom-call(bf16[1024,2048]{1,0:T(8,128)(2,1)} %get-tuple-element.5.w_ref, bf16[2048,512]{1,0:T(8,128)(2,1)} %bitcast.13.p_ref), custom_call_target="tpu_custom_call" | custom-call | tf_op jit(solution)/shard_map/pallas_call | solution.py:117
  56.6 1.3 %copy-done.1 = f32[1024,512]{1,0:T(8,128)} copy-done((f32[1024,512]{1,0:T(8,128)}, f32[1024,512]{1,0:T(8,128)S(1)}, u32[]{:S(2)}) %copy-start.1) | copy-done | bytes 2097176
  58.0 3.7 %collective-permute-start.2 = (bf16[16,2048]{1,0:T(8,128)(2,1)}, bf16[16,2048]{1,0:T(8,128)(2,1)}, u32[]{:S(2)}, u32[]{:S(2)}) collective-permute-start(bf16[16,2048]{1,0:T(8,128)(2,1)} %copy-done.7), channel_id=1, source_target_pairs={{0,6},{1,7},{2,0},{3,1},{4,2},{5,3},{6,4},{7,5},{8,14},{9,15},{10,... | collective-permute-start | bytes 196616 | tf_op jit(solution)/shard_map/ppermute | solution.py:168
  61.6 1.0 collective-permute-start
  62.7 1.4 %collective-permute-done.2 = bf16[16,2048]{1,0:T(8,128)(2,1)} collective-permute-done((bf16[16,2048]{1,0:T(8,128)(2,1)}, bf16[16,2048]{1,0:T(8,128)(2,1)}, u32[]{:S(2)}, u32[]{:S(2)}) %collective-permute-start.2) | collective-permute-done | bytes 65568 | tf_op jit(solution)/shard_map/ppermute | solution.py:168
  64.0 3.1 %collective-permute-done.1 = bf16[16,2048]{1,0:T(8,128)(2,1)} collective-permute-done((bf16[16,2048]{1,0:T(8,128)(2,1)}, bf16[16,2048]{1,0:T(8,128)(2,1)}, u32[]{:S(2)}, u32[]{:S(2)}) %collective-permute-start.1) | collective-permute-done | bytes 65568 | tf_op jit(solution)/shard_map/ppermute | solution.py:168
  67.1 0.9 collective-permute-done
  68.1 0.9 pad_maximum_fusion.m_ref
  69.0 1.0 copy-done.3
  70.0 30.8 %shard_map.78 = f32[256,1024]{1,0:T(8,128)S(1)} custom-call(bf16[16,6144]{1,0:T(8,128)(2,1)S(1)} %pad_maximum_fusion.m_ref, bf16[3,256,192]{2,1,0:T(8,128)(2,1)S(1)} %copy-done.4, bf16[4,1024,192]{2,1,0:T(8,128)(2,1)S(1)} %add_convert_fusion.oh_ref, bf16[4,256,192]{2,1,0:T(8,128)(2,1)S(1)} %copy-done.3), custom_call_target="tpu_custom_call" | custom-call | tf_op jit(solution)/shard_map/pallas_call | solution.py:93
  101.1 1.9 %collective-permute-done.3 = f32[128,1024]{1,0:T(8,128)S(1)} collective-permute-done((f32[128,1024]{1,0:T(8,128)S(1)}, f32[128,1024]{1,0:T(8,128)S(1)}, u32[]{:S(2)}, u32[]{:S(2)}) %collective-permute-start.3) | collective-permute-done | bytes 524320 | tf_op jit(solution)/shard_map/ppermute | solution.py:180
  103.0 0.9 multiply_bitcast_fusion
  (40 shorter events, 4.4 us)
Async XLA Ops:
  7.2 10.8 %copy-start = (bf16[1024,512]{1,0:T(8,128)(2,1)S(1)}, bf16[1024,512]{1,0:T(8,128)(2,1)}, u32[]{:S(2)}) copy-start(bf16[1024,512]{1,0:T(8,128)(2,1)} %param.7) | copy-start | bytes 3145732
  12.8 10.0 %all-to-all-start = ((bf16[4,13,512]{2,1,0:T(8,128)(2,1)}), bf16[4,13,512]{2,1,0:T(8,128)(2,1)S(1)}, u32[]{:S(2)}, u32[]{:S(2)}) async-start(bf16[4,13,512]{2,1,0:T(8,128)(2,1)} %fusion.15), calls=%async_computation | async-start | bytes 131072 | tf_op jit(solution)/shard_map/all_to_all | solution.py:151
  21.7 5.7 %copy-start.10 = (s32[1024,12]{0,1:T(8,128)S(1)}, s32[1024,12]{0,1:T(8,128)}, u32[]{:S(2)}) copy-start(s32[1024,12]{0,1:T(8,128)} %param.10) | copy-start | bytes 147460
  22.8 4.6 %copy-start.8 = (bf16[4,13,512]{2,1,0:T(8,128)(2,1)}, bf16[4,13,512]{2,1,0:T(8,128)(2,1)S(1)}, u32[]{:S(2)}) copy-start(bf16[4,13,512]{2,1,0:T(8,128)(2,1)S(1)} %all-to-all-done) | copy-start | bytes 159748
  22.8 28.4 %all-to-all-start.1 = ((bf16[4,512,512]{2,1,0:T(8,128)(2,1)}), bf16[4,512,512]{2,1,0:T(8,128)(2,1)}, u32[]{:S(2)}, u32[]{:S(2)}) async-start(bf16[4,512,512]{2,1,0:T(8,128)(2,1)} %fusion.9), calls=%async_computation.1 | async-start | bytes 4194304 | tf_op jit(solution)/shard_map/all_to_all | solution.py:148
  27.3 76.5 %reduce-scatter.2.cloned.1.call-start = ((), (), s32[]{:S(2)}) async-start(), calls=%async_computation.3 | async-start | bytes 2359296 | tf_op jit(solution)/shard_map/reduce_scatter | solution.py:175
  29.5 0.8 copy-start.9
  29.5 1.0 copy-start.4
  41.5 0.8 copy-start.2
  42.3 1.1 copy-start.5
  43.4 0.6 copy-start.7
  56.6 1.3 %copy-start.1 = (f32[1024,512]{1,0:T(8,128)}, f32[1024,512]{1,0:T(8,128)S(1)}, u32[]{:S(2)}) copy-start(f32[1024,512]{1,0:T(8,128)S(1)} %shard_map.79) | copy-start | bytes 6291460
  58.0 6.0 %collective-permute-start.2 = (bf16[16,2048]{1,0:T(8,128)(2,1)}, bf16[16,2048]{1,0:T(8,128)(2,1)}, u32[]{:S(2)}, u32[]{:S(2)}) collective-permute-start(bf16[16,2048]{1,0:T(8,128)(2,1)} %copy-done.7), channel_id=1, source_target_pairs={{0,6},{1,7},{2,0},{3,1},{4,2},{5,3},{6,4},{7,5},{8,14},{9,15},{10,... | collective-permute-start | bytes 196616 | tf_op jit(solution)/shard_map/ppermute | solution.py:168
  61.6 5.5 %collective-permute-start.1 = (bf16[16,2048]{1,0:T(8,128)(2,1)}, bf16[16,2048]{1,0:T(8,128)(2,1)}, u32[]{:S(2)}, u32[]{:S(2)}) collective-permute-start(bf16[16,2048]{1,0:T(8,128)(2,1)} %copy-done.7), channel_id=1, source_target_pairs={{0,4},{1,5},{2,6},{3,7},{4,0},{5,1},{6,2},{7,3},{8,12},{9,13},{10,... | collective-permute-start | bytes 196616 | tf_op jit(solution)/shard_map/ppermute | solution.py:168
  61.6 6.4 %collective-permute-start = (bf16[16,2048]{1,0:T(8,128)(2,1)}, bf16[16,2048]{1,0:T(8,128)(2,1)}, u32[]{:S(2)}, u32[]{:S(2)}) collective-permute-start(bf16[16,2048]{1,0:T(8,128)(2,1)} %copy-done.7), channel_id=1, source_target_pairs={{0,2},{1,3},{2,4},{3,5},{4,6},{5,7},{6,0},{7,1},{8,10},{9,11},{10,... | collective-permute-start | bytes 196616 | tf_op jit(solution)/shard_map/ppermute | solution.py:168
  69.0 1.0 copy-start.3
  70.0 30.8 %copy-start.6 = (f32[256,1024]{1,0:T(8,128)S(1)}, f32[256,1024]{1,0:T(8,128)}, u32[]{:S(2)}) copy-start(f32[256,1024]{1,0:T(8,128)} %copy-done.5) | copy-start | bytes 3145732
  101.0 2.0 %collective-permute-start.3 = (f32[128,1024]{1,0:T(8,128)S(1)}, f32[128,1024]{1,0:T(8,128)S(1)}, u32[]{:S(2)}, u32[]{:S(2)}) collective-permute-start(f32[128,1024]{1,0:T(8,128)S(1)} %constant_dynamic-slice_fusion), channel_id=1, source_target_pairs={{0,1},{1,0},{2,3},{3,2},{4,5},{5,4},{6,7},{7,6},{8,9},{9,8},{10,11... | collective-permute-start | bytes 1572872 | tf_op jit(solution)/shard_map/ppermute | solution.py:180
Sparse Core Ops, SparseCore 0:
  58.1 36.4 reduce-scatter.1

commit v4 on v3

--- a/solution.py
+++ b/solution.py
@@ -129,6 +129,17 @@
     )(weighted_t, profiles)
 
 
+def exchange(blocks, groups):
+    if groups & (groups - 1):
+        return lax.all_to_all(blocks, "elem", 0, 0, tiled=True)
+    me = lax.axis_index("elem")
+    got = [lax.dynamic_index_in_dim(blocks, me, 0, keepdims=False)]
+    for m in range(1, groups):
+        send = lax.dynamic_index_in_dim(blocks, me ^ m, 0, keepdims=False)
+        got.append(lax.ppermute(send, "elem", [(i, i ^ m) for i in range(groups)]))
+    return jnp.stack(got)
+
+
 def on_device(params, profiles, weights, destinations, table):
     groups = lax.axis_size("elem")
     members = lax.axis_size("grp")
@@ -145,10 +156,10 @@
     sel = sel.astype(jnp.bfloat16)
 
     prof_c = jnp.einsum("eis,sq->eiq", sel, profiles, preferred_element_type=jnp.float32).astype(jnp.bfloat16)
-    prof_r = lax.all_to_all(prof_c, "elem", 0, 0, tiled=True)
     meta = jnp.concatenate([params, weights[None, :]], axis=0)
     meta_c = jnp.einsum("eis,js->eji", sel, meta, preferred_element_type=jnp.float32).astype(jnp.bfloat16)
-    meta_r = lax.all_to_all(meta_c, "elem", 0, 0, tiled=True)
+    meta_r = exchange(meta_c, groups)
+    prof_r = exchange(prof_c, groups)
 
     npar = params.shape[0]
     q = profiles.shape[1]

time: 111 us -> 122 us (1.099)
  waiting for transfers between devices: 15.7 us -> 27.9 us
  other arithmetic: 5.51 us -> 7.88 us
  matrix products: 7.6 us -> 5.6 us
  starting transfers between devices: 14.4 us -> 12.8 us
    ppermute x0 -> x6, waiting for transfers between devices: none -> 19.6 us  [exchange(): got.append(lax.ppermute(send, 'elem', [(i, i ^ m) for i in range(groups)]))]
    all_to_all x2 -> x0, starting transfers between devices: 9.64 us -> none  [the longest x1 5.19 us: on_device(): meta_r = lax.all_to_all(meta_c, 'elem', 0, 0, tiled=True)]
    all_to_all x2 -> x0, waiting for transfers between devices: 8.38 us -> none  [the longest x1 7.23 us: on_device(): prof_r = lax.all_to_all(prof_c, 'elem', 0, 0, tiled=True)]
    ppermute x0 -> x6, starting transfers between devices: none -> 8.04 us  [exchange(): got.append(lax.ppermute(send, 'elem', [(i, i ^ m) for i in range(groups)]))]
    dynamic_slice x0 -> x2, local copies, waits for them, and re-layouts: none -> 2 us  [exchange(): got = [lax.dynamic_index_in_dim(blocks, me, 0, keepdims=False)]]
    unnamed x24 -> x22, local copies, waits for them, and re-layouts: 5.26 us -> 3.43 us
    another operation x0 -> x1, other arithmetic: none -> 1.62 us  [exchange(): return jnp.stack(got)]
    dot_general x1, matrix products: 3.7 us -> 2.34 us  [on_device(): jnp.einsum('eis,sq->eiq', sel, profiles, preferred_element_type=jnp.float32)]
  transfers between devices with their start and end apart: 7 -> 11, of which waited for: 6 -> 5; matrix products, arithmetic and copies ran while one was open for 8% -> 8% of each run, Pallas kernels for 38% -> 34%
where the time goes in v4:
time: 122 us; the launch traced here: 121 us
  Pallas kernels  46.4 us (38%)
  waiting for transfers between devices  27.9 us (23%)
  between operations  14.3 us (12%)
  starting transfers between devices  12.8 us (10%)
  other arithmetic  7.88 us (6%)
  local copies, waits for them, and re-layouts  6.26 us (5%)
  matrix products  5.6 us (5%)
    pallas_call x2, Pallas kernels, gram_rows(): pl.pallas_call(functools.partial(gram_kernel, npar=npar), grid=(samples /...  41.8 us
    ppermute x6, waiting for transfers between devices, exchange(): got.append(lax.ppermute(send, 'elem', [(i, i ^ m) for i in range(groups)]))  19.6 us
    ppermute x6, starting transfers between devices, exchange(): got.append(lax.ppermute(send, 'elem', [(i, i ^ m) for i in range(groups)]))  8.04 us
    ppermute x3, waiting for transfers between devices, on_device(): lax.ppermute(meta_r, 'grp', [(i, (i + 2 * k) % members) for i in range(me...  6.49 us
    pallas_call x1, Pallas kernels, moment_sums(): pl.pallas_call(functools.partial(moment_kernel, scale=scale), grid=(terms...  4.69 us
    ppermute x3, starting transfers between devices, on_device(): lax.ppermute(meta_r, 'grp', [(i, (i + 2 * k) % members) for i in range(me...  4.67 us
    unnamed x22, local copies, waits for them, and re-layouts  3.43 us
  transfers between devices with their start and end apart: 11, of which 5 were waited for; matrix products, arithmetic and copies ran while one was open for 8% of the time, Pallas kernels for 34%

profile of v4, /device:TPU:0, one launch (start us, length us, event | category | flops | bytes accessed | tf_op | source)
XLA Modules:
  0.0 121.3 jit_solution(708046689686261548)
XLA Ops:
  7.2 1.3 %fusion.16 = f32[1024]{0:T(1024)S(1)} fusion(s32[1024]{0:T(1024)} %param.9), kind=kOutput, calls=%fused_computation.16 | convolution fusion | flops 9452544 | bytes 8192 | tf_op jit(solution)/shard_map/dot_general | solution.py:153
  10.2 2.0 %fusion.12 = bf16[13,4,512]{2,0,1:T(8,128)(2,1)S(1)} fusion(pred[512,1024]{1,0:T(8,128)(4,1)S(1)} %iota_compare_fusion.2, pred[4,1024]{1,0:T(4,128)(4,1)S(1)} %iota_compare_fusion.12, bf16[1,1024]{1,0:T(2,128)(2,1)S(1)} %broadcast_in_dim.10, bf16[12,1024]{1,0:T(8,128)(2,1)} %param.6), kind=kOutput, calls=%fused_computation.14 | convolution fusion | flops 56702976 | bytes 608256 | tf_op jit(solution)/shard_map/eis,js->eji/dot_general | solution.py:160
  12.8 3.9 %collective-permute-start.2 = (bf16[13,512]{1,0:T(8,128)(2,1)}, bf16[13,512]{1,0:T(8,128)(2,1)}, u32[]{:S(2)}, u32[]{:S(2)}) collective-permute-start(bf16[13,512]{1,0:T(8,128)(2,1)} %get-tuple-element.15), channel_id=1, source_target_pairs={{0,24},{8,16},{16,8},{24,0},{1,25},{9,17},{17,9},{25,1},{2,26},{10... | collective-permute-start | bytes 39944 | tf_op jit(solution)/shard_map/ppermute | solution.py:139
  17.3 2.3 %fusion.9 = bf16[4,512,512]{2,1,0:T(8,128)(2,1)S(1)} fusion(pred[512,1024]{1,0:T(8,128)(4,1)S(1)} %iota_compare_fusion.2, pred[4,1024]{1,0:T(4,128)(4,1)S(1)} %iota_compare_fusion.12, bf16[1024,512]{1,0:T(8,128)(2,1)S(1)} %copy-done), kind=kOutput, calls=%fused_computation.13 | convolution fusion | flops 2150629376 | bytes 3674112 | tf_op jit(solution)/shard_map/eis,sq->eiq/dot_general | solution.py:158
  19.6 1.4 %constant_dynamic-slice_fusion = (bf16[1,512,512]{2,1,0:T(8,128)(2,1)}, bf16[512,512]{1,0:T(8,128)(2,1)}, bf16[512,512]{1,0:T(8,128)(2,1)}, bf16[512,512]{1,0:T(8,128)(2,1)}) fusion(bf16[4,512,512]{2,1,0:T(8,128)(2,1)S(1)} %fusion.9, s32[]{:T(128)S(6)} %select_n.43, s32[]{:T(128)S(6)} %select_n.46, s32[]{:T(128)S(6)} %select_n.45, s32[]{:T(128)S(6)} %select_n.44), kind=kLoop, calls=%fused_computation.46 | loop fusion | bytes 4194320 | tf_op jit(solution)/shard_map/jit(dynamic_index_in_dim)/dynamic_slice | solution.py:136
  21.0 1.5 %collective-permute-start.9 = (bf16[512,512]{1,0:T(8,128)(2,1)}, bf16[512,512]{1,0:T(8,128)(2,1)}, u32[]{:S(2)}, u32[]{:S(2)}) collective-permute-start(bf16[512,512]{1,0:T(8,128)(2,1)} %get-tuple-element.7), channel_id=1, source_target_pairs={{0,24},{8,16},{16,8},{24,0},{1,25},{9,17},{17,9},{25,1},{2,26},{10... | collective-permute-start | bytes 1572872 | tf_op jit(solution)/shard_map/ppermute | solution.py:139
  22.5 2.0 %collective-permute-start.7 = (bf16[512,512]{1,0:T(8,128)(2,1)}, bf16[512,512]{1,0:T(8,128)(2,1)}, u32[]{:S(2)}, u32[]{:S(2)}) collective-permute-start(bf16[512,512]{1,0:T(8,128)(2,1)} %get-tuple-element.9), channel_id=1, source_target_pairs={{0,8},{8,0},{16,24},{24,16},{1,9},{9,1},{17,25},{25,17},{2,10},{10... | collective-permute-start | bytes 1572872 | tf_op jit(solution)/shard_map/ppermute | solution.py:139
  27.4 19.5 %collective-permute-done = bf16[13,512]{1,0:T(8,128)(2,1)S(1)} collective-permute-done((bf16[13,512]{1,0:T(8,128)(2,1)}, bf16[13,512]{1,0:T(8,128)(2,1)S(1)}, u32[]{:S(2)}, u32[]{:S(2)}) %collective-permute-start) | collective-permute-done | bytes 13344 | tf_op jit(solution)/shard_map/ppermute | solution.py:139
  46.9 0.7 maximum_bitcast_fusion
  47.8 11.0 %shard_map.77 = (f32[256,1024]{1,0:T(8,128)S(1)}, bf16[1024,2048]{1,0:T(8,128)(2,1)}) custom-call(bf16[16,2048]{1,0:T(8,128)(2,1)S(1)} %pad.4.m_ref, bf16[3,256,192]{2,1,0:T(8,128)(2,1)S(1)} %copy-done.4, bf16[4,1024,192]{2,1,0:T(8,128)(2,1)S(1)} %add_convert_fusion.oh_ref, bf16[4,256,192]{2,1,0:T(8,128)(2,1)S(1)} %constant_dynamic-slice_fusion.2.ohr_ref), custom_call_target="tpu_custom_call" | custom-call | tf_op jit(solution)/shard_map/pallas_call | solution.py:93
  58.8 1.0 copy-done.5
  59.8 1.6 %pad_maximum_fusion = bf16[4,512,512]{2,1,0:T(8,128)(2,1)S(1)} fusion(bf16[1,512,512]{2,1,0:T(8,128)(2,1)} %bitcast.24, bf16[1,512,512]{2,1,0:T(8,128)(2,1)} %bitcast.22, bf16[1,512,512]{2,1,0:T(8,128)(2,1)} %bitcast.20, bf16[1,512,512]{2,1,0:T(8,128)(2,1)S(1)} %copy-done.8), kind=kLoop, calls=%fused_computation.11 | loop fusion | flops 3145728 | bytes 4194304 | tf_op jit(solution)/shard_map/stack | solution.py:140
  61.4 4.7 %shard_map.79 = f32[1024,512]{1,0:T(8,128)S(1)} custom-call(bf16[1024,2048]{1,0:T(8,128)(2,1)} %get-tuple-element.5.w_ref, bf16[2048,512]{1,0:T(8,128)(2,1)S(1)} %bitcast.47), custom_call_target="tpu_custom_call" | custom-call | tf_op jit(solution)/shard_map/pallas_call | solution.py:117
  66.1 1.3 %copy-done.1 = f32[1024,512]{1,0:T(8,128)} copy-done((f32[1024,512]{1,0:T(8,128)}, f32[1024,512]{1,0:T(8,128)S(1)}, u32[]{:S(2)}) %copy-start.1) | copy-done | bytes 2097176
  67.5 3.7 %collective-permute-start.5 = (bf16[16,2048]{1,0:T(8,128)(2,1)}, bf16[16,2048]{1,0:T(8,128)(2,1)}, u32[]{:S(2)}, u32[]{:S(2)}) collective-permute-start(bf16[16,2048]{1,0:T(8,128)(2,1)} %copy-done.7), channel_id=1, source_target_pairs={{0,6},{1,7},{2,0},{3,1},{4,2},{5,3},{6,4},{7,5},{8,14},{9,15},{10,... | collective-permute-start | bytes 196616 | tf_op jit(solution)/shard_map/ppermute | solution.py:179
  71.1 1.0 collective-permute-start.3
  72.2 1.7 %collective-permute-done.5 = bf16[16,2048]{1,0:T(8,128)(2,1)} collective-permute-done((bf16[16,2048]{1,0:T(8,128)(2,1)}, bf16[16,2048]{1,0:T(8,128)(2,1)}, u32[]{:S(2)}, u32[]{:S(2)}) %collective-permute-start.5) | collective-permute-done | bytes 65568 | tf_op jit(solution)/shard_map/ppermute | solution.py:179
  73.9 3.0 %collective-permute-done.4 = bf16[16,2048]{1,0:T(8,128)(2,1)} collective-permute-done((bf16[16,2048]{1,0:T(8,128)(2,1)}, bf16[16,2048]{1,0:T(8,128)(2,1)}, u32[]{:S(2)}, u32[]{:S(2)}) %collective-permute-start.4) | collective-permute-done | bytes 65568 | tf_op jit(solution)/shard_map/ppermute | solution.py:179
  76.8 1.8 %collective-permute-done.3 = bf16[16,2048]{1,0:T(8,128)(2,1)} collective-permute-done((bf16[16,2048]{1,0:T(8,128)(2,1)}, bf16[16,2048]{1,0:T(8,128)(2,1)}, u32[]{:S(2)}, u32[]{:S(2)}) %collective-permute-start.3) | collective-permute-done | bytes 65568 | tf_op jit(solution)/shard_map/ppermute | solution.py:179
  78.6 0.9 pad_maximum_fusion.1.m_ref
  79.6 1.0 copy-done.3
  80.6 30.8 %shard_map.78 = f32[256,1024]{1,0:T(8,128)S(1)} custom-call(bf16[16,6144]{1,0:T(8,128)(2,1)S(1)} %pad_maximum_fusion.1.m_ref, bf16[3,256,192]{2,1,0:T(8,128)(2,1)S(1)} %copy-done.4, bf16[4,1024,192]{2,1,0:T(8,128)(2,1)S(1)} %add_convert_fusion.oh_ref, bf16[4,256,192]{2,1,0:T(8,128)(2,1)S(1)} %copy-done.3), custom_call_target="tpu_custom_call" | custom-call | tf_op jit(solution)/shard_map/pallas_call | solution.py:93
  111.7 1.9 %collective-permute-done.6 = f32[128,1024]{1,0:T(8,128)S(1)} collective-permute-done((f32[128,1024]{1,0:T(8,128)S(1)}, f32[128,1024]{1,0:T(8,128)S(1)}, u32[]{:S(2)}, u32[]{:S(2)}) %collective-permute-start.6) | collective-permute-done | bytes 524320 | tf_op jit(solution)/shard_map/ppermute | solution.py:191
  113.6 0.9 multiply_bitcast_fusion
  (50 shorter events, 6.1 us)
Async XLA Ops:
  7.2 10.1 %copy-start = (bf16[1024,512]{1,0:T(8,128)(2,1)S(1)}, bf16[1024,512]{1,0:T(8,128)(2,1)}, u32[]{:S(2)}) copy-start(bf16[1024,512]{1,0:T(8,128)(2,1)} %param.7) | copy-start | bytes 3145732
  7.2 107.3 %reduce-scatter.2.cloned.1.call-start = ((), (), s32[]{:S(2)}) async-start(), calls=%async_computation.1 | async-start | bytes 2359296 | tf_op jit(solution)/shard_map/reduce_scatter | solution.py:186
  12.8 14.3 %collective-permute-start.2 = (bf16[13,512]{1,0:T(8,128)(2,1)}, bf16[13,512]{1,0:T(8,128)(2,1)}, u32[]{:S(2)}, u32[]{:S(2)}) collective-permute-start(bf16[13,512]{1,0:T(8,128)(2,1)} %get-tuple-element.15), channel_id=1, source_target_pairs={{0,24},{8,16},{16,8},{24,0},{1,25},{9,17},{17,9},{25,1},{2,26},{10... | collective-permute-start | bytes 39944 | tf_op jit(solution)/shard_map/ppermute | solution.py:139
  16.8 10.6 %collective-permute-start.1 = (bf16[13,512]{1,0:T(8,128)(2,1)}, bf16[13,512]{1,0:T(8,128)(2,1)}, u32[]{:S(2)}, u32[]{:S(2)}) collective-permute-start(bf16[13,512]{1,0:T(8,128)(2,1)} %get-tuple-element.16), channel_id=1, source_target_pairs={{0,16},{8,24},{16,0},{24,8},{1,17},{9,25},{17,1},{25,9},{2,18},{10... | collective-permute-start | bytes 39944 | tf_op jit(solution)/shard_map/ppermute | solution.py:139
  19.6 4.9 %copy-start.9 = (s32[1024,12]{0,1:T(8,128)S(1)}, s32[1024,12]{0,1:T(8,128)}, u32[]{:S(2)}) copy-start(s32[1024,12]{0,1:T(8,128)} %param.10) | copy-start | bytes 147460
  21.0 38.8 %collective-permute-start.9 = (bf16[512,512]{1,0:T(8,128)(2,1)}, bf16[512,512]{1,0:T(8,128)(2,1)}, u32[]{:S(2)}, u32[]{:S(2)}) collective-permute-start(bf16[512,512]{1,0:T(8,128)(2,1)} %get-tuple-element.7), channel_id=1, source_target_pairs={{0,24},{8,16},{16,8},{24,0},{1,25},{9,17},{17,9},{25,1},{2,26},{10... | collective-permute-start | bytes 1572872 | tf_op jit(solution)/shard_map/ppermute | solution.py:139
  22.5 37.3 %collective-permute-start.8 = (bf16[512,512]{1,0:T(8,128)(2,1)}, bf16[512,512]{1,0:T(8,128)(2,1)}, u32[]{:S(2)}, u32[]{:S(2)}) collective-permute-start(bf16[512,512]{1,0:T(8,128)(2,1)} %get-tuple-element.8), channel_id=1, source_target_pairs={{0,16},{8,24},{16,0},{24,8},{1,17},{9,25},{17,1},{25,9},{2,18},{10... | collective-permute-start | bytes 1572872 | tf_op jit(solution)/shard_map/ppermute | solution.py:139
  22.5 37.3 %collective-permute-start.7 = (bf16[512,512]{1,0:T(8,128)(2,1)}, bf16[512,512]{1,0:T(8,128)(2,1)}, u32[]{:S(2)}, u32[]{:S(2)}) collective-permute-start(bf16[512,512]{1,0:T(8,128)(2,1)} %get-tuple-element.9), channel_id=1, source_target_pairs={{0,8},{8,0},{16,24},{24,16},{1,9},{9,1},{17,25},{25,17},{2,10},{10... | collective-permute-start | bytes 1572872 | tf_op jit(solution)/shard_map/ppermute | solution.py:139
  26.6 21.2 %copy-start.4 = (bf16[3,256,192]{2,1,0:T(8,128)(2,1)S(1)}, bf16[3,256,192]{2,1,0:T(8,128)(2,1)}, u32[]{:S(2)}) copy-start(bf16[3,256,192]{2,1,0:T(8,128)(2,1)} %constant.73.clone.pick_ref) | copy-start | bytes 884740
  27.2 19.7 %collective-permute-start = (bf16[13,512]{1,0:T(8,128)(2,1)}, bf16[13,512]{1,0:T(8,128)(2,1)S(1)}, u32[]{:S(2)}, u32[]{:S(2)}) collective-permute-start(bf16[13,512]{1,0:T(8,128)(2,1)} %get-tuple-element.17), channel_id=1, source_target_pairs={{0,8},{8,0},{16,24},{24,16},{1,9},{9,1},{17,25},{25,17},{2,10},{10... | collective-permute-start | bytes 39944 | tf_op jit(solution)/shard_map/ppermute | solution.py:139
  27.3 32.4 %copy-start.2 = (bf16[4,256,192]{2,1,0:T(8,128)(2,1)}, bf16[4,256,192]{2,1,0:T(8,128)(2,1)S(1)}, u32[]{:S(2)}) copy-start(bf16[4,256,192]{2,1,0:T(8,128)(2,1)S(1)} %constant_dynamic-slice_fusion.2.ohr_ref) | copy-start | bytes 1179652
  27.3 32.5 %copy-start.8 = (bf16[1,512,512]{2,1,0:T(8,128)(2,1)S(1)}, bf16[1,512,512]{2,1,0:T(8,128)(2,1)}, u32[]{:S(2)}) copy-start(bf16[1,512,512]{2,1,0:T(8,128)(2,1)} %get-tuple-element.6) | copy-start | bytes 1572868
  47.8 12.0 %copy-start.7 = (bf16[16,2048]{1,0:T(8,128)(2,1)}, bf16[16,2048]{1,0:T(8,128)(2,1)S(1)}, u32[]{:S(2)}) copy-start(bf16[16,2048]{1,0:T(8,128)(2,1)S(1)} %pad.4.m_ref) | copy-start | bytes 196612
  58.8 1.0 copy-start.5
  66.1 1.3 %copy-start.1 = (f32[1024,512]{1,0:T(8,128)}, f32[1024,512]{1,0:T(8,128)S(1)}, u32[]{:S(2)}) copy-start(f32[1024,512]{1,0:T(8,128)S(1)} %shard_map.79) | copy-start | bytes 6291460
  67.5 6.4 %collective-permute-start.5 = (bf16[16,2048]{1,0:T(8,128)(2,1)}, bf16[16,2048]{1,0:T(8,128)(2,1)}, u32[]{:S(2)}, u32[]{:S(2)}) collective-permute-start(bf16[16,2048]{1,0:T(8,128)(2,1)} %copy-done.7), channel_id=1, source_target_pairs={{0,6},{1,7},{2,0},{3,1},{4,2},{5,3},{6,4},{7,5},{8,14},{9,15},{10,... | collective-permute-start | bytes 196616 | tf_op jit(solution)/shard_map/ppermute | solution.py:179
  71.1 5.7 %collective-permute-start.4 = (bf16[16,2048]{1,0:T(8,128)(2,1)}, bf16[16,2048]{1,0:T(8,128)(2,1)}, u32[]{:S(2)}, u32[]{:S(2)}) collective-permute-start(bf16[16,2048]{1,0:T(8,128)(2,1)} %copy-done.7), channel_id=1, source_target_pairs={{0,4},{1,5},{2,6},{3,7},{4,0},{5,1},{6,2},{7,3},{8,12},{9,13},{10,... | collective-permute-start | bytes 196616 | tf_op jit(solution)/shard_map/ppermute | solution.py:179
  71.1 7.5 %collective-permute-start.3 = (bf16[16,2048]{1,0:T(8,128)(2,1)}, bf16[16,2048]{1,0:T(8,128)(2,1)}, u32[]{:S(2)}, u32[]{:S(2)}) collective-permute-start(bf16[16,2048]{1,0:T(8,128)(2,1)} %copy-done.7), channel_id=1, source_target_pairs={{0,2},{1,3},{2,4},{3,5},{4,6},{5,7},{6,0},{7,1},{8,10},{9,11},{10,... | collective-permute-start | bytes 196616 | tf_op jit(solution)/shard_map/ppermute | solution.py:179
  79.6 1.1 copy-start.3
  80.6 30.8 %copy-start.6 = (f32[256,1024]{1,0:T(8,128)S(1)}, f32[256,1024]{1,0:T(8,128)}, u32[]{:S(2)}) copy-start(f32[256,1024]{1,0:T(8,128)} %copy-done.5) | copy-start | bytes 3145732
  111.6 2.0 %collective-permute-start.6 = (f32[128,1024]{1,0:T(8,128)S(1)}, f32[128,1024]{1,0:T(8,128)S(1)}, u32[]{:S(2)}, u32[]{:S(2)}) collective-permute-start(f32[128,1024]{1,0:T(8,128)S(1)} %constant_dynamic-slice_fusion.1), channel_id=1, source_target_pairs={{0,1},{1,0},{2,3},{3,2},{4,5},{5,4},{6,7},{7,6},{8,9},{9,8},{10,11... | collective-permute-start | bytes 1572872 | tf_op jit(solution)/shard_map/ppermute | solution.py:191
Sparse Core Ops, SparseCore 0:
  67.6 36.0 reduce-scatter.1

commit v5 on v4

--- a/solution.py
+++ b/solution.py
@@ -24,13 +24,12 @@
     npar = table.shape[1]
     width = LEVELS ** GROUP
     n_groups = -(-npar // GROUP)
-    maps = []
+    codes = []
     for start in range(0, n_groups * GROUP, GROUP):
         code = jnp.zeros((table.shape[0],), jnp.int32)
         for j in range(start, start + GROUP):
             code = code * LEVELS + (table[:, j] if j < npar else 0)
-        onehot = (code[:, None] == jnp.arange(width, dtype=jnp.int32)[None, :]).astype(jnp.bfloat16)
-        maps.append(jnp.concatenate([onehot] * 3, axis=1))
+        codes.append(code)
     pick = np.zeros((GROUP, n_groups * width, 3 * LEVELS * rows), np.float32)
     for g in range(n_groups):
         for c in range(width):
@@ -40,15 +39,29 @@
                 col = degree * rows + j if j < npar else 0
                 for piece in range(3):
                     pick[pos, g * width + c, piece * LEVELS * rows + col] = 1.0
-    return jnp.stack(maps), jnp.asarray(pick, jnp.bfloat16)
-
-
-def gram_kernel(m_ref, pick_ref, oh_ref, ohr_ref, gram_ref, *wt_refs, npar):
-    @pl.when(pl.program_id(0) == 0)
+    return jnp.stack(codes)[:, :, None], jnp.asarray(pick, jnp.bfloat16)
+
+
+def gram_kernel(row0_ref, *refs, npar, n_meta, per, picked, with_weighted):
+    metas = refs[:n_meta]
+    pick_ref, code_ref, gram_ref = refs[n_meta:n_meta + 3]
+    wt_refs = refs[n_meta + 3:-1] if with_weighted else ()
+    oh_ref = refs[-1]
+    step = pl.program_id(0)
+    groups, _, width3 = oh_ref.shape
+    width = width3 // 3
+
+    @pl.when(step == 0)
     def _():
         gram_ref[...] = jnp.zeros_like(gram_ref)
-
-    coords = m_ref[...].astype(jnp.float32)
+        lanes = lax.broadcasted_iota(jnp.int32, (1, width3), 1) % width
+        for g in range(groups):
+            oh_ref[g] = (code_ref[g] == lanes).astype(jnp.bfloat16)
+
+    m = metas[0][...]
+    for k in range(1, n_meta):
+        m = jnp.where(step >= k * per, metas[k][...], m)
+    coords = m.astype(jnp.float32)
     values = [jnp.ones_like(coords), coords]
     for degree in range(1, LEVELS - 1):
         nxt = ((2.0 * degree + 1.0) * coords * values[-1] - degree * values[-2]) / (degree + 1.0)
@@ -61,14 +74,13 @@
     for pos in range(pick_ref.shape[0]):
         factor = jnp.dot(pick_ref[pos], pieces, preferred_element_type=jnp.float32)
         combos = factor if combos is None else combos * factor
-    groups = oh_ref.shape[0]
-    width = combos.shape[0] // groups
+    row0 = pl.multiple_of(row0_ref[0], picked)
     basis = None
     rows = None
     for g in range(groups):
         piece = split3(combos[g * width:(g + 1) * width])
         factor = jnp.dot(oh_ref[g], piece, preferred_element_type=jnp.float32)
-        part = jnp.dot(ohr_ref[g], piece, preferred_element_type=jnp.float32)
+        part = jnp.dot(oh_ref[g, pl.ds(row0, picked), :], piece, preferred_element_type=jnp.float32)
         basis = factor if basis is None else basis * factor
         rows = part if rows is None else rows * part
     w = coords[npar:npar + 1]
@@ -77,34 +89,46 @@
     gram_ref[...] += lax.dot_general(
         weighted_rows, low, (((1,), (1,)), ((), ())), preferred_element_type=jnp.float32
     )
-    if wt_refs:
+    if with_weighted:
         wt_refs[0][...] = (w * basis).astype(jnp.bfloat16)
 
 
-def gram_rows(meta, pick, rhs, rhs_rows, npar, with_weighted, block=256):
-    rows, samples = meta.shape
-    groups, terms, width3 = rhs.shape
-    picked = rhs_rows.shape[1]
-    out_specs = [pl.BlockSpec((picked, terms), lambda i: (0, 0))]
+def gram_rows(metas, pick, codes, row0, picked, npar, with_weighted, block=256):
+    rows, samples = metas[0].shape
+    per = samples // block
+    n_meta = len(metas)
+    groups, terms, _ = codes.shape
+    width3 = 3 * LEVELS ** GROUP
+
+    def meta_map(k):
+        return lambda i, r: (0, jnp.clip(i - k * per, 0, per - 1))
+
+    out_specs = [pl.BlockSpec((picked, terms), lambda i, r: (0, 0))]
     out_shape = [jax.ShapeDtypeStruct((picked, terms), jnp.float32)]
     if with_weighted:
-        out_specs.append(pl.BlockSpec((terms, block), lambda i: (0, i)))
+        out_specs.append(pl.BlockSpec((terms, block), lambda i, r: (0, i)))
         out_shape.append(jax.ShapeDtypeStruct((terms, samples), jnp.bfloat16))
-    return pl.pallas_call(
-        functools.partial(gram_kernel, npar=npar),
-        grid=(samples // block,),
-        in_specs=[
-            pl.BlockSpec((rows, block), lambda i: (0, i)),
-            pl.BlockSpec(pick.shape, lambda i: (0, 0, 0)),
-            pl.BlockSpec((groups, terms, width3), lambda i: (0, 0, 0)),
-            pl.BlockSpec((groups, picked, width3), lambda i: (0, 0, 0)),
+    grid_spec = pltpu.PrefetchScalarGridSpec(
+        num_scalar_prefetch=1,
+        grid=(n_meta * per,),
+        in_specs=[pl.BlockSpec((rows, block), meta_map(k)) for k in range(n_meta)] + [
+            pl.BlockSpec(pick.shape, lambda i, r: (0, 0, 0)),
+            pl.BlockSpec(codes.shape, lambda i, r: (0, 0, 0)),
         ],
         out_specs=out_specs,
+        scratch_shapes=[pltpu.VMEM((groups, terms, width3), jnp.bfloat16)],
+    )
+    kernel = functools.partial(
+        gram_kernel, npar=npar, n_meta=n_meta, per=per, picked=picked, with_weighted=with_weighted
+    )
+    return pl.pallas_call(
+        kernel,
+        grid_spec=grid_spec,
         out_shape=out_shape,
         compiler_params=pltpu.CompilerParams(
             dimension_semantics=("arbitrary",), vmem_limit_bytes=48 * 1024 * 1024
         ),
-    )(meta, pick, rhs, rhs_rows)
+    )(row0, *metas, pick, codes)
 
 
 def moment_kernel(w_ref, p_ref, o_ref, *, scale):
@@ -156,19 +180,20 @@
     sel = sel.astype(jnp.bfloat16)
 
     prof_c = jnp.einsum("eis,sq->eiq", sel, profiles, preferred_element_type=jnp.float32).astype(jnp.bfloat16)
-    meta = jnp.concatenate([params, weights[None, :]], axis=0)
+    npar = params.shape[0]
+    rows = -(-(npar + 1) // 16) * 16
+    meta = jnp.concatenate(
+        [params, weights[None, :], jnp.zeros((rows - npar - 1, samples), params.dtype)], axis=0
+    )
     meta_c = jnp.einsum("eis,js->eji", sel, meta, preferred_element_type=jnp.float32).astype(jnp.bfloat16)
     meta_r = exchange(meta_c, groups)
     prof_r = exchange(prof_c, groups)
 
-    npar = params.shape[0]
     q = profiles.shape[1]
     terms = table.shape[0]
     slots = groups * cap
-    rows = -(-(npar + 1) // 16) * 16
     prof_r = prof_r.reshape(slots, q)
-    meta_r = jnp.transpose(meta_r, (1, 0, 2)).reshape(npar + 1, slots)
-    meta_r = jnp.pad(meta_r, ((0, rows - npar - 1), (0, 0)))
+    meta_r = jnp.transpose(meta_r, (1, 0, 2)).reshape(rows, slots)
 
     me = lax.axis_index("grp")
     core = me % 2
@@ -179,12 +204,12 @@
         lax.ppermute(meta_r, "grp", [(i, (i + 2 * k) % members) for i in range(members)])
         for k in range(1, pairs)
     ]
-    rhs, pick = term_maps(table, rows)
-    rhs_rows = lax.dynamic_slice_in_dim(rhs, chip * 2 * own_rows, 2 * own_rows, axis=1)
-    gram_own, weighted_t = gram_rows(meta_r, pick, rhs, rhs_rows, npar, True)
+    codes, pick = term_maps(table, rows)
+    row0 = (chip * 2 * own_rows).astype(jnp.int32).reshape(1)
+    gram_own, weighted_t = gram_rows([meta_r], pick, codes, row0, 2 * own_rows, npar, True)
     moment_part = moment_sums(weighted_t, prof_r, scale)
     moment_rows = lax.psum_scatter(moment_part, "grp", scatter_dimension=0, tiled=True)
-    (gram_oth,) = gram_rows(jnp.concatenate(others, axis=1), pick, rhs, rhs_rows, npar, False)
+    (gram_oth,) = gram_rows(others, pick, codes, row0, 2 * own_rows, npar, False)
     gram_chip = gram_own + gram_oth
     keep = lax.dynamic_slice_in_dim(gram_chip, core * own_rows, own_rows, axis=0)
     send = lax.dynamic_slice_in_dim(gram_chip, (1 - core) * own_rows, own_rows, axis=0)

time: 122 us -> 118 us (0.967)
  other arithmetic: 7.88 us -> 4.48 us
  waiting for transfers between devices: 27.9 us -> 24.6 us
  starting transfers between devices: 12.8 us -> 15.5 us
  Pallas kernels: 46.4 us -> 48.9 us
    ppermute x3, waiting for transfers between devices: 6.49 us -> 3.23 us  [on_device(): lax.ppermute(meta_r, 'grp', [(i, (i + 2 * k) % members) for i in range(me...]
    pallas_call x2, Pallas kernels: 41.8 us -> 44.3 us  [gram_rows(): pl.pallas_call(kernel, grid_spec=grid_spec, out_shape=out_shape, compiler...]
    another operation x3 -> x0, other arithmetic: 1.73 us -> none  [term_maps(): return (jnp.stack(maps), jnp.asarray(pick, jnp.bfloat16))]
    ppermute x6, starting transfers between devices: 8.04 us -> 9.61 us  [exchange(): got.append(lax.ppermute(send, 'elem', [(i, i ^ m) for i in range(groups)]))]
  transfers between devices with their start and end apart: 11 -> 11, of which waited for: 5 -> 6; matrix products, arithmetic and copies ran while one was open for 8% -> 4% of each run, Pallas kernels for 34% -> 38%
where the time goes in v5:
time: 118 us
  Pallas kernels  48.9 us (41%)
  waiting for transfers between devices  24.6 us (21%)
  starting transfers between devices  15.5 us (13%)
  between operations  14.3 us (12%)
  local copies, waits for them, and re-layouts  5.12 us (4%)
  matrix products  4.84 us (4%)
  other arithmetic  4.48 us (4%)
    pallas_call x2, Pallas kernels, gram_rows(): pl.pallas_call(kernel, grid_spec=grid_spec, out_shape=out_shape, compiler...  44.3 us
    ppermute x6, waiting for transfers between devices, exchange(): got.append(lax.ppermute(send, 'elem', [(i, i ^ m) for i in range(groups)]))  19.5 us
    ppermute x6, starting transfers between devices, exchange(): got.append(lax.ppermute(send, 'elem', [(i, i ^ m) for i in range(groups)]))  9.61 us
    ppermute x3, starting transfers between devices, on_device(): lax.ppermute(meta_r, 'grp', [(i, (i + 2 * k) % members) for i in range(me...  5.77 us
    pallas_call x1, Pallas kernels, moment_sums(): pl.pallas_call(functools.partial(moment_kernel, scale=scale), grid=(terms...  4.69 us
    ppermute x3, waiting for transfers between devices, on_device(): lax.ppermute(meta_r, 'grp', [(i, (i + 2 * k) % members) for i in range(me...  3.23 us
  transfers between devices with their start and end apart: 11, of which 6 were waited for; matrix products, arithmetic and copies ran while one was open for 4% of the time, Pallas kernels for 38%

profile of v5, /device:TPU:0, one launch (start us, length us, event | category | flops | bytes accessed | tf_op | source)
XLA Modules:
  0.0 117.8 jit_solution(7882736127838566530)
XLA Ops:
  7.2 1.3 %fusion.16 = f32[1024]{0:T(1024)S(1)} fusion(s32[1024]{0:T(1024)} %param.9), kind=kOutput, calls=%fused_computation.15 | convolution fusion | flops 9452544 | bytes 8192 | tf_op jit(solution)/shard_map/dot_general | solution.py:177
  8.5 0.7 iota_compare_fusion.8
  9.5 2.3 %fusion.9 = bf16[4,512,512]{2,1,0:T(8,128)(2,1)S(1)} fusion(pred[512,1024]{1,0:T(8,128)(4,1)S(1)} %iota_compare_fusion.2, pred[4,1024]{1,0:T(4,128)(4,1)S(1)} %iota_compare_fusion.8, bf16[1024,512]{1,0:T(8,128)(2,1)S(1)} %copy-done), kind=kOutput, calls=%fused_computation.12 | convolution fusion | flops 2150629376 | bytes 3674112 | tf_op jit(solution)/shard_map/eis,sq->eiq/dot_general | solution.py:182
  11.9 1.4 %constant_dynamic-slice_fusion = (bf16[1,512,512]{2,1,0:T(8,128)(2,1)}, bf16[512,512]{1,0:T(8,128)(2,1)}, bf16[512,512]{1,0:T(8,128)(2,1)}, bf16[512,512]{1,0:T(8,128)(2,1)}) fusion(bf16[4,512,512]{2,1,0:T(8,128)(2,1)S(1)} %fusion.9, s32[]{:T(128)S(6)} %select_n.41, s32[]{:T(128)S(6)} %select_n.44, s32[]{:T(128)S(6)} %select_n.43, s32[]{:T(128)S(6)} %select_n.42), kind=kLoop, calls=%fused_computation.39 | loop fusion | bytes 4194320 | tf_op jit(solution)/shard_map/jit(dynamic_index_in_dim)/dynamic_slice | solution.py:160
  13.3 3.9 %collective-permute-start.9 = (bf16[512,512]{1,0:T(8,128)(2,1)}, bf16[512,512]{1,0:T(8,128)(2,1)}, u32[]{:S(2)}, u32[]{:S(2)}) collective-permute-start(bf16[512,512]{1,0:T(8,128)(2,1)} %get-tuple-element.7), channel_id=1, source_target_pairs={{0,24},{8,16},{16,8},{24,0},{1,25},{9,17},{17,9},{25,1},{2,26},{10... | collective-permute-start | bytes 1572872 | tf_op jit(solution)/shard_map/ppermute | solution.py:163
  17.9 1.2 %fusion.12 = bf16[16,4,512]{2,0,1:T(8,128)(2,1)S(1)} fusion(pred[512,1024]{1,0:T(8,128)(4,1)S(1)} %iota_compare_fusion.2, pred[4,1024]{1,0:T(4,128)(4,1)S(1)} %iota_compare_fusion.8, bf16[1,1024]{1,0:T(2,128)(2,1)S(1)} %broadcast_in_dim.26, bf16[12,1024]{1,0:T(8,128)(2,1)S(1)} %copy-done.10, bf16[16]{0:T(256)(128)(2,1)S(1)} %pad.14.clone), kind=kOutput, calls=%fused_computation.13 | convolution fusion | flops 69337088 | bytes 620576 | tf_op jit(solution)/shard_map/eis,js->eji/dot_general | solution.py:188
  19.7 2.9 %collective-permute-start.2 = (bf16[16,512]{1,0:T(8,128)(2,1)S(1)}, bf16[16,512]{1,0:T(8,128)(2,1)S(1)}, u32[]{:S(2)}, u32[]{:S(2)}) collective-permute-start(bf16[16,512]{1,0:T(8,128)(2,1)S(1)} %get-tuple-element.15), channel_id=1, source_target_pairs={{0,24},{8,16},{16,8},{24,0},{1,25},{9,17},{17,9},{25,1},{2,26},{10... | collective-permute-start | bytes 49160 | tf_op jit(solution)/shard_map/ppermute | solution.py:163
  23.2 17.8 %collective-permute-done.2 = bf16[16,512]{1,0:T(8,128)(2,1)S(1)} collective-permute-done((bf16[16,512]{1,0:T(8,128)(2,1)S(1)}, bf16[16,512]{1,0:T(8,128)(2,1)S(1)}, u32[]{:S(2)}, u32[]{:S(2)}) %collective-permute-start.2) | collective-permute-done | bytes 16416 | tf_op jit(solution)/shard_map/ppermute | solution.py:163
  41.1 1.7 %collective-permute-start = (bf16[16,512]{1,0:T(8,128)(2,1)}, bf16[16,512]{1,0:T(8,128)(2,1)}, u32[]{:S(2)}, u32[]{:S(2)}) collective-permute-start(bf16[16,512]{1,0:T(8,128)(2,1)} %get-tuple-element.17), channel_id=1, source_target_pairs={{0,8},{8,0},{16,24},{24,16},{1,9},{9,1},{17,25},{25,17},{2,10},{10... | collective-permute-start | bytes 49160 | tf_op jit(solution)/shard_map/ppermute | solution.py:163
  43.5 1.6 %collective-permute-done = bf16[16,512]{1,0:T(8,128)(2,1)} collective-permute-done((bf16[16,512]{1,0:T(8,128)(2,1)}, bf16[16,512]{1,0:T(8,128)(2,1)}, u32[]{:S(2)}, u32[]{:S(2)}) %collective-permute-start) | collective-permute-done | bytes 16416 | tf_op jit(solution)/shard_map/ppermute | solution.py:163
  45.1 0.8 maximum_bitcast_fusion
  45.9 11.6 %shard_map.77 = (f32[256,1024]{1,0:T(8,128)S(1)}, bf16[1024,2048]{1,0:T(8,128)(2,1)}) custom-call(s32[1]{0:T(128)} %bitcast.row0_ref, bf16[16,2048]{1,0:T(8,128)(2,1)S(1)} %bitcast.46, bf16[3,256,192]{2,1,0:T(8,128)(2,1)S(1)} %copy-done.2, s32[4,1024,1]{2,1,0:T(8,128)S(1)} %copy.9.refs_2_.refs_4_), custom_call_target="tpu_custom_call" | custom-call | tf_op jit(solution)/shard_map/pallas_call | solution.py:124
  57.5 1.0 copy-done.3
  58.5 1.6 %pad_maximum_fusion = bf16[4,512,512]{2,1,0:T(8,128)(2,1)S(1)} fusion(bf16[1,512,512]{2,1,0:T(8,128)(2,1)} %bitcast.22, bf16[1,512,512]{2,1,0:T(8,128)(2,1)} %bitcast.20, bf16[1,512,512]{2,1,0:T(8,128)(2,1)} %bitcast.18, bf16[1,512,512]{2,1,0:T(8,128)(2,1)S(1)} %copy-done.6), kind=kLoop, calls=%fused_computation.10 | loop fusion | flops 3145728 | bytes 4194304 | tf_op jit(solution)/shard_map/stack | solution.py:164
  60.2 4.7 %shard_map.79 = f32[1024,512]{1,0:T(8,128)S(1)} custom-call(bf16[1024,2048]{1,0:T(8,128)(2,1)} %get-tuple-element.5.w_ref, bf16[2048,512]{1,0:T(8,128)(2,1)S(1)} %bitcast.45), custom_call_target="tpu_custom_call" | custom-call | tf_op jit(solution)/shard_map/pallas_call | solution.py:141
  64.9 1.3 %copy-done.1 = f32[1024,512]{1,0:T(8,128)} copy-done((f32[1024,512]{1,0:T(8,128)}, f32[1024,512]{1,0:T(8,128)S(1)}, u32[]{:S(2)}) %copy-start.1) | copy-done | bytes 2097176
  66.2 1.8 %collective-permute-start.3 = (bf16[16,2048]{1,0:T(8,128)(2,1)}, bf16[16,2048]{1,0:T(8,128)(2,1)}, u32[]{:S(2)}, u32[]{:S(2)}) collective-permute-start(bf16[16,2048]{1,0:T(8,128)(2,1)} %bitcast.47), channel_id=1, source_target_pairs={{0,2},{1,3},{2,4},{3,5},{4,6},{5,7},{6,0},{7,1},{8,10},{9,11},{10,... | collective-permute-start | bytes 196616 | tf_op jit(solution)/shard_map/ppermute | solution.py:204
  68.1 2.6 %collective-permute-start.4 = (bf16[16,2048]{1,0:T(8,128)(2,1)}, bf16[16,2048]{1,0:T(8,128)(2,1)}, u32[]{:S(2)}, u32[]{:S(2)}) collective-permute-start(bf16[16,2048]{1,0:T(8,128)(2,1)} %bitcast.48), channel_id=1, source_target_pairs={{0,4},{1,5},{2,6},{3,7},{4,0},{5,1},{6,2},{7,3},{8,12},{9,13},{10,... | collective-permute-start | bytes 196616 | tf_op jit(solution)/shard_map/ppermute | solution.py:204
  70.6 1.3 %collective-permute-start.5 = (bf16[16,2048]{1,0:T(8,128)(2,1)}, bf16[16,2048]{1,0:T(8,128)(2,1)}, u32[]{:S(2)}, u32[]{:S(2)}) collective-permute-start(bf16[16,2048]{1,0:T(8,128)(2,1)} %bitcast.49), channel_id=1, source_target_pairs={{0,6},{1,7},{2,0},{3,1},{4,2},{5,3},{6,4},{7,5},{8,14},{9,15},{10,... | collective-permute-start | bytes 196616 | tf_op jit(solution)/shard_map/ppermute | solution.py:204
  72.6 0.9 collective-permute-done.4.refs_1_
  73.5 1.7 %collective-permute-done.5.refs_2_ = bf16[16,2048]{1,0:T(8,128)(2,1)} collective-permute-done((bf16[16,2048]{1,0:T(8,128)(2,1)}, bf16[16,2048]{1,0:T(8,128)(2,1)}, u32[]{:S(2)}, u32[]{:S(2)}) %collective-permute-start.5) | collective-permute-done | bytes 65568 | tf_op jit(solution)/shard_map/ppermute | solution.py:204
  75.2 32.7 %shard_map.78 = f32[256,1024]{1,0:T(8,128)S(1)} custom-call(s32[1]{0:T(128)} %bitcast.row0_ref, bf16[16,2048]{1,0:T(8,128)(2,1)} %collective-permute-done.3.refs_0_, bf16[16,2048]{1,0:T(8,128)(2,1)} %collective-permute-done.4.refs_1_, bf16[16,2048]{1,0:T(8,128)(2,1)} %collective-permute-done.5.refs_2_, bf16[3,256,192]{2,1,0:T(8,128)(2,1)S(1)} %copy-done.2, ...), custom_call_target="tpu_custom_call" | custom-call | tf_op jit(solution)/shard_map/pallas_call | solution.py:124
  108.2 1.9 %collective-permute-done.6 = f32[128,1024]{1,0:T(8,128)S(1)} collective-permute-done((f32[128,1024]{1,0:T(8,128)S(1)}, f32[128,1024]{1,0:T(8,128)S(1)}, u32[]{:S(2)}, u32[]{:S(2)}) %collective-permute-start.6) | collective-permute-done | bytes 524320 | tf_op jit(solution)/shard_map/ppermute | solution.py:216
  110.1 0.9 multiply_bitcast_fusion
  (44 shorter events, 3.8 us)
Async XLA Ops:
  7.2 2.4 %copy-start = (bf16[1024,512]{1,0:T(8,128)(2,1)S(1)}, bf16[1024,512]{1,0:T(8,128)(2,1)}, u32[]{:S(2)}) copy-start(bf16[1024,512]{1,0:T(8,128)(2,1)} %param.7) | copy-start | bytes 3145732
  7.2 103.8 %reduce-scatter.2.cloned.1.call-start = ((), (), s32[]{:S(2)}) async-start(), calls=%async_computation.1 | async-start | bytes 2359296 | tf_op jit(solution)/shard_map/reduce_scatter | solution.py:211
  11.9 5.9 %copy-start.9 = (bf16[1024]{0:T(1024)(128)(2,1)S(1)}, bf16[1024]{0:T(1024)(128)(2,1)}, u32[]{:S(2)}) copy-start(bf16[1024]{0:T(1024)(128)(2,1)} %param.8) | copy-start | bytes 6148
  11.9 6.0 %copy-start.10 = (bf16[12,1024]{1,0:T(8,128)(2,1)S(1)}, bf16[12,1024]{1,0:T(8,128)(2,1)}, u32[]{:S(2)}) copy-start(bf16[12,1024]{1,0:T(8,128)(2,1)} %param.6) | copy-start | bytes 73732
  13.3 9.9 %copy-start.7 = (s32[1024,12]{0,1:T(8,128)S(1)}, s32[1024,12]{0,1:T(8,128)}, u32[]{:S(2)}) copy-start(s32[1024,12]{0,1:T(8,128)} %param.10) | copy-start | bytes 147460
  13.3 45.2 %collective-permute-start.9 = (bf16[512,512]{1,0:T(8,128)(2,1)}, bf16[512,512]{1,0:T(8,128)(2,1)}, u32[]{:S(2)}, u32[]{:S(2)}) collective-permute-start(bf16[512,512]{1,0:T(8,128)(2,1)} %get-tuple-element.7), channel_id=1, source_target_pairs={{0,24},{8,16},{16,8},{24,0},{1,25},{9,17},{17,9},{25,1},{2,26},{10... | collective-permute-start | bytes 1572872 | tf_op jit(solution)/shard_map/ppermute | solution.py:163
  17.2 41.3 %collective-permute-start.8 = (bf16[512,512]{1,0:T(8,128)(2,1)}, bf16[512,512]{1,0:T(8,128)(2,1)}, u32[]{:S(2)}, u32[]{:S(2)}) collective-permute-start(bf16[512,512]{1,0:T(8,128)(2,1)} %get-tuple-element.8), channel_id=1, source_target_pairs={{0,16},{8,24},{16,0},{24,8},{1,17},{9,25},{17,1},{25,9},{2,18},{10... | collective-permute-start | bytes 1572872 | tf_op jit(solution)/shard_map/ppermute | solution.py:163
  17.7 40.8 %collective-permute-start.7 = (bf16[512,512]{1,0:T(8,128)(2,1)}, bf16[512,512]{1,0:T(8,128)(2,1)}, u32[]{:S(2)}, u32[]{:S(2)}) collective-permute-start(bf16[512,512]{1,0:T(8,128)(2,1)} %get-tuple-element.9), channel_id=1, source_target_pairs={{0,8},{8,0},{16,24},{24,16},{1,9},{9,1},{17,25},{25,17},{2,10},{10... | collective-permute-start | bytes 1572872 | tf_op jit(solution)/shard_map/ppermute | solution.py:163
  19.1 26.8 %copy-start.2 = (bf16[3,256,192]{2,1,0:T(8,128)(2,1)S(1)}, bf16[3,256,192]{2,1,0:T(8,128)(2,1)}, u32[]{:S(2)}) copy-start(bf16[3,256,192]{2,1,0:T(8,128)(2,1)} %constant.71.clone.refs_1_.refs_3_) | copy-start | bytes 884740
  19.7 21.3 %collective-permute-start.2 = (bf16[16,512]{1,0:T(8,128)(2,1)S(1)}, bf16[16,512]{1,0:T(8,128)(2,1)S(1)}, u32[]{:S(2)}, u32[]{:S(2)}) collective-permute-start(bf16[16,512]{1,0:T(8,128)(2,1)S(1)} %get-tuple-element.15), channel_id=1, source_target_pairs={{0,24},{8,16},{16,8},{24,0},{1,25},{9,17},{17,9},{25,1},{2,26},{10... | collective-permute-start | bytes 49160 | tf_op jit(solution)/shard_map/ppermute | solution.py:163
  22.7 20.8 %collective-permute-start.1 = (bf16[16,512]{1,0:T(8,128)(2,1)}, bf16[16,512]{1,0:T(8,128)(2,1)}, u32[]{:S(2)}, u32[]{:S(2)}) collective-permute-start(bf16[16,512]{1,0:T(8,128)(2,1)} %get-tuple-element.16), channel_id=1, source_target_pairs={{0,16},{8,24},{16,0},{24,8},{1,17},{9,25},{17,1},{25,9},{2,18},{10... | collective-permute-start | bytes 49160 | tf_op jit(solution)/shard_map/ppermute | solution.py:163
  41.1 1.7 %copy-start.8 = (bf16[16,512]{1,0:T(8,128)(2,1)}, bf16[16,512]{1,0:T(8,128)(2,1)S(1)}, u32[]{:S(2)}) copy-start(bf16[16,512]{1,0:T(8,128)(2,1)S(1)} %collective-permute-done.2) | copy-start | bytes 49156
  41.1 4.1 %collective-permute-start = (bf16[16,512]{1,0:T(8,128)(2,1)}, bf16[16,512]{1,0:T(8,128)(2,1)}, u32[]{:S(2)}, u32[]{:S(2)}) collective-permute-start(bf16[16,512]{1,0:T(8,128)(2,1)} %get-tuple-element.17), channel_id=1, source_target_pairs={{0,8},{8,0},{16,24},{24,16},{1,9},{9,1},{17,25},{25,17},{2,10},{10... | collective-permute-start | bytes 49160 | tf_op jit(solution)/shard_map/ppermute | solution.py:163
  43.4 15.1 %copy-start.6 = (bf16[1,512,512]{2,1,0:T(8,128)(2,1)S(1)}, bf16[1,512,512]{2,1,0:T(8,128)(2,1)}, u32[]{:S(2)}) copy-start(bf16[1,512,512]{2,1,0:T(8,128)(2,1)} %get-tuple-element.6) | copy-start | bytes 1572868
  45.9 12.6 %copy-start.5 = (bf16[4,2,8,512]{3,2,0,1:T(8,128)(2,1)}, bf16[4,2,8,512]{3,2,0,1:T(8,128)(2,1)S(1)}, u32[]{:S(2)}) copy-start(bf16[4,2,8,512]{3,2,0,1:T(8,128)(2,1)S(1)} %copy.11) | copy-start | bytes 196612
  57.5 1.0 copy-start.3
  64.9 1.3 %copy-start.1 = (f32[1024,512]{1,0:T(8,128)}, f32[1024,512]{1,0:T(8,128)S(1)}, u32[]{:S(2)}) copy-start(f32[1024,512]{1,0:T(8,128)S(1)} %shard_map.79) | copy-start | bytes 6291460
  66.2 6.4 %collective-permute-start.3 = (bf16[16,2048]{1,0:T(8,128)(2,1)}, bf16[16,2048]{1,0:T(8,128)(2,1)}, u32[]{:S(2)}, u32[]{:S(2)}) collective-permute-start(bf16[16,2048]{1,0:T(8,128)(2,1)} %bitcast.47), channel_id=1, source_target_pairs={{0,2},{1,3},{2,4},{3,5},{4,6},{5,7},{6,0},{7,1},{8,10},{9,11},{10,... | collective-permute-start | bytes 196616 | tf_op jit(solution)/shard_map/ppermute | solution.py:204
  68.1 5.5 %collective-permute-start.4 = (bf16[16,2048]{1,0:T(8,128)(2,1)}, bf16[16,2048]{1,0:T(8,128)(2,1)}, u32[]{:S(2)}, u32[]{:S(2)}) collective-permute-start(bf16[16,2048]{1,0:T(8,128)(2,1)} %bitcast.48), channel_id=1, source_target_pairs={{0,4},{1,5},{2,6},{3,7},{4,0},{5,1},{6,2},{7,3},{8,12},{9,13},{10,... | collective-permute-start | bytes 196616 | tf_op jit(solution)/shard_map/ppermute | solution.py:204
  70.6 4.6 %collective-permute-start.5 = (bf16[16,2048]{1,0:T(8,128)(2,1)}, bf16[16,2048]{1,0:T(8,128)(2,1)}, u32[]{:S(2)}, u32[]{:S(2)}) collective-permute-start(bf16[16,2048]{1,0:T(8,128)(2,1)} %bitcast.49), channel_id=1, source_target_pairs={{0,6},{1,7},{2,0},{3,1},{4,2},{5,3},{6,4},{7,5},{8,14},{9,15},{10,... | collective-permute-start | bytes 196616 | tf_op jit(solution)/shard_map/ppermute | solution.py:204
  72.0 35.9 %copy-start.4 = (f32[256,1024]{1,0:T(8,128)S(1)}, f32[256,1024]{1,0:T(8,128)}, u32[]{:S(2)}) copy-start(f32[256,1024]{1,0:T(8,128)} %copy-done.3) | copy-start | bytes 3145732
  108.1 2.0 %collective-permute-start.6 = (f32[128,1024]{1,0:T(8,128)S(1)}, f32[128,1024]{1,0:T(8,128)S(1)}, u32[]{:S(2)}, u32[]{:S(2)}) collective-permute-start(f32[128,1024]{1,0:T(8,128)S(1)} %constant_dynamic-slice_fusion.1), channel_id=1, source_target_pairs={{0,1},{1,0},{2,3},{3,2},{4,5},{5,4},{6,7},{7,6},{8,9},{9,8},{10,11... | collective-permute-start | bytes 1572872 | tf_op jit(solution)/shard_map/ppermute | solution.py:216
Sparse Core Ops, SparseCore 0:
  66.3 37.5 reduce-scatter.1

commit v6 on v5

--- a/solution.py
+++ b/solution.py
@@ -93,7 +93,7 @@
         wt_refs[0][...] = (w * basis).astype(jnp.bfloat16)
 
 
-def gram_rows(metas, pick, codes, row0, picked, npar, with_weighted, block=256):
+def gram_rows(metas, pick, codes, row0, picked, npar, with_weighted, block=512):
     rows, samples = metas[0].shape
     per = samples // block
     n_meta = len(metas)
@@ -131,37 +131,46 @@
     )(row0, *metas, pick, codes)
 
 
-def moment_kernel(w_ref, p_ref, o_ref, *, scale):
-    o_ref[...] = jnp.dot(w_ref[...], p_ref[...], preferred_element_type=jnp.float32) * scale
+def moment_kernel(w_ref, *refs, scale):
+    p_refs, o_ref = refs[:-1], refs[-1]
+    cap = p_refs[0].shape[0]
+    acc = None
+    for k, p_ref in enumerate(p_refs):
+        part = jnp.dot(w_ref[:, k * cap:(k + 1) * cap], p_ref[...], preferred_element_type=jnp.float32)
+        acc = part if acc is None else acc + part
+    o_ref[...] = acc * scale
 
 
 def moment_sums(weighted_t, profiles, scale, block=256):
     terms, samples = weighted_t.shape
-    q = profiles.shape[1]
+    cap, q = profiles[0].shape
     return pl.pallas_call(
         functools.partial(moment_kernel, scale=scale),
         grid=(terms // block,),
-        in_specs=[
-            pl.BlockSpec((block, samples), lambda i: (i, 0)),
-            pl.BlockSpec((samples, q), lambda i: (0, 0)),
-        ],
+        in_specs=[pl.BlockSpec((block, samples), lambda i: (i, 0))]
+        + [pl.BlockSpec((cap, q), lambda i: (0, 0)) for _ in profiles],
         out_specs=pl.BlockSpec((block, q), lambda i: (i, 0)),
         out_shape=jax.ShapeDtypeStruct((terms, q), jnp.float32),
         compiler_params=pltpu.CompilerParams(
             dimension_semantics=("arbitrary",), vmem_limit_bytes=48 * 1024 * 1024
         ),
-    )(weighted_t, profiles)
+    )(weighted_t, *profiles)
 
 
 def exchange(blocks, groups):
     if groups & (groups - 1):
-        return lax.all_to_all(blocks, "elem", 0, 0, tiled=True)
-    me = lax.axis_index("elem")
-    got = [lax.dynamic_index_in_dim(blocks, me, 0, keepdims=False)]
+        got = lax.all_to_all(blocks, "elem", 0, 0, tiled=True)
+        return [got[t] for t in range(groups)]
+    got = [blocks[0]]
     for m in range(1, groups):
-        send = lax.dynamic_index_in_dim(blocks, me ^ m, 0, keepdims=False)
-        got.append(lax.ppermute(send, "elem", [(i, i ^ m) for i in range(groups)]))
-    return jnp.stack(got)
+        got.append(lax.ppermute(blocks[m], "elem", [(i, i ^ m) for i in range(groups)]))
+    return got
+
+
+def partners(groups):
+    if groups & (groups - 1):
+        return jnp.arange(groups, dtype=jnp.int32)
+    return lax.axis_index("elem") ^ jnp.arange(groups, dtype=jnp.int32)
 
 
 def on_device(params, profiles, weights, destinations, table):
@@ -171,7 +180,7 @@
     cap = samples // 2
     scale = 1.0 / (members * samples)
 
-    mine = destinations[:, None] == jnp.arange(groups, dtype=jnp.int32)[None, :]
+    mine = destinations[:, None] == partners(groups)[None, :]
     idx = jnp.arange(samples, dtype=jnp.int32)
     earlier = (idx[:, None] > idx[None, :]).astype(jnp.bfloat16)
     counts = jnp.dot(earlier, mine.astype(jnp.bfloat16), preferred_element_type=jnp.float32)
@@ -186,13 +195,11 @@
         [params, weights[None, :], jnp.zeros((rows - npar - 1, samples), params.dtype)], axis=0
     )
     meta_c = jnp.einsum("eis,js->eji", sel, meta, preferred_element_type=jnp.float32).astype(jnp.bfloat16)
-    meta_r = exchange(meta_c, groups)
+    meta_r = jnp.stack(exchange(meta_c, groups))
     prof_r = exchange(prof_c, groups)
 
-    q = profiles.shape[1]
     terms = table.shape[0]
     slots = groups * cap
-    prof_r = prof_r.reshape(slots, q)
     meta_r = jnp.transpose(meta_r, (1, 0, 2)).reshape(rows, slots)
 
     me = lax.axis_index("grp")

time: 118 us -> 112 us (0.949)
  Pallas kernels: 48.9 us -> 43.9 us
  other arithmetic: 4.48 us -> 2.93 us
    pallas_call x2, Pallas kernels: 44.3 us -> 38.8 us  [gram_rows(): pl.pallas_call(kernel, grid_spec=grid_spec, out_shape=out_shape, compiler...]
    dynamic_slice x2 -> x0, local copies, waits for them, and re-layouts: 1.99 us -> none  [exchange(): got = [lax.dynamic_index_in_dim(blocks, me, 0, keepdims=False)]]
    another operation x1 -> x0, other arithmetic: 1.62 us -> none  [exchange(): return jnp.stack(got)]
    squeeze x0 -> x1, local copies, waits for them, and re-layouts: none -> 1.35 us  [exchange(): blocks[m]]
  transfers between devices with their start and end apart: 11 -> 11, of which waited for: 6 -> 6; matrix products, arithmetic and copies ran while one was open for 4% -> 4% of each run, Pallas kernels for 38% -> 35%
where the time goes in v6:
time: 112 us; the launch traced here: 111 us
  Pallas kernels  43.9 us (39%)
  waiting for transfers between devices  25.2 us (22%)
  starting transfers between devices  15 us (13%)
  between operations  14.3 us (13%)
  local copies, waits for them, and re-layouts  5.11 us (5%)
  matrix products  4.91 us (4%)
  other arithmetic  2.93 us (3%)
    pallas_call x2, Pallas kernels, gram_rows(): pl.pallas_call(kernel, grid_spec=grid_spec, out_shape=out_shape, compiler...  38.8 us
    ppermute x6, waiting for transfers between devices, exchange(): lax.ppermute(blocks[m], 'elem', [(i, i ^ m) for i in range(groups)])  20 us
    ppermute x6, starting transfers between devices, exchange(): lax.ppermute(blocks[m], 'elem', [(i, i ^ m) for i in range(groups)])  9.3 us
    ppermute x3, starting transfers between devices, on_device(): lax.ppermute(meta_r, 'grp', [(i, (i + 2 * k) % members) for i in range(me...  5.56 us
    pallas_call x1, Pallas kernels, moment_sums(): pl.pallas_call(functools.partial(moment_kernel, scale=scale), grid=(terms...  5.16 us
    ppermute x3, waiting for transfers between devices, on_device(): lax.ppermute(meta_r, 'grp', [(i, (i + 2 * k) % members) for i in range(me...  3.32 us
    unnamed x22, local copies, waits for them, and re-layouts  2.35 us
    dot_general x1, matrix products, on_device(): jnp.einsum('eis,sq->eiq', sel, profiles, preferred_element_type=jnp.float32)  2.34 us
  transfers between devices with their start and end apart: 11, of which 6 were waited for; matrix products, arithmetic and copies ran while one was open for 4% of the time, Pallas kernels for 35%

profile of v6, /device:TPU:0, one launch (start us, length us, event | category | flops | bytes accessed | tf_op | source)
XLA Modules:
  0.0 111.4 jit_solution(21503990961338546)
XLA Ops:
  7.2 1.3 %fusion.19 = f32[1024]{0:T(1024)S(1)} fusion(s32[1024]{0:T(1024)} %param.9, s32[4]{0:T(128)S(1)} %iota_xor_fusion), kind=kOutput, calls=%fused_computation.15 | convolution fusion | flops 9452544 | bytes 8208 | tf_op jit(solution)/shard_map/dot_general | solution.py:186
  8.6 0.8 broadcast_compare_fusion
  9.7 2.3 %fusion.9 = bf16[4,512,512]{2,1,0:T(8,128)(2,1)S(1)} fusion(pred[512,1024]{1,0:T(8,128)(4,1)S(1)} %iota_compare_fusion.2, pred[4,1024]{1,0:T(4,128)(4,1)S(1)} %broadcast_compare_fusion, bf16[1024,512]{1,0:T(8,128)(2,1)S(1)} %copy-done), kind=kOutput, calls=%fused_computation.11 | convolution fusion | flops 2150629376 | bytes 3674112 | tf_op jit(solution)/shard_map/eis,sq->eiq/dot_general | solution.py:191
  12.0 1.4 %slice_bitcast_fusion = (bf16[512,512]{1,0:T(8,128)(2,1)}, bf16[512,512]{1,0:T(8,128)(2,1)}, bf16[512,512]{1,0:T(8,128)(2,1)}, bf16[512,512]{1,0:T(8,128)(2,1)}) fusion(bf16[4,512,512]{2,1,0:T(8,128)(2,1)S(1)} %fusion.9), kind=kLoop, calls=%fused_computation.17 | loop fusion | bytes 4194304 | tf_op jit(solution)/shard_map/squeeze | solution.py:166
  13.4 3.0 %collective-permute-start.7 = (bf16[512,512]{1,0:T(8,128)(2,1)}, bf16[512,512]{1,0:T(8,128)(2,1)}, u32[]{:S(2)}, u32[]{:S(2)}) collective-permute-start(bf16[512,512]{1,0:T(8,128)(2,1)} %get-tuple-element.8), channel_id=1, source_target_pairs={{0,8},{8,0},{16,24},{24,16},{1,9},{9,1},{17,25},{25,17},{2,10},{10... | collective-permute-start | bytes 1572872 | tf_op jit(solution)/shard_map/ppermute | solution.py:166
  16.4 1.5 %collective-permute-start.8 = (bf16[512,512]{1,0:T(8,128)(2,1)}, bf16[512,512]{1,0:T(8,128)(2,1)}, u32[]{:S(2)}, u32[]{:S(2)}) collective-permute-start(bf16[512,512]{1,0:T(8,128)(2,1)} %get-tuple-element.7), channel_id=1, source_target_pairs={{0,16},{8,24},{16,0},{24,8},{1,17},{9,25},{17,1},{25,9},{2,18},{10... | collective-permute-start | bytes 1572872 | tf_op jit(solution)/shard_map/ppermute | solution.py:166
  18.0 1.2 %fusion.15 = bf16[4,16,512]{2,1,0:T(8,128)(2,1)S(1)} fusion(pred[512,1024]{1,0:T(8,128)(4,1)S(1)} %iota_compare_fusion.2, pred[4,1024]{1,0:T(4,128)(4,1)S(1)} %broadcast_compare_fusion, bf16[1,1024]{1,0:T(2,128)(2,1)S(1)} %broadcast_in_dim.26, bf16[12,1024]{1,0:T(8,128)(2,1)S(1)} %copy-done.10, bf16[16]{0:T(256)(128)(2,1)S(1)} %pad.10.clone), kind=kOutput, calls=%fused_computation.13 | convolution fusion | flops 69337088 | bytes 620576 | tf_op jit(solution)/shard_map/eis,js->eji/dot_general | solution.py:197
  19.9 2.9 %collective-permute-start.2 = (bf16[16,512]{1,0:T(8,128)(2,1)S(1)}, bf16[16,512]{1,0:T(8,128)(2,1)S(1)}, u32[]{:S(2)}, u32[]{:S(2)}) collective-permute-start(bf16[16,512]{1,0:T(8,128)(2,1)S(1)} %get-tuple-element.15), channel_id=1, source_target_pairs={{0,24},{8,16},{16,8},{24,0},{1,25},{9,17},{17,9},{25,1},{2,26},{10... | collective-permute-start | bytes 49160 | tf_op jit(solution)/shard_map/ppermute | solution.py:166
  23.3 18.1 %collective-permute-done.2 = bf16[16,512]{1,0:T(8,128)(2,1)S(1)} collective-permute-done((bf16[16,512]{1,0:T(8,128)(2,1)S(1)}, bf16[16,512]{1,0:T(8,128)(2,1)S(1)}, u32[]{:S(2)}, u32[]{:S(2)}) %collective-permute-start.2) | collective-permute-done | bytes 16416 | tf_op jit(solution)/shard_map/ppermute | solution.py:166
  41.4 1.4 %collective-permute-start = (bf16[16,512]{1,0:T(8,128)(2,1)}, bf16[16,512]{1,0:T(8,128)(2,1)}, u32[]{:S(2)}, u32[]{:S(2)}) collective-permute-start(bf16[16,512]{1,0:T(8,128)(2,1)} %get-tuple-element.17), channel_id=1, source_target_pairs={{0,8},{8,0},{16,24},{24,16},{1,9},{9,1},{17,25},{25,17},{2,10},{10... | collective-permute-start | bytes 49160 | tf_op jit(solution)/shard_map/ppermute | solution.py:166
  43.5 2.0 %collective-permute-done = bf16[16,512]{1,0:T(8,128)(2,1)} collective-permute-done((bf16[16,512]{1,0:T(8,128)(2,1)}, bf16[16,512]{1,0:T(8,128)(2,1)}, u32[]{:S(2)}, u32[]{:S(2)}) %collective-permute-start) | collective-permute-done | bytes 16416 | tf_op jit(solution)/shard_map/ppermute | solution.py:166
  45.5 0.8 maximum_bitcast_fusion
  46.3 10.2 %shard_map.77 = (f32[256,1024]{1,0:T(8,128)S(1)}, bf16[1024,2048]{1,0:T(8,128)(2,1)}) custom-call(s32[1]{0:T(128)} %bitcast.row0_ref, bf16[16,2048]{1,0:T(8,128)(2,1)S(1)} %bitcast.43, bf16[3,256,192]{2,1,0:T(8,128)(2,1)S(1)} %copy-done.3, s32[4,1024,1]{2,1,0:T(8,128)S(1)} %copy.10.refs_2_.refs_4_), custom_call_target="tpu_custom_call" | custom-call | tf_op jit(solution)/shard_map/pallas_call | solution.py:124
  56.5 1.0 copy-done.4
  57.5 5.2 %shard_map.79 = f32[1024,512]{1,0:T(8,128)S(1)} custom-call(bf16[1024,2048]{1,0:T(8,128)(2,1)} %get-tuple-element.5.w_ref, bf16[512,512]{1,0:T(8,128)(2,1)S(1)} %copy-done.2, bf16[512,512]{1,0:T(8,128)(2,1)} %collective-permute-done.7.refs_1_, bf16[512,512]{1,0:T(8,128)(2,1)} %collective-permute-done.8.refs_2_, bf16[512,512]{1,0:T(8,128)(2,1)} %collective-permute-done.9.refs_3_), custom_call_target="tpu_custom_call" | custom-call | tf_op jit(solution)/shard_map/pallas_call | solution.py:147
  62.7 1.3 %copy-done.1 = f32[1024,512]{1,0:T(8,128)} copy-done((f32[1024,512]{1,0:T(8,128)}, f32[1024,512]{1,0:T(8,128)S(1)}, u32[]{:S(2)}) %copy-start.1) | copy-done | bytes 2097176
  64.0 1.6 %collective-permute-start.3 = (bf16[16,2048]{1,0:T(8,128)(2,1)}, bf16[16,2048]{1,0:T(8,128)(2,1)}, u32[]{:S(2)}, u32[]{:S(2)}) collective-permute-start(bf16[16,2048]{1,0:T(8,128)(2,1)} %bitcast.44), channel_id=1, source_target_pairs={{0,2},{1,3},{2,4},{3,5},{4,6},{5,7},{6,0},{7,1},{8,10},{9,11},{10,... | collective-permute-start | bytes 196616 | tf_op jit(solution)/shard_map/ppermute | solution.py:211
  65.7 2.6 %collective-permute-start.4 = (bf16[16,2048]{1,0:T(8,128)(2,1)}, bf16[16,2048]{1,0:T(8,128)(2,1)}, u32[]{:S(2)}, u32[]{:S(2)}) collective-permute-start(bf16[16,2048]{1,0:T(8,128)(2,1)} %bitcast.45), channel_id=1, source_target_pairs={{0,4},{1,5},{2,6},{3,7},{4,0},{5,1},{6,2},{7,3},{8,12},{9,13},{10,... | collective-permute-start | bytes 196616 | tf_op jit(solution)/shard_map/ppermute | solution.py:211
  68.3 1.3 %collective-permute-start.5 = (bf16[16,2048]{1,0:T(8,128)(2,1)}, bf16[16,2048]{1,0:T(8,128)(2,1)}, u32[]{:S(2)}, u32[]{:S(2)}) collective-permute-start(bf16[16,2048]{1,0:T(8,128)(2,1)} %bitcast.46), channel_id=1, source_target_pairs={{0,6},{1,7},{2,0},{3,1},{4,2},{5,3},{6,4},{7,5},{8,14},{9,15},{10,... | collective-permute-start | bytes 196616 | tf_op jit(solution)/shard_map/ppermute | solution.py:211
  69.6 0.9 collective-permute-done.3.refs_0_
  71.2 1.8 %collective-permute-done.5.refs_2_ = bf16[16,2048]{1,0:T(8,128)(2,1)} collective-permute-done((bf16[16,2048]{1,0:T(8,128)(2,1)}, bf16[16,2048]{1,0:T(8,128)(2,1)}, u32[]{:S(2)}, u32[]{:S(2)}) %collective-permute-start.5) | collective-permute-done | bytes 65568 | tf_op jit(solution)/shard_map/ppermute | solution.py:211
  72.9 28.5 %shard_map.78 = f32[256,1024]{1,0:T(8,128)S(1)} custom-call(s32[1]{0:T(128)} %bitcast.row0_ref, bf16[16,2048]{1,0:T(8,128)(2,1)} %collective-permute-done.3.refs_0_, bf16[16,2048]{1,0:T(8,128)(2,1)} %collective-permute-done.4.refs_1_, bf16[16,2048]{1,0:T(8,128)(2,1)} %collective-permute-done.5.refs_2_, bf16[3,256,192]{2,1,0:T(8,128)(2,1)S(1)} %copy-done.3, ...), custom_call_target="tpu_custom_call" | custom-call | tf_op jit(solution)/shard_map/pallas_call | solution.py:124
  101.8 1.9 %collective-permute-done.6 = f32[128,1024]{1,0:T(8,128)S(1)} collective-permute-done((f32[128,1024]{1,0:T(8,128)S(1)}, f32[128,1024]{1,0:T(8,128)S(1)}, u32[]{:S(2)}, u32[]{:S(2)}) %collective-permute-start.6) | collective-permute-done | bytes 524320 | tf_op jit(solution)/shard_map/ppermute | solution.py:223
  103.7 0.9 multiply_bitcast_fusion
  (44 shorter events, 3.3 us)
Async XLA Ops:
  7.2 2.5 %copy-start = (bf16[1024,512]{1,0:T(8,128)(2,1)S(1)}, bf16[1024,512]{1,0:T(8,128)(2,1)}, u32[]{:S(2)}) copy-start(bf16[1024,512]{1,0:T(8,128)(2,1)} %param.7) | copy-start | bytes 3145732
  7.2 97.3 %reduce-scatter.2.cloned.1.call-start = ((), (), s32[]{:S(2)}) async-start(), calls=%async_computation.1 | async-start | bytes 2359296 | tf_op jit(solution)/shard_map/reduce_scatter | solution.py:218
  12.0 5.9 %copy-start.9 = (bf16[1024]{0:T(1024)(128)(2,1)S(1)}, bf16[1024]{0:T(1024)(128)(2,1)}, u32[]{:S(2)}) copy-start(bf16[1024]{0:T(1024)(128)(2,1)} %param.8) | copy-start | bytes 6148
  12.0 6.0 %copy-start.10 = (bf16[12,1024]{1,0:T(8,128)(2,1)S(1)}, bf16[12,1024]{1,0:T(8,128)(2,1)}, u32[]{:S(2)}) copy-start(bf16[12,1024]{1,0:T(8,128)(2,1)} %param.6) | copy-start | bytes 73732
  13.4 9.9 %copy-start.7 = (s32[1024,12]{0,1:T(8,128)S(1)}, s32[1024,12]{0,1:T(8,128)}, u32[]{:S(2)}) copy-start(s32[1024,12]{0,1:T(8,128)} %param.10) | copy-start | bytes 147460
  13.4 44.1 %collective-permute-start.7 = (bf16[512,512]{1,0:T(8,128)(2,1)}, bf16[512,512]{1,0:T(8,128)(2,1)}, u32[]{:S(2)}, u32[]{:S(2)}) collective-permute-start(bf16[512,512]{1,0:T(8,128)(2,1)} %get-tuple-element.8), channel_id=1, source_target_pairs={{0,8},{8,0},{16,24},{24,16},{1,9},{9,1},{17,25},{25,17},{2,10},{10... | collective-permute-start | bytes 1572872 | tf_op jit(solution)/shard_map/ppermute | solution.py:166
  16.4 41.1 %collective-permute-start.8 = (bf16[512,512]{1,0:T(8,128)(2,1)}, bf16[512,512]{1,0:T(8,128)(2,1)}, u32[]{:S(2)}, u32[]{:S(2)}) collective-permute-start(bf16[512,512]{1,0:T(8,128)(2,1)} %get-tuple-element.7), channel_id=1, source_target_pairs={{0,16},{8,24},{16,0},{24,8},{1,17},{9,25},{17,1},{25,9},{2,18},{10... | collective-permute-start | bytes 1572872 | tf_op jit(solution)/shard_map/ppermute | solution.py:166
  17.9 39.6 %collective-permute-start.9 = (bf16[512,512]{1,0:T(8,128)(2,1)}, bf16[512,512]{1,0:T(8,128)(2,1)}, u32[]{:S(2)}, u32[]{:S(2)}) collective-permute-start(bf16[512,512]{1,0:T(8,128)(2,1)} %get-tuple-element.6), channel_id=1, source_target_pairs={{0,24},{8,16},{16,8},{24,0},{1,25},{9,17},{17,9},{25,1},{2,26},{10... | collective-permute-start | bytes 1572872 | tf_op jit(solution)/shard_map/ppermute | solution.py:166
  19.2 27.0 %copy-start.3 = (bf16[3,256,192]{2,1,0:T(8,128)(2,1)S(1)}, bf16[3,256,192]{2,1,0:T(8,128)(2,1)}, u32[]{:S(2)}) copy-start(bf16[3,256,192]{2,1,0:T(8,128)(2,1)} %constant.49.clone.refs_1_.refs_3_) | copy-start | bytes 884740
  19.9 21.5 %collective-permute-start.2 = (bf16[16,512]{1,0:T(8,128)(2,1)S(1)}, bf16[16,512]{1,0:T(8,128)(2,1)S(1)}, u32[]{:S(2)}, u32[]{:S(2)}) collective-permute-start(bf16[16,512]{1,0:T(8,128)(2,1)S(1)} %get-tuple-element.15), channel_id=1, source_target_pairs={{0,24},{8,16},{16,8},{24,0},{1,25},{9,17},{17,9},{25,1},{2,26},{10... | collective-permute-start | bytes 49160 | tf_op jit(solution)/shard_map/ppermute | solution.py:166
  22.8 20.7 %collective-permute-start.1 = (bf16[16,512]{1,0:T(8,128)(2,1)}, bf16[16,512]{1,0:T(8,128)(2,1)}, u32[]{:S(2)}, u32[]{:S(2)}) collective-permute-start(bf16[16,512]{1,0:T(8,128)(2,1)} %get-tuple-element.16), channel_id=1, source_target_pairs={{0,16},{8,24},{16,0},{24,8},{1,17},{9,25},{17,1},{25,9},{2,18},{10... | collective-permute-start | bytes 49160 | tf_op jit(solution)/shard_map/ppermute | solution.py:166
  41.4 1.4 %copy-start.8 = (bf16[16,512]{1,0:T(8,128)(2,1)}, bf16[16,512]{1,0:T(8,128)(2,1)S(1)}, u32[]{:S(2)}) copy-start(bf16[16,512]{1,0:T(8,128)(2,1)S(1)} %collective-permute-done.2) | copy-start | bytes 49156
  41.4 4.1 %collective-permute-start = (bf16[16,512]{1,0:T(8,128)(2,1)}, bf16[16,512]{1,0:T(8,128)(2,1)}, u32[]{:S(2)}, u32[]{:S(2)}) collective-permute-start(bf16[16,512]{1,0:T(8,128)(2,1)} %get-tuple-element.17), channel_id=1, source_target_pairs={{0,8},{8,0},{16,24},{24,16},{1,9},{9,1},{17,25},{25,17},{2,10},{10... | collective-permute-start | bytes 49160 | tf_op jit(solution)/shard_map/ppermute | solution.py:166
  43.5 14.0 %copy-start.2 = (bf16[512,512]{1,0:T(8,128)(2,1)S(1)}, bf16[512,512]{1,0:T(8,128)(2,1)}, u32[]{:S(2)}) copy-start(bf16[512,512]{1,0:T(8,128)(2,1)} %get-tuple-element.9.refs_0_) | copy-start | bytes 1572868
  46.2 11.3 %copy-start.6 = (bf16[4,2,8,512]{3,2,0,1:T(8,128)(2,1)}, bf16[4,2,8,512]{3,2,0,1:T(8,128)(2,1)S(1)}, u32[]{:S(2)}) copy-start(bf16[4,2,8,512]{3,2,0,1:T(8,128)(2,1)S(1)} %copy.12) | copy-start | bytes 196612
  56.5 1.0 copy-start.4
  62.7 1.3 %copy-start.1 = (f32[1024,512]{1,0:T(8,128)}, f32[1024,512]{1,0:T(8,128)S(1)}, u32[]{:S(2)}) copy-start(f32[1024,512]{1,0:T(8,128)S(1)} %shard_map.79) | copy-start | bytes 6291460
  64.0 6.4 %collective-permute-start.3 = (bf16[16,2048]{1,0:T(8,128)(2,1)}, bf16[16,2048]{1,0:T(8,128)(2,1)}, u32[]{:S(2)}, u32[]{:S(2)}) collective-permute-start(bf16[16,2048]{1,0:T(8,128)(2,1)} %bitcast.44), channel_id=1, source_target_pairs={{0,2},{1,3},{2,4},{3,5},{4,6},{5,7},{6,0},{7,1},{8,10},{9,11},{10,... | collective-permute-start | bytes 196616 | tf_op jit(solution)/shard_map/ppermute | solution.py:211
  65.7 5.5 %collective-permute-start.4 = (bf16[16,2048]{1,0:T(8,128)(2,1)}, bf16[16,2048]{1,0:T(8,128)(2,1)}, u32[]{:S(2)}, u32[]{:S(2)}) collective-permute-start(bf16[16,2048]{1,0:T(8,128)(2,1)} %bitcast.45), channel_id=1, source_target_pairs={{0,4},{1,5},{2,6},{3,7},{4,0},{5,1},{6,2},{7,3},{8,12},{9,13},{10,... | collective-permute-start | bytes 196616 | tf_op jit(solution)/shard_map/ppermute | solution.py:211
  68.3 4.7 %collective-permute-start.5 = (bf16[16,2048]{1,0:T(8,128)(2,1)}, bf16[16,2048]{1,0:T(8,128)(2,1)}, u32[]{:S(2)}, u32[]{:S(2)}) collective-permute-start(bf16[16,2048]{1,0:T(8,128)(2,1)} %bitcast.46), channel_id=1, source_target_pairs={{0,6},{1,7},{2,0},{3,1},{4,2},{5,3},{6,4},{7,5},{8,14},{9,15},{10,... | collective-permute-start | bytes 196616 | tf_op jit(solution)/shard_map/ppermute | solution.py:211
  69.6 31.9 %copy-start.5 = (f32[256,1024]{1,0:T(8,128)S(1)}, f32[256,1024]{1,0:T(8,128)}, u32[]{:S(2)}) copy-start(f32[256,1024]{1,0:T(8,128)} %copy-done.4) | copy-start | bytes 3145732
  101.7 2.0 %collective-permute-start.6 = (f32[128,1024]{1,0:T(8,128)S(1)}, f32[128,1024]{1,0:T(8,128)S(1)}, u32[]{:S(2)}, u32[]{:S(2)}) collective-permute-start(f32[128,1024]{1,0:T(8,128)S(1)} %constant_dynamic-slice_fusion), channel_id=1, source_target_pairs={{0,1},{1,0},{2,3},{3,2},{4,5},{5,4},{6,7},{7,6},{8,9},{9,8},{10,11... | collective-permute-start | bytes 1572872 | tf_op jit(solution)/shard_map/ppermute | solution.py:223
Sparse Core Ops, SparseCore 0:
  64.2 36.2 reduce-scatter.1

commit v7 on v6

--- a/solution.py
+++ b/solution.py
@@ -93,7 +93,7 @@
         wt_refs[0][...] = (w * basis).astype(jnp.bfloat16)
 
 
-def gram_rows(metas, pick, codes, row0, picked, npar, with_weighted, block=512):
+def gram_rows(metas, pick, codes, row0, picked, npar, with_weighted, block=1024):
     rows, samples = metas[0].shape
     per = samples // block
     n_meta = len(metas)
@@ -198,6 +198,7 @@
     meta_r = jnp.stack(exchange(meta_c, groups))
     prof_r = exchange(prof_c, groups)
 
+    q = profiles.shape[1]
     terms = table.shape[0]
     slots = groups * cap
     meta_r = jnp.transpose(meta_r, (1, 0, 2)).reshape(rows, slots)
@@ -215,8 +216,24 @@
     row0 = (chip * 2 * own_rows).astype(jnp.int32).reshape(1)
     gram_own, weighted_t = gram_rows([meta_r], pick, codes, row0, 2 * own_rows, npar, True)
     moment_part = moment_sums(weighted_t, prof_r, scale)
-    moment_rows = lax.psum_scatter(moment_part, "grp", scatter_dimension=0, tiled=True)
-    (gram_oth,) = gram_rows(others, pick, codes, row0, 2 * own_rows, npar, False)
+    blocks = moment_part.reshape(pairs, 2, own_rows, q)
+    mine = lax.dynamic_index_in_dim(blocks, core, axis=1, keepdims=False)
+    theirs = lax.dynamic_index_in_dim(blocks, 1 - core, axis=1, keepdims=False)
+    swapped = lax.ppermute(theirs, "grp", [(i, i ^ 1) for i in range(members)])
+    (gram_oth,) = gram_rows(others[:1], pick, codes, row0, 2 * own_rows, npar, False)
+    chip_sum = mine + swapped
+    moment_rows = lax.dynamic_index_in_dim(chip_sum, chip, axis=0, keepdims=False)
+    arrived = [
+        lax.ppermute(
+            lax.dynamic_index_in_dim(chip_sum, (chip + k) % pairs, axis=0, keepdims=False),
+            "grp", [(i, (i + 2 * k) % members) for i in range(members)])
+        for k in range(1, pairs)
+    ]
+    if len(others) > 1:
+        (gram_b,) = gram_rows(others[1:], pick, codes, row0, 2 * own_rows, npar, False)
+        gram_oth = gram_oth + gram_b
+    for block in arrived:
+        moment_rows = moment_rows + block
     gram_chip = gram_own + gram_oth
     keep = lax.dynamic_slice_in_dim(gram_chip, core * own_rows, own_rows, axis=0)
     send = lax.dynamic_slice_in_dim(gram_chip, (1 - core) * own_rows, own_rows, axis=0)

time: 112 us -> 125 us (1.12)
  waiting for transfers between devices: 25.2 us -> 41 us
  between operations: 14.3 us -> 0.92 us
  other arithmetic: 2.93 us -> 7.49 us
  local copies, waits for them, and re-layouts: 5.11 us -> 9.64 us
  starting transfers between devices: 15 us -> 18 us
  Pallas kernels: 43.9 us -> 42.4 us
    ppermute x0 -> x4, waiting for transfers between devices: none -> 19.6 us  [the longest x3 19.6 us: on_device(): lax.ppermute(lax.dynamic_index_in_dim(chip_sum, (chip + k) % pairs, axis=...]
    ppermute x0 -> x4, starting transfers between devices: none -> 3.17 us  [the longest x3 3.16 us: on_device(): lax.ppermute(lax.dynamic_index_in_dim(chip_sum, (chip + k) % pairs, axis=...]
    broadcast_in_dim x1 -> x2, other arithmetic: 0.86 us -> 3.8 us  [on_device(): return (gram_out[None], moment_rows[None])]
    unnamed x22 -> x26, local copies, waits for them, and re-layouts: 2.35 us -> 4.37 us
    ppermute x3, waiting for transfers between devices: 3.32 us -> 1.32 us  [on_device(): lax.ppermute(meta_r, 'grp', [(i, (i + 2 * k) % members) for i in range(me...]
    ppermute x1, waiting for transfers between devices: 1.89 us -> 0.01 us  [on_device(): recv = lax.ppermute(send, 'grp', [(i, i ^ 1) for i in range(members)])]
    pallas_call x2 -> x3, Pallas kernels: 38.8 us -> 37.2 us  [gram_rows(): pl.pallas_call(kernel, grid_spec=grid_spec, out_shape=out_shape, compiler...]
    add x0 -> x1, other arithmetic: none -> 1.44 us  [on_device(): chip_sum = mine + swapped]
  transfers between devices with their start and end apart: 11 -> 14, of which waited for: 6 -> 5; matrix products, arithmetic and copies ran while one was open for 4% -> 7% of each run, Pallas kernels for 35% -> 30%
where the time goes in v7:
time: 125 us; the launch traced here: 124 us
  Pallas kernels  42.4 us (34%)
  waiting for transfers between devices  41 us (33%)
  starting transfers between devices  18 us (14%)
  local copies, waits for them, and re-layouts  9.64 us (8%)
  other arithmetic  7.49 us (6%)
  matrix products  4.92 us (4%)
    pallas_call x3, Pallas kernels, gram_rows(): pl.pallas_call(kernel, grid_spec=grid_spec, out_shape=out_shape, compiler...  37.2 us
    ppermute x6, waiting for transfers between devices, exchange(): lax.ppermute(blocks[m], 'elem', [(i, i ^ m) for i in range(groups)])  20 us
    ppermute x3, waiting for transfers between devices, on_device(): lax.ppermute(lax.dynamic_index_in_dim(chip_sum, (chip + k) % pairs, axis=...  19.6 us
    ppermute x6, starting transfers between devices, exchange(): lax.ppermute(blocks[m], 'elem', [(i, i ^ m) for i in range(groups)])  9.3 us
    ppermute x3, starting transfers between devices, on_device(): lax.ppermute(meta_r, 'grp', [(i, (i + 2 * k) % members) for i in range(me...  5.53 us
    pallas_call x1, Pallas kernels, moment_sums(): pl.pallas_call(functools.partial(moment_kernel, scale=scale), grid=(terms...  5.16 us
    unnamed x26, local copies, waits for them, and re-layouts  4.37 us
    broadcast_in_dim x2, other arithmetic, on_device(): return (gram_out[None], moment_rows[None])  3.8 us
  transfers between devices with their start and end apart: 14, of which 5 were waited for; matrix products, arithmetic and copies ran while one was open for 7% of the time, Pallas kernels for 30%

profile of v7, /device:TPU:0, one launch (start us, length us, event | category | flops | bytes accessed | tf_op | source)
XLA Modules:
  0.0 124.3 jit_solution(13089269727201598809)
XLA Ops:
  0.7 1.3 %fusion.19 = f32[1024]{0:T(1024)S(1)} fusion(s32[1024]{0:T(1024)} %param.9, s32[4]{0:T(128)S(1)} %iota_xor_fusion), kind=kOutput, calls=%fused_computation.15 | convolution fusion | flops 9452544 | bytes 8208 | tf_op jit(solution)/shard_map/dot_general | solution.py:186
  3.1 2.3 %fusion.9 = bf16[4,512,512]{2,1,0:T(8,128)(2,1)S(1)} fusion(pred[512,1024]{1,0:T(8,128)(4,1)S(1)} %iota_compare_fusion.2, pred[4,1024]{1,0:T(4,128)(4,1)S(1)} %broadcast_compare_fusion, bf16[1024,512]{1,0:T(8,128)(2,1)S(1)} %copy-done), kind=kOutput, calls=%fused_computation.11 | convolution fusion | flops 2150629376 | bytes 3674112 | tf_op jit(solution)/shard_map/eis,sq->eiq/dot_general | solution.py:191
  5.5 1.4 %slice_bitcast_fusion = (bf16[512,512]{1,0:T(8,128)(2,1)}, bf16[512,512]{1,0:T(8,128)(2,1)}, bf16[512,512]{1,0:T(8,128)(2,1)}, bf16[512,512]{1,0:T(8,128)(2,1)}) fusion(bf16[4,512,512]{2,1,0:T(8,128)(2,1)S(1)} %fusion.9), kind=kLoop, calls=%fused_computation.20 | loop fusion | bytes 4194304 | tf_op jit(solution)/shard_map/squeeze | solution.py:166
  6.8 3.0 %collective-permute-start.7 = (bf16[512,512]{1,0:T(8,128)(2,1)}, bf16[512,512]{1,0:T(8,128)(2,1)}, u32[]{:S(2)}, u32[]{:S(2)}) collective-permute-start(bf16[512,512]{1,0:T(8,128)(2,1)} %get-tuple-element.8), channel_id=1, source_target_pairs={{0,8},{8,0},{16,24},{24,16},{1,9},{9,1},{17,25},{25,17},{2,10},{10... | collective-permute-start | bytes 1572872 | tf_op jit(solution)/shard_map/ppermute | solution.py:166
  9.8 1.5 %collective-permute-start.8 = (bf16[512,512]{1,0:T(8,128)(2,1)}, bf16[512,512]{1,0:T(8,128)(2,1)}, u32[]{:S(2)}, u32[]{:S(2)}) collective-permute-start(bf16[512,512]{1,0:T(8,128)(2,1)} %get-tuple-element.7), channel_id=1, source_target_pairs={{0,16},{8,24},{16,0},{24,8},{1,17},{9,25},{17,1},{25,9},{2,18},{10... | collective-permute-start | bytes 1572872 | tf_op jit(solution)/shard_map/ppermute | solution.py:166
  13.3 2.9 %collective-permute-start.2 = (bf16[16,512]{1,0:T(8,128)(2,1)S(1)}, bf16[16,512]{1,0:T(8,128)(2,1)S(1)}, u32[]{:S(2)}, u32[]{:S(2)}) collective-permute-start(bf16[16,512]{1,0:T(8,128)(2,1)S(1)} %get-tuple-element.18), channel_id=1, source_target_pairs={{0,24},{8,16},{16,8},{24,0},{1,25},{9,17},{17,9},{25,1},{2,26},{10... | collective-permute-start | bytes 49160 | tf_op jit(solution)/shard_map/ppermute | solution.py:166
  16.8 18.1 %collective-permute-done.2 = bf16[16,512]{1,0:T(8,128)(2,1)S(1)} collective-permute-done((bf16[16,512]{1,0:T(8,128)(2,1)S(1)}, bf16[16,512]{1,0:T(8,128)(2,1)S(1)}, u32[]{:S(2)}, u32[]{:S(2)}) %collective-permute-start.2) | collective-permute-done | bytes 16416 | tf_op jit(solution)/shard_map/ppermute | solution.py:166
  34.8 1.4 %collective-permute-start = (bf16[16,512]{1,0:T(8,128)(2,1)}, bf16[16,512]{1,0:T(8,128)(2,1)}, u32[]{:S(2)}, u32[]{:S(2)}) collective-permute-start(bf16[16,512]{1,0:T(8,128)(2,1)} %get-tuple-element.20), channel_id=1, source_target_pairs={{0,8},{8,0},{16,24},{24,16},{1,9},{9,1},{17,25},{25,17},{2,10},{10... | collective-permute-start | bytes 49160 | tf_op jit(solution)/shard_map/ppermute | solution.py:166
  37.0 1.9 %collective-permute-done = bf16[16,512]{1,0:T(8,128)(2,1)} collective-permute-done((bf16[16,512]{1,0:T(8,128)(2,1)}, bf16[16,512]{1,0:T(8,128)(2,1)}, u32[]{:S(2)}, u32[]{:S(2)}) %collective-permute-start) | collective-permute-done | bytes 16416 | tf_op jit(solution)/shard_map/ppermute | solution.py:166
  40.3 10.3 %shard_map.77 = (f32[256,1024]{1,0:T(8,128)S(1)}, bf16[1024,2048]{1,0:T(8,128)(2,1)}) custom-call(s32[1]{0:T(128)} %bitcast.row0_ref, bf16[16,2048]{1,0:T(8,128)(2,1)} %bitcast.30.refs_0_, bf16[3,256,192]{2,1,0:T(8,128)(2,1)S(1)} %copy-done.3, s32[4,1024,1]{2,1,0:T(8,128)S(1)} %copy.10.refs_2_.refs_3_), custom_call_target="tpu_custom_call" | custom-call | tf_op jit(solution)/shard_map/pallas_call | solution.py:124
  51.6 5.2 %shard_map.80 = f32[1024,512]{1,0:T(8,128)S(1)} custom-call(bf16[1024,2048]{1,0:T(8,128)(2,1)} %get-tuple-element.5.w_ref, bf16[512,512]{1,0:T(8,128)(2,1)S(1)} %copy-done.4, bf16[512,512]{1,0:T(8,128)(2,1)} %collective-permute-done.7.refs_1_, bf16[512,512]{1,0:T(8,128)(2,1)} %collective-permute-done.8.refs_2_, bf16[512,512]{1,0:T(8,128)(2,1)} %collective-permute-done.9.refs_3_), custom_call_target="tpu_custom_call" | custom-call | tf_op jit(solution)/shard_map/pallas_call | solution.py:147
  56.8 1.3 %copy-done.1 = f32[1024,512]{1,0:T(8,128)} copy-done((f32[1024,512]{1,0:T(8,128)}, f32[1024,512]{1,0:T(8,128)S(1)}, u32[]{:S(2)}) %copy-start.1) | copy-done | bytes 2097176
  59.1 1.6 %collective-permute-start.3 = (bf16[16,2048]{1,0:T(8,128)(2,1)}, bf16[16,2048]{1,0:T(8,128)(2,1)}, u32[]{:S(2)}, u32[]{:S(2)}) collective-permute-start(bf16[16,2048]{1,0:T(8,128)(2,1)} %bitcast.30.refs_0_), channel_id=1, source_target_pairs={{0,2},{1,3},{2,4},{3,5},{4,6},{5,7},{6,0},{7,1},{8,10},{9,11},{10,... | collective-permute-start | bytes 196616 | tf_op jit(solution)/shard_map/ppermute | solution.py:212
  60.7 2.6 %collective-permute-start.4 = (bf16[16,2048]{1,0:T(8,128)(2,1)}, bf16[16,2048]{1,0:T(8,128)(2,1)}, u32[]{:S(2)}, u32[]{:S(2)}) collective-permute-start(bf16[16,2048]{1,0:T(8,128)(2,1)} %bitcast.30.refs_0_), channel_id=1, source_target_pairs={{0,4},{1,5},{2,6},{3,7},{4,0},{5,1},{6,2},{7,3},{8,12},{9,13},{10,... | collective-permute-start | bytes 196616 | tf_op jit(solution)/shard_map/ppermute | solution.py:212
  63.3 1.3 %collective-permute-start.5 = (bf16[16,2048]{1,0:T(8,128)(2,1)}, bf16[16,2048]{1,0:T(8,128)(2,1)}, u32[]{:S(2)}, u32[]{:S(2)}) collective-permute-start(bf16[16,2048]{1,0:T(8,128)(2,1)} %bitcast.30.refs_0_), channel_id=1, source_target_pairs={{0,6},{1,7},{2,0},{3,1},{4,2},{5,3},{6,4},{7,5},{8,14},{9,15},{10,... | collective-permute-start | bytes 196616 | tf_op jit(solution)/shard_map/ppermute | solution.py:212
  64.7 1.3 %collective-permute-done.3.refs_0_ = bf16[16,2048]{1,0:T(8,128)(2,1)} collective-permute-done((bf16[16,2048]{1,0:T(8,128)(2,1)}, bf16[16,2048]{1,0:T(8,128)(2,1)}, u32[]{:S(2)}, u32[]{:S(2)}) %collective-permute-start.3) | collective-permute-done | bytes 65568 | tf_op jit(solution)/shard_map/ppermute | solution.py:212
  66.0 9.4 %shard_map.78 = f32[256,1024]{1,0:T(8,128)S(1)} custom-call(s32[1]{0:T(128)} %bitcast.row0_ref, bf16[16,2048]{1,0:T(8,128)(2,1)} %collective-permute-done.3.refs_0_, bf16[3,256,192]{2,1,0:T(8,128)(2,1)S(1)} %copy-done.3, s32[4,1024,1]{2,1,0:T(8,128)S(1)} %copy.10.refs_2_.refs_3_), custom_call_target="tpu_custom_call" | custom-call | tf_op jit(solution)/shard_map/pallas_call | solution.py:124
  75.4 17.6 %shard_map.79 = f32[256,1024]{1,0:T(8,128)S(1)} custom-call(s32[1]{0:T(128)} %bitcast.row0_ref, bf16[16,2048]{1,0:T(8,128)(2,1)} %collective-permute-done.4.refs_0_, bf16[16,2048]{1,0:T(8,128)(2,1)} %collective-permute-done.5.refs_1_, bf16[3,256,192]{2,1,0:T(8,128)(2,1)S(1)} %copy-done.3, s32[4,1024,1]{2,1,0:T(8,128)S(1)} %copy.10.refs_2_.refs_3_), custom_call_target="tpu_custom_call" | custom-call | tf_op jit(solution)/shard_map/pallas_call | solution.py:124
  95.2 1.4 %bitcast_add_fusion = f32[4,128,512]{2,1,0:T(8,128)S(1)} fusion(f32[4,128,512]{2,1,0:T(8,128)} %collective-permute-done.10, f32[4,2,128,512]{3,2,1,0:T(8,128)S(1)} %bitcast.64, s32[]{:T(128)S(6)} %select_n.58), kind=kLoop, calls=%fused_computation.16 | loop fusion | flops 262144 | bytes 3145732 | tf_op jit(solution)/shard_map/add | solution.py:224
  97.7 2.5 %collective-permute-start.13 = (f32[128,512]{1,0:T(8,128)S(1)}, f32[128,512]{1,0:T(8,128)S(1)}, u32[]{:S(2)}, u32[]{:S(2)}) collective-permute-start(f32[128,512]{1,0:T(8,128)S(1)} %get-tuple-element.11), channel_id=1, source_target_pairs={{0,6},{1,7},{2,0},{3,1},{4,2},{5,3},{6,4},{7,5},{8,14},{9,15},{10,... | collective-permute-start | bytes 786440 | tf_op jit(solution)/shard_map/ppermute | solution.py:227
  100.9 2.1 %multiply_bitcast_fusion = f32[1,128,1024]{2,1,0:T(8,128)} fusion(f32[128,1024]{1,0:T(8,128)} %collective-permute-done.6, f32[256,1024]{1,0:T(8,128)} %copy-done.8, s32[]{:T(128)S(6)} %select_n.56), kind=kLoop, calls=%fused_computation.24 | loop fusion | flops 262144 | bytes 1572868 | tf_op jit(solution)/shard_map/broadcast_in_dim | solution.py:242
  102.9 5.1 %collective-permute-done.13 = f32[128,512]{1,0:T(8,128)S(1)} collective-permute-done((f32[128,512]{1,0:T(8,128)S(1)}, f32[128,512]{1,0:T(8,128)S(1)}, u32[]{:S(2)}, u32[]{:S(2)}) %collective-permute-start.13) | collective-permute-done | bytes 262176 | tf_op jit(solution)/shard_map/ppermute | solution.py:227
  108.1 14.5 %collective-permute-done.12 = f32[128,512]{1,0:T(8,128)S(1)} collective-permute-done((f32[128,512]{1,0:T(8,128)S(1)}, f32[128,512]{1,0:T(8,128)S(1)}, u32[]{:S(2)}, u32[]{:S(2)}) %collective-permute-start.12) | collective-permute-done | bytes 262176 | tf_op jit(solution)/shard_map/ppermute | solution.py:227
  122.6 1.7 %fusion.23 = f32[1,128,512]{2,1,0:T(8,128)} fusion(f32[128,512]{1,0:T(8,128)S(1)} %collective-permute-done.13, f32[128,512]{1,0:T(8,128)S(1)} %collective-permute-done.12, f32[128,512]{1,0:T(8,128)S(1)} %collective-permute-done.11, f32[4,128,512]{2,1,0:T(8,128)} %copy-done.7, s32[]{:T(128)S(6)} %select_n.60), kind=kLoop, calls=%fused_computation.28 | loop fusion | flops 196608 | bytes 1310724 | tf_op jit(solution)/shard_map/broadcast_in_dim | solution.py:242
  (58 shorter events, 11.6 us)
Async XLA Ops:
  0.6 2.5 %copy-start = (bf16[1024,512]{1,0:T(8,128)(2,1)S(1)}, bf16[1024,512]{1,0:T(8,128)(2,1)}, u32[]{:S(2)}) copy-start(bf16[1024,512]{1,0:T(8,128)(2,1)} %param.7) | copy-start | bytes 3145732
  5.4 5.9 %copy-start.11 = (bf16[1024]{0:T(1024)(128)(2,1)S(1)}, bf16[1024]{0:T(1024)(128)(2,1)}, u32[]{:S(2)}) copy-start(bf16[1024]{0:T(1024)(128)(2,1)} %param.8) | copy-start | bytes 6148
  5.5 6.0 %copy-start.12 = (bf16[12,1024]{1,0:T(8,128)(2,1)S(1)}, bf16[12,1024]{1,0:T(8,128)(2,1)}, u32[]{:S(2)}) copy-start(bf16[12,1024]{1,0:T(8,128)(2,1)} %param.6) | copy-start | bytes 73732
  6.8 9.9 %copy-start.9 = (s32[1024,12]{0,1:T(8,128)S(1)}, s32[1024,12]{0,1:T(8,128)}, u32[]{:S(2)}) copy-start(s32[1024,12]{0,1:T(8,128)} %param.10) | copy-start | bytes 147460
  6.8 44.7 %collective-permute-start.7 = (bf16[512,512]{1,0:T(8,128)(2,1)}, bf16[512,512]{1,0:T(8,128)(2,1)}, u32[]{:S(2)}, u32[]{:S(2)}) collective-permute-start(bf16[512,512]{1,0:T(8,128)(2,1)} %get-tuple-element.8), channel_id=1, source_target_pairs={{0,8},{8,0},{16,24},{24,16},{1,9},{9,1},{17,25},{25,17},{2,10},{10... | collective-permute-start | bytes 1572872 | tf_op jit(solution)/shard_map/ppermute | solution.py:166
  9.8 41.8 %collective-permute-start.8 = (bf16[512,512]{1,0:T(8,128)(2,1)}, bf16[512,512]{1,0:T(8,128)(2,1)}, u32[]{:S(2)}, u32[]{:S(2)}) collective-permute-start(bf16[512,512]{1,0:T(8,128)(2,1)} %get-tuple-element.7), channel_id=1, source_target_pairs={{0,16},{8,24},{16,0},{24,8},{1,17},{9,25},{17,1},{25,9},{2,18},{10... | collective-permute-start | bytes 1572872 | tf_op jit(solution)/shard_map/ppermute | solution.py:166
  11.3 40.3 %collective-permute-start.9 = (bf16[512,512]{1,0:T(8,128)(2,1)}, bf16[512,512]{1,0:T(8,128)(2,1)}, u32[]{:S(2)}, u32[]{:S(2)}) collective-permute-start(bf16[512,512]{1,0:T(8,128)(2,1)} %get-tuple-element.6), channel_id=1, source_target_pairs={{0,24},{8,16},{16,8},{24,0},{1,25},{9,17},{17,9},{25,1},{2,26},{10... | collective-permute-start | bytes 1572872 | tf_op jit(solution)/shard_map/ppermute | solution.py:166
  12.7 27.6 %copy-start.3 = (bf16[3,256,192]{2,1,0:T(8,128)(2,1)S(1)}, bf16[3,256,192]{2,1,0:T(8,128)(2,1)}, u32[]{:S(2)}) copy-start(bf16[3,256,192]{2,1,0:T(8,128)(2,1)} %constant.84.clone.refs_1_.refs_2_) | copy-start | bytes 884740
  13.3 21.5 %collective-permute-start.2 = (bf16[16,512]{1,0:T(8,128)(2,1)S(1)}, bf16[16,512]{1,0:T(8,128)(2,1)S(1)}, u32[]{:S(2)}, u32[]{:S(2)}) collective-permute-start(bf16[16,512]{1,0:T(8,128)(2,1)S(1)} %get-tuple-element.18), channel_id=1, source_target_pairs={{0,24},{8,16},{16,8},{24,0},{1,25},{9,17},{17,9},{25,1},{2,26},{10... | collective-permute-start | bytes 49160 | tf_op jit(solution)/shard_map/ppermute | solution.py:166
  16.2 20.7 %collective-permute-start.1 = (bf16[16,512]{1,0:T(8,128)(2,1)}, bf16[16,512]{1,0:T(8,128)(2,1)}, u32[]{:S(2)}, u32[]{:S(2)}) collective-permute-start(bf16[16,512]{1,0:T(8,128)(2,1)} %get-tuple-element.19), channel_id=1, source_target_pairs={{0,16},{8,24},{16,0},{24,8},{1,17},{9,25},{17,1},{25,9},{2,18},{10... | collective-permute-start | bytes 49160 | tf_op jit(solution)/shard_map/ppermute | solution.py:166
  34.8 1.4 %copy-start.10 = (bf16[16,512]{1,0:T(8,128)(2,1)}, bf16[16,512]{1,0:T(8,128)(2,1)S(1)}, u32[]{:S(2)}) copy-start(bf16[16,512]{1,0:T(8,128)(2,1)S(1)} %collective-permute-done.2) | copy-start | bytes 49156
  34.8 4.1 %collective-permute-start = (bf16[16,512]{1,0:T(8,128)(2,1)}, bf16[16,512]{1,0:T(8,128)(2,1)}, u32[]{:S(2)}, u32[]{:S(2)}) collective-permute-start(bf16[16,512]{1,0:T(8,128)(2,1)} %get-tuple-element.20), channel_id=1, source_target_pairs={{0,8},{8,0},{16,24},{24,16},{1,9},{9,1},{17,25},{25,17},{2,10},{10... | collective-permute-start | bytes 49160 | tf_op jit(solution)/shard_map/ppermute | solution.py:166
  36.9 14.7 %copy-start.4 = (bf16[512,512]{1,0:T(8,128)(2,1)S(1)}, bf16[512,512]{1,0:T(8,128)(2,1)}, u32[]{:S(2)}) copy-start(bf16[512,512]{1,0:T(8,128)(2,1)} %get-tuple-element.9.refs_0_) | copy-start | bytes 1572868
  56.8 1.3 %copy-start.1 = (f32[1024,512]{1,0:T(8,128)}, f32[1024,512]{1,0:T(8,128)S(1)}, u32[]{:S(2)}) copy-start(f32[1024,512]{1,0:T(8,128)S(1)} %shard_map.80) | copy-start | bytes 6291460
  59.1 36.1 %collective-permute-start.10 = (f32[4,128,512]{2,1,0:T(8,128)}, f32[4,128,512]{2,1,0:T(8,128)}, u32[]{:S(2)}, u32[]{:S(2)}) collective-permute-start(f32[4,128,512]{2,1,0:T(8,128)} %dynamic-slice_bitcast_fusion), channel_id=1, source_target_pairs={{0,1},{1,0},{2,3},{3,2},{4,5},{5,4},{6,7},{7,6},{8,9},{9,8},{10,11... | collective-permute-start | bytes 3145736 | tf_op jit(solution)/shard_map/ppermute | solution.py:222
  59.1 6.8 %collective-permute-start.3 = (bf16[16,2048]{1,0:T(8,128)(2,1)}, bf16[16,2048]{1,0:T(8,128)(2,1)}, u32[]{:S(2)}, u32[]{:S(2)}) collective-permute-start(bf16[16,2048]{1,0:T(8,128)(2,1)} %bitcast.30.refs_0_), channel_id=1, source_target_pairs={{0,2},{1,3},{2,4},{3,5},{4,6},{5,7},{6,0},{7,1},{8,10},{9,11},{10,... | collective-permute-start | bytes 196616 | tf_op jit(solution)/shard_map/ppermute | solution.py:212
  60.7 14.7 %collective-permute-start.4 = (bf16[16,2048]{1,0:T(8,128)(2,1)}, bf16[16,2048]{1,0:T(8,128)(2,1)}, u32[]{:S(2)}, u32[]{:S(2)}) collective-permute-start(bf16[16,2048]{1,0:T(8,128)(2,1)} %bitcast.30.refs_0_), channel_id=1, source_target_pairs={{0,4},{1,5},{2,6},{3,7},{4,0},{5,1},{6,2},{7,3},{8,12},{9,13},{10,... | collective-permute-start | bytes 196616 | tf_op jit(solution)/shard_map/ppermute | solution.py:212
  63.3 12.1 %collective-permute-start.5 = (bf16[16,2048]{1,0:T(8,128)(2,1)}, bf16[16,2048]{1,0:T(8,128)(2,1)}, u32[]{:S(2)}, u32[]{:S(2)}) collective-permute-start(bf16[16,2048]{1,0:T(8,128)(2,1)} %bitcast.30.refs_0_), channel_id=1, source_target_pairs={{0,6},{1,7},{2,0},{3,1},{4,2},{5,3},{6,4},{7,5},{8,14},{9,15},{10,... | collective-permute-start | bytes 196616 | tf_op jit(solution)/shard_map/ppermute | solution.py:212
  75.4 17.6 %copy-start.6 = (f32[256,1024]{1,0:T(8,128)S(1)}, f32[256,1024]{1,0:T(8,128)}, u32[]{:S(2)}) copy-start(f32[256,1024]{1,0:T(8,128)} %copy-done.5) | copy-start | bytes 3145732
  93.0 2.2 %copy-start.2 = (f32[1024,512]{1,0:T(8,128)S(1)}, f32[1024,512]{1,0:T(8,128)}, u32[]{:S(2)}) copy-start(f32[1024,512]{1,0:T(8,128)} %copy-done.1) | copy-start | bytes 6291460
  95.2 5.7 %collective-permute-start.6 = (f32[128,1024]{1,0:T(8,128)}, f32[128,1024]{1,0:T(8,128)}, u32[]{:S(2)}, u32[]{:S(2)}) collective-permute-start(f32[128,1024]{1,0:T(8,128)} %constant_dynamic-slice_fusion), channel_id=1, source_target_pairs={{0,1},{1,0},{2,3},{3,2},{4,5},{5,4},{6,7},{7,6},{8,9},{9,8},{10,11... | collective-permute-start | bytes 1572872 | tf_op jit(solution)/shard_map/ppermute | solution.py:240
  97.7 10.3 %collective-permute-start.13 = (f32[128,512]{1,0:T(8,128)S(1)}, f32[128,512]{1,0:T(8,128)S(1)}, u32[]{:S(2)}, u32[]{:S(2)}) collective-permute-start(f32[128,512]{1,0:T(8,128)S(1)} %get-tuple-element.11), channel_id=1, source_target_pairs={{0,6},{1,7},{2,0},{3,1},{4,2},{5,3},{6,4},{7,5},{8,14},{9,15},{10,... | collective-permute-start | bytes 786440 | tf_op jit(solution)/shard_map/ppermute | solution.py:227
  100.2 22.3 %collective-permute-start.12 = (f32[128,512]{1,0:T(8,128)S(1)}, f32[128,512]{1,0:T(8,128)S(1)}, u32[]{:S(2)}, u32[]{:S(2)}) collective-permute-start(f32[128,512]{1,0:T(8,128)S(1)} %get-tuple-element.12), channel_id=1, source_target_pairs={{0,4},{1,5},{2,6},{3,7},{4,0},{5,1},{6,2},{7,3},{8,12},{9,13},{10,... | collective-permute-start | bytes 786440 | tf_op jit(solution)/shard_map/ppermute | solution.py:227
  100.2 22.3 %collective-permute-start.11 = (f32[128,512]{1,0:T(8,128)S(1)}, f32[128,512]{1,0:T(8,128)S(1)}, u32[]{:S(2)}, u32[]{:S(2)}) collective-permute-start(f32[128,512]{1,0:T(8,128)S(1)} %get-tuple-element.10), channel_id=1, source_target_pairs={{0,2},{1,3},{2,4},{3,5},{4,6},{5,7},{6,0},{7,1},{8,10},{9,11},{10,... | collective-permute-start | bytes 786440 | tf_op jit(solution)/shard_map/ppermute | solution.py:227
  (3 other events, 3.0 us)

commit v8 on v7

--- a/solution.py
+++ b/solution.py
@@ -220,7 +220,6 @@
     mine = lax.dynamic_index_in_dim(blocks, core, axis=1, keepdims=False)
     theirs = lax.dynamic_index_in_dim(blocks, 1 - core, axis=1, keepdims=False)
     swapped = lax.ppermute(theirs, "grp", [(i, i ^ 1) for i in range(members)])
-    (gram_oth,) = gram_rows(others[:1], pick, codes, row0, 2 * own_rows, npar, False)
     chip_sum = mine + swapped
     moment_rows = lax.dynamic_index_in_dim(chip_sum, chip, axis=0, keepdims=False)
     arrived = [
@@ -229,9 +228,7 @@
             "grp", [(i, (i + 2 * k) % members) for i in range(members)])
         for k in range(1, pairs)
     ]
-    if len(others) > 1:
-        (gram_b,) = gram_rows(others[1:], pick, codes, row0, 2 * own_rows, npar, False)
-        gram_oth = gram_oth + gram_b
+    (gram_oth,) = gram_rows(others, pick, codes, row0, 2 * own_rows, npar, False)
     for block in arrived:
         moment_rows = moment_rows + block
     gram_chip = gram_own + gram_oth

time: 125 us -> 128 us (1.024)
  waiting for transfers between devices: 41 us -> 45.5 us
  Pallas kernels: 42.4 us -> 41 us
    ppermute x3, waiting for transfers between devices: 1.32 us -> 4.31 us  [on_device(): lax.ppermute(meta_r, 'grp', [(i, (i + 2 * k) % members) for i in range(me...]
    ppermute x3, waiting for transfers between devices: 19.6 us -> 21.2 us  [on_device(): lax.ppermute(lax.dynamic_index_in_dim(chip_sum, (chip + k) % pairs, axis=...]
    pallas_call x3 -> x2, Pallas kernels: 37.2 us -> 35.8 us  [gram_rows(): pl.pallas_call(kernel, grid_spec=grid_spec, out_shape=out_shape, compiler...]
  transfers between devices with their start and end apart: 14 -> 14, of which waited for: 5 -> 7; matrix products, arithmetic and copies ran while one was open for 7% -> 7% of each run, Pallas kernels for 30% -> 28%
where the time goes in v8:
time: 128 us
  waiting for transfers between devices  45.5 us (36%)
  Pallas kernels  41 us (32%)
  starting transfers between devices  18.2 us (14%)
  local copies, waits for them, and re-layouts  9.65 us (8%)
  other arithmetic  7.34 us (6%)
  matrix products  4.92 us (4%)
    pallas_call x2, Pallas kernels, gram_rows(): pl.pallas_call(kernel, grid_spec=grid_spec, out_shape=out_shape, compiler...  35.8 us
    ppermute x3, waiting for transfers between devices, on_device(): lax.ppermute(lax.dynamic_index_in_dim(chip_sum, (chip + k) % pairs, axis=...  21.2 us
    ppermute x6, waiting for transfers between devices, exchange(): lax.ppermute(blocks[m], 'elem', [(i, i ^ m) for i in range(groups)])  20 us
    ppermute x6, starting transfers between devices, exchange(): lax.ppermute(blocks[m], 'elem', [(i, i ^ m) for i in range(groups)])  9.3 us
    ppermute x3, starting transfers between devices, on_device(): lax.ppermute(meta_r, 'grp', [(i, (i + 2 * k) % members) for i in range(me...  5.53 us
    pallas_call x1, Pallas kernels, moment_sums(): pl.pallas_call(functools.partial(moment_kernel, scale=scale), grid=(terms...  5.16 us
    unnamed x26, local copies, waits for them, and re-layouts  4.37 us
    ppermute x3, waiting for transfers between devices, on_device(): lax.ppermute(meta_r, 'grp', [(i, (i + 2 * k) % members) for i in range(me...  4.31 us
  transfers between devices with their start and end apart: 14, of which 7 were waited for; matrix products, arithmetic and copies ran while one was open for 7% of the time, Pallas kernels for 28%

profile of v8, /device:TPU:0, one launch (start us, length us, event | category | flops | bytes accessed | tf_op | source)
XLA Modules:
  0.0 127.5 jit_solution(9589965027689822794)
XLA Ops:
  0.7 1.3 %fusion.19 = f32[1024]{0:T(1024)S(1)} fusion(s32[1024]{0:T(1024)} %param.9, s32[4]{0:T(128)S(1)} %iota_xor_fusion), kind=kOutput, calls=%fused_computation.15 | convolution fusion | flops 9452544 | bytes 8208 | tf_op jit(solution)/shard_map/dot_general | solution.py:186
  3.1 2.3 %fusion.9 = bf16[4,512,512]{2,1,0:T(8,128)(2,1)S(1)} fusion(pred[512,1024]{1,0:T(8,128)(4,1)S(1)} %iota_compare_fusion.2, pred[4,1024]{1,0:T(4,128)(4,1)S(1)} %broadcast_compare_fusion, bf16[1024,512]{1,0:T(8,128)(2,1)S(1)} %copy-done), kind=kOutput, calls=%fused_computation.11 | convolution fusion | flops 2150629376 | bytes 3674112 | tf_op jit(solution)/shard_map/eis,sq->eiq/dot_general | solution.py:191
  5.5 1.4 %slice_bitcast_fusion = (bf16[512,512]{1,0:T(8,128)(2,1)}, bf16[512,512]{1,0:T(8,128)(2,1)}, bf16[512,512]{1,0:T(8,128)(2,1)}, bf16[512,512]{1,0:T(8,128)(2,1)}) fusion(bf16[4,512,512]{2,1,0:T(8,128)(2,1)S(1)} %fusion.9), kind=kLoop, calls=%fused_computation.19 | loop fusion | bytes 4194304 | tf_op jit(solution)/shard_map/squeeze | solution.py:166
  6.8 3.0 %collective-permute-start.7 = (bf16[512,512]{1,0:T(8,128)(2,1)}, bf16[512,512]{1,0:T(8,128)(2,1)}, u32[]{:S(2)}, u32[]{:S(2)}) collective-permute-start(bf16[512,512]{1,0:T(8,128)(2,1)} %get-tuple-element.8), channel_id=1, source_target_pairs={{0,8},{8,0},{16,24},{24,16},{1,9},{9,1},{17,25},{25,17},{2,10},{10... | collective-permute-start | bytes 1572872 | tf_op jit(solution)/shard_map/ppermute | solution.py:166
  9.8 1.5 %collective-permute-start.8 = (bf16[512,512]{1,0:T(8,128)(2,1)}, bf16[512,512]{1,0:T(8,128)(2,1)}, u32[]{:S(2)}, u32[]{:S(2)}) collective-permute-start(bf16[512,512]{1,0:T(8,128)(2,1)} %get-tuple-element.7), channel_id=1, source_target_pairs={{0,16},{8,24},{16,0},{24,8},{1,17},{9,25},{17,1},{25,9},{2,18},{10... | collective-permute-start | bytes 1572872 | tf_op jit(solution)/shard_map/ppermute | solution.py:166
  13.3 2.9 %collective-permute-start.2 = (bf16[16,512]{1,0:T(8,128)(2,1)S(1)}, bf16[16,512]{1,0:T(8,128)(2,1)S(1)}, u32[]{:S(2)}, u32[]{:S(2)}) collective-permute-start(bf16[16,512]{1,0:T(8,128)(2,1)S(1)} %get-tuple-element.18), channel_id=1, source_target_pairs={{0,24},{8,16},{16,8},{24,0},{1,25},{9,17},{17,9},{25,1},{2,26},{10... | collective-permute-start | bytes 49160 | tf_op jit(solution)/shard_map/ppermute | solution.py:166
  16.8 18.1 %collective-permute-done.2 = bf16[16,512]{1,0:T(8,128)(2,1)S(1)} collective-permute-done((bf16[16,512]{1,0:T(8,128)(2,1)S(1)}, bf16[16,512]{1,0:T(8,128)(2,1)S(1)}, u32[]{:S(2)}, u32[]{:S(2)}) %collective-permute-start.2) | collective-permute-done | bytes 16416 | tf_op jit(solution)/shard_map/ppermute | solution.py:166
  34.8 1.4 %collective-permute-start = (bf16[16,512]{1,0:T(8,128)(2,1)}, bf16[16,512]{1,0:T(8,128)(2,1)}, u32[]{:S(2)}, u32[]{:S(2)}) collective-permute-start(bf16[16,512]{1,0:T(8,128)(2,1)} %get-tuple-element.20), channel_id=1, source_target_pairs={{0,8},{8,0},{16,24},{24,16},{1,9},{9,1},{17,25},{25,17},{2,10},{10... | collective-permute-start | bytes 49160 | tf_op jit(solution)/shard_map/ppermute | solution.py:166
  37.0 1.9 %collective-permute-done = bf16[16,512]{1,0:T(8,128)(2,1)} collective-permute-done((bf16[16,512]{1,0:T(8,128)(2,1)}, bf16[16,512]{1,0:T(8,128)(2,1)}, u32[]{:S(2)}, u32[]{:S(2)}) %collective-permute-start) | collective-permute-done | bytes 16416 | tf_op jit(solution)/shard_map/ppermute | solution.py:166
  40.3 10.3 %shard_map.77 = (f32[256,1024]{1,0:T(8,128)S(1)}, bf16[1024,2048]{1,0:T(8,128)(2,1)}) custom-call(s32[1]{0:T(128)} %bitcast.row0_ref, bf16[16,2048]{1,0:T(8,128)(2,1)} %bitcast.30.refs_0_, bf16[3,256,192]{2,1,0:T(8,128)(2,1)S(1)} %copy-done.4, s32[4,1024,1]{2,1,0:T(8,128)S(1)} %copy.10.refs_2_.refs_4_), custom_call_target="tpu_custom_call" | custom-call | tf_op jit(solution)/shard_map/pallas_call | solution.py:124
  51.6 5.2 %shard_map.79 = f32[1024,512]{1,0:T(8,128)S(1)} custom-call(bf16[1024,2048]{1,0:T(8,128)(2,1)} %get-tuple-element.5.w_ref, bf16[512,512]{1,0:T(8,128)(2,1)S(1)} %copy-done.3, bf16[512,512]{1,0:T(8,128)(2,1)} %collective-permute-done.7.refs_1_, bf16[512,512]{1,0:T(8,128)(2,1)} %collective-permute-done.8.refs_2_, bf16[512,512]{1,0:T(8,128)(2,1)} %collective-permute-done.9.refs_3_), custom_call_target="tpu_custom_call" | custom-call | tf_op jit(solution)/shard_map/pallas_call | solution.py:147
  56.8 1.3 %copy-done.1 = f32[1024,512]{1,0:T(8,128)} copy-done((f32[1024,512]{1,0:T(8,128)}, f32[1024,512]{1,0:T(8,128)S(1)}, u32[]{:S(2)}) %copy-start.1) | copy-done | bytes 2097176
  59.1 1.6 %collective-permute-start.3 = (bf16[16,2048]{1,0:T(8,128)(2,1)}, bf16[16,2048]{1,0:T(8,128)(2,1)}, u32[]{:S(2)}, u32[]{:S(2)}) collective-permute-start(bf16[16,2048]{1,0:T(8,128)(2,1)} %bitcast.30.refs_0_), channel_id=1, source_target_pairs={{0,2},{1,3},{2,4},{3,5},{4,6},{5,7},{6,0},{7,1},{8,10},{9,11},{10,... | collective-permute-start | bytes 196616 | tf_op jit(solution)/shard_map/ppermute | solution.py:212
  60.7 2.6 %collective-permute-start.4 = (bf16[16,2048]{1,0:T(8,128)(2,1)}, bf16[16,2048]{1,0:T(8,128)(2,1)}, u32[]{:S(2)}, u32[]{:S(2)}) collective-permute-start(bf16[16,2048]{1,0:T(8,128)(2,1)} %bitcast.30.refs_0_), channel_id=1, source_target_pairs={{0,4},{1,5},{2,6},{3,7},{4,0},{5,1},{6,2},{7,3},{8,12},{9,13},{10,... | collective-permute-start | bytes 196616 | tf_op jit(solution)/shard_map/ppermute | solution.py:212
  63.3 1.3 %collective-permute-start.5 = (bf16[16,2048]{1,0:T(8,128)(2,1)}, bf16[16,2048]{1,0:T(8,128)(2,1)}, u32[]{:S(2)}, u32[]{:S(2)}) collective-permute-start(bf16[16,2048]{1,0:T(8,128)(2,1)} %bitcast.30.refs_0_), channel_id=1, source_target_pairs={{0,6},{1,7},{2,0},{3,1},{4,2},{5,3},{6,4},{7,5},{8,14},{9,15},{10,... | collective-permute-start | bytes 196616 | tf_op jit(solution)/shard_map/ppermute | solution.py:212
  64.7 1.3 %collective-permute-done.3.refs_0_ = bf16[16,2048]{1,0:T(8,128)(2,1)} collective-permute-done((bf16[16,2048]{1,0:T(8,128)(2,1)}, bf16[16,2048]{1,0:T(8,128)(2,1)}, u32[]{:S(2)}, u32[]{:S(2)}) %collective-permute-start.3) | collective-permute-done | bytes 65568 | tf_op jit(solution)/shard_map/ppermute | solution.py:212
  66.0 2.8 %collective-permute-done.4.refs_1_ = bf16[16,2048]{1,0:T(8,128)(2,1)} collective-permute-done((bf16[16,2048]{1,0:T(8,128)(2,1)}, bf16[16,2048]{1,0:T(8,128)(2,1)}, u32[]{:S(2)}, u32[]{:S(2)}) %collective-permute-start.4) | collective-permute-done | bytes 65568 | tf_op jit(solution)/shard_map/ppermute | solution.py:212
  69.0 25.6 %shard_map.78 = f32[256,1024]{1,0:T(8,128)S(1)} custom-call(s32[1]{0:T(128)} %bitcast.row0_ref, bf16[16,2048]{1,0:T(8,128)(2,1)} %collective-permute-done.3.refs_0_, bf16[16,2048]{1,0:T(8,128)(2,1)} %collective-permute-done.4.refs_1_, bf16[16,2048]{1,0:T(8,128)(2,1)} %collective-permute-done.5.refs_2_, bf16[3,256,192]{2,1,0:T(8,128)(2,1)S(1)} %copy-done.4, ...), custom_call_target="tpu_custom_call" | custom-call | tf_op jit(solution)/shard_map/pallas_call | solution.py:124
  96.6 1.4 %bitcast_add_fusion = f32[4,128,512]{2,1,0:T(8,128)S(1)} fusion(f32[4,128,512]{2,1,0:T(8,128)} %collective-permute-done.10, f32[4,2,128,512]{3,2,1,0:T(8,128)S(1)} %bitcast.64, s32[]{:T(128)S(6)} %select_n.58), kind=kLoop, calls=%fused_computation.16 | loop fusion | flops 262144 | bytes 3145732 | tf_op jit(solution)/shard_map/add | solution.py:223
  99.1 2.8 %collective-permute-start.13 = (f32[128,512]{1,0:T(8,128)S(1)}, f32[128,512]{1,0:T(8,128)S(1)}, u32[]{:S(2)}, u32[]{:S(2)}) collective-permute-start(f32[128,512]{1,0:T(8,128)S(1)} %get-tuple-element.11), channel_id=1, source_target_pairs={{0,6},{1,7},{2,0},{3,1},{4,2},{5,3},{6,4},{7,5},{8,14},{9,15},{10,... | collective-permute-start | bytes 786440 | tf_op jit(solution)/shard_map/ppermute | solution.py:226
  102.5 2.1 %multiply_bitcast_fusion = f32[1,128,1024]{2,1,0:T(8,128)} fusion(f32[128,1024]{1,0:T(8,128)} %collective-permute-done.6, f32[256,1024]{1,0:T(8,128)} %copy-done.7, s32[]{:T(128)S(6)} %select_n.56), kind=kLoop, calls=%fused_computation.23 | loop fusion | flops 262144 | bytes 1572868 | tf_op jit(solution)/shard_map/broadcast_in_dim | solution.py:239
  104.6 4.1 %collective-permute-done.13 = f32[128,512]{1,0:T(8,128)S(1)} collective-permute-done((f32[128,512]{1,0:T(8,128)S(1)}, f32[128,512]{1,0:T(8,128)S(1)}, u32[]{:S(2)}, u32[]{:S(2)}) %collective-permute-start.13) | collective-permute-done | bytes 262176 | tf_op jit(solution)/shard_map/ppermute | solution.py:226
  108.6 17.1 %collective-permute-done.12 = f32[128,512]{1,0:T(8,128)S(1)} collective-permute-done((f32[128,512]{1,0:T(8,128)S(1)}, f32[128,512]{1,0:T(8,128)S(1)}, u32[]{:S(2)}, u32[]{:S(2)}) %collective-permute-start.12) | collective-permute-done | bytes 262176 | tf_op jit(solution)/shard_map/ppermute | solution.py:226
  125.8 1.7 %fusion.23 = f32[1,128,512]{2,1,0:T(8,128)} fusion(f32[128,512]{1,0:T(8,128)S(1)} %collective-permute-done.13, f32[128,512]{1,0:T(8,128)S(1)} %collective-permute-done.12, f32[128,512]{1,0:T(8,128)S(1)} %collective-permute-done.11, f32[4,128,512]{2,1,0:T(8,128)} %copy-done.8, s32[]{:T(128)S(6)} %select_n.60), kind=kLoop, calls=%fused_computation.27 | loop fusion | flops 196608 | bytes 1310724 | tf_op jit(solution)/shard_map/broadcast_in_dim | solution.py:239
  (57 shorter events, 11.7 us)
Async XLA Ops:
  0.6 2.5 %copy-start = (bf16[1024,512]{1,0:T(8,128)(2,1)S(1)}, bf16[1024,512]{1,0:T(8,128)(2,1)}, u32[]{:S(2)}) copy-start(bf16[1024,512]{1,0:T(8,128)(2,1)} %param.7) | copy-start | bytes 3145732
  5.4 5.9 %copy-start.11 = (bf16[1024]{0:T(1024)(128)(2,1)S(1)}, bf16[1024]{0:T(1024)(128)(2,1)}, u32[]{:S(2)}) copy-start(bf16[1024]{0:T(1024)(128)(2,1)} %param.8) | copy-start | bytes 6148
  5.5 6.0 %copy-start.12 = (bf16[12,1024]{1,0:T(8,128)(2,1)S(1)}, bf16[12,1024]{1,0:T(8,128)(2,1)}, u32[]{:S(2)}) copy-start(bf16[12,1024]{1,0:T(8,128)(2,1)} %param.6) | copy-start | bytes 73732
  6.8 9.9 %copy-start.9 = (s32[1024,12]{0,1:T(8,128)S(1)}, s32[1024,12]{0,1:T(8,128)}, u32[]{:S(2)}) copy-start(s32[1024,12]{0,1:T(8,128)} %param.10) | copy-start | bytes 147460
  6.8 44.7 %collective-permute-start.7 = (bf16[512,512]{1,0:T(8,128)(2,1)}, bf16[512,512]{1,0:T(8,128)(2,1)}, u32[]{:S(2)}, u32[]{:S(2)}) collective-permute-start(bf16[512,512]{1,0:T(8,128)(2,1)} %get-tuple-element.8), channel_id=1, source_target_pairs={{0,8},{8,0},{16,24},{24,16},{1,9},{9,1},{17,25},{25,17},{2,10},{10... | collective-permute-start | bytes 1572872 | tf_op jit(solution)/shard_map/ppermute | solution.py:166
  9.8 41.8 %collective-permute-start.8 = (bf16[512,512]{1,0:T(8,128)(2,1)}, bf16[512,512]{1,0:T(8,128)(2,1)}, u32[]{:S(2)}, u32[]{:S(2)}) collective-permute-start(bf16[512,512]{1,0:T(8,128)(2,1)} %get-tuple-element.7), channel_id=1, source_target_pairs={{0,16},{8,24},{16,0},{24,8},{1,17},{9,25},{17,1},{25,9},{2,18},{10... | collective-permute-start | bytes 1572872 | tf_op jit(solution)/shard_map/ppermute | solution.py:166
  11.3 40.3 %collective-permute-start.9 = (bf16[512,512]{1,0:T(8,128)(2,1)}, bf16[512,512]{1,0:T(8,128)(2,1)}, u32[]{:S(2)}, u32[]{:S(2)}) collective-permute-start(bf16[512,512]{1,0:T(8,128)(2,1)} %get-tuple-element.6), channel_id=1, source_target_pairs={{0,24},{8,16},{16,8},{24,0},{1,25},{9,17},{17,9},{25,1},{2,26},{10... | collective-permute-start | bytes 1572872 | tf_op jit(solution)/shard_map/ppermute | solution.py:166
  12.7 27.6 %copy-start.4 = (bf16[3,256,192]{2,1,0:T(8,128)(2,1)S(1)}, bf16[3,256,192]{2,1,0:T(8,128)(2,1)}, u32[]{:S(2)}) copy-start(bf16[3,256,192]{2,1,0:T(8,128)(2,1)} %constant.84.clone.refs_1_.refs_3_) | copy-start | bytes 884740
  13.3 21.5 %collective-permute-start.2 = (bf16[16,512]{1,0:T(8,128)(2,1)S(1)}, bf16[16,512]{1,0:T(8,128)(2,1)S(1)}, u32[]{:S(2)}, u32[]{:S(2)}) collective-permute-start(bf16[16,512]{1,0:T(8,128)(2,1)S(1)} %get-tuple-element.18), channel_id=1, source_target_pairs={{0,24},{8,16},{16,8},{24,0},{1,25},{9,17},{17,9},{25,1},{2,26},{10... | collective-permute-start | bytes 49160 | tf_op jit(solution)/shard_map/ppermute | solution.py:166
  16.2 20.7 %collective-permute-start.1 = (bf16[16,512]{1,0:T(8,128)(2,1)}, bf16[16,512]{1,0:T(8,128)(2,1)}, u32[]{:S(2)}, u32[]{:S(2)}) collective-permute-start(bf16[16,512]{1,0:T(8,128)(2,1)} %get-tuple-element.19), channel_id=1, source_target_pairs={{0,16},{8,24},{16,0},{24,8},{1,17},{9,25},{17,1},{25,9},{2,18},{10... | collective-permute-start | bytes 49160 | tf_op jit(solution)/shard_map/ppermute | solution.py:166
  34.8 1.4 %copy-start.10 = (bf16[16,512]{1,0:T(8,128)(2,1)}, bf16[16,512]{1,0:T(8,128)(2,1)S(1)}, u32[]{:S(2)}) copy-start(bf16[16,512]{1,0:T(8,128)(2,1)S(1)} %collective-permute-done.2) | copy-start | bytes 49156
  34.8 4.1 %collective-permute-start = (bf16[16,512]{1,0:T(8,128)(2,1)}, bf16[16,512]{1,0:T(8,128)(2,1)}, u32[]{:S(2)}, u32[]{:S(2)}) collective-permute-start(bf16[16,512]{1,0:T(8,128)(2,1)} %get-tuple-element.20), channel_id=1, source_target_pairs={{0,8},{8,0},{16,24},{24,16},{1,9},{9,1},{17,25},{25,17},{2,10},{10... | collective-permute-start | bytes 49160 | tf_op jit(solution)/shard_map/ppermute | solution.py:166
  36.9 14.7 %copy-start.3 = (bf16[512,512]{1,0:T(8,128)(2,1)S(1)}, bf16[512,512]{1,0:T(8,128)(2,1)}, u32[]{:S(2)}) copy-start(bf16[512,512]{1,0:T(8,128)(2,1)} %get-tuple-element.9.refs_0_) | copy-start | bytes 1572868
  56.8 1.3 %copy-start.1 = (f32[1024,512]{1,0:T(8,128)}, f32[1024,512]{1,0:T(8,128)S(1)}, u32[]{:S(2)}) copy-start(f32[1024,512]{1,0:T(8,128)S(1)} %shard_map.79) | copy-start | bytes 6291460
  59.1 37.5 %collective-permute-start.10 = (f32[4,128,512]{2,1,0:T(8,128)}, f32[4,128,512]{2,1,0:T(8,128)}, u32[]{:S(2)}, u32[]{:S(2)}) collective-permute-start(f32[4,128,512]{2,1,0:T(8,128)} %dynamic-slice_bitcast_fusion), channel_id=1, source_target_pairs={{0,1},{1,0},{2,3},{3,2},{4,5},{5,4},{6,7},{7,6},{8,9},{9,8},{10,11... | collective-permute-start | bytes 3145736 | tf_op jit(solution)/shard_map/ppermute | solution.py:222
  59.1 6.8 %collective-permute-start.3 = (bf16[16,2048]{1,0:T(8,128)(2,1)}, bf16[16,2048]{1,0:T(8,128)(2,1)}, u32[]{:S(2)}, u32[]{:S(2)}) collective-permute-start(bf16[16,2048]{1,0:T(8,128)(2,1)} %bitcast.30.refs_0_), channel_id=1, source_target_pairs={{0,2},{1,3},{2,4},{3,5},{4,6},{5,7},{6,0},{7,1},{8,10},{9,11},{10,... | collective-permute-start | bytes 196616 | tf_op jit(solution)/shard_map/ppermute | solution.py:212
  60.7 8.0 %collective-permute-start.4 = (bf16[16,2048]{1,0:T(8,128)(2,1)}, bf16[16,2048]{1,0:T(8,128)(2,1)}, u32[]{:S(2)}, u32[]{:S(2)}) collective-permute-start(bf16[16,2048]{1,0:T(8,128)(2,1)} %bitcast.30.refs_0_), channel_id=1, source_target_pairs={{0,4},{1,5},{2,6},{3,7},{4,0},{5,1},{6,2},{7,3},{8,12},{9,13},{10,... | collective-permute-start | bytes 196616 | tf_op jit(solution)/shard_map/ppermute | solution.py:212
  63.3 5.7 %collective-permute-start.5 = (bf16[16,2048]{1,0:T(8,128)(2,1)}, bf16[16,2048]{1,0:T(8,128)(2,1)}, u32[]{:S(2)}, u32[]{:S(2)}) collective-permute-start(bf16[16,2048]{1,0:T(8,128)(2,1)} %bitcast.30.refs_0_), channel_id=1, source_target_pairs={{0,6},{1,7},{2,0},{3,1},{4,2},{5,3},{6,4},{7,5},{8,14},{9,15},{10,... | collective-permute-start | bytes 196616 | tf_op jit(solution)/shard_map/ppermute | solution.py:212
  64.7 29.9 %copy-start.6 = (f32[256,1024]{1,0:T(8,128)S(1)}, f32[256,1024]{1,0:T(8,128)}, u32[]{:S(2)}) copy-start(f32[256,1024]{1,0:T(8,128)} %copy-done.5) | copy-start | bytes 3145732
  94.5 2.1 %copy-start.2 = (f32[1024,512]{1,0:T(8,128)S(1)}, f32[1024,512]{1,0:T(8,128)}, u32[]{:S(2)}) copy-start(f32[1024,512]{1,0:T(8,128)} %copy-done.1) | copy-start | bytes 6291460
  96.6 5.9 %collective-permute-start.6 = (f32[128,1024]{1,0:T(8,128)}, f32[128,1024]{1,0:T(8,128)}, u32[]{:S(2)}, u32[]{:S(2)}) collective-permute-start(f32[128,1024]{1,0:T(8,128)} %constant_dynamic-slice_fusion), channel_id=1, source_target_pairs={{0,1},{1,0},{2,3},{3,2},{4,5},{5,4},{6,7},{7,6},{8,9},{9,8},{10,11... | collective-permute-start | bytes 1572872 | tf_op jit(solution)/shard_map/ppermute | solution.py:237
  99.1 9.5 %collective-permute-start.13 = (f32[128,512]{1,0:T(8,128)S(1)}, f32[128,512]{1,0:T(8,128)S(1)}, u32[]{:S(2)}, u32[]{:S(2)}) collective-permute-start(f32[128,512]{1,0:T(8,128)S(1)} %get-tuple-element.11), channel_id=1, source_target_pairs={{0,6},{1,7},{2,0},{3,1},{4,2},{5,3},{6,4},{7,5},{8,14},{9,15},{10,... | collective-permute-start | bytes 786440 | tf_op jit(solution)/shard_map/ppermute | solution.py:226
  101.9 23.9 %collective-permute-start.12 = (f32[128,512]{1,0:T(8,128)S(1)}, f32[128,512]{1,0:T(8,128)S(1)}, u32[]{:S(2)}, u32[]{:S(2)}) collective-permute-start(f32[128,512]{1,0:T(8,128)S(1)} %get-tuple-element.12), channel_id=1, source_target_pairs={{0,4},{1,5},{2,6},{3,7},{4,0},{5,1},{6,2},{7,3},{8,12},{9,13},{10,... | collective-permute-start | bytes 786440 | tf_op jit(solution)/shard_map/ppermute | solution.py:226
  102.3 23.5 %collective-permute-start.11 = (f32[128,512]{1,0:T(8,128)S(1)}, f32[128,512]{1,0:T(8,128)S(1)}, u32[]{:S(2)}, u32[]{:S(2)}) collective-permute-start(f32[128,512]{1,0:T(8,128)S(1)} %get-tuple-element.10), channel_id=1, source_target_pairs={{0,2},{1,3},{2,4},{3,5},{4,6},{5,7},{6,0},{7,1},{8,10},{9,11},{10,... | collective-permute-start | bytes 786440 | tf_op jit(solution)/shard_map/ppermute | solution.py:226
  (3 other events, 3.0 us)

commit v9 on v8

--- a/solution.py
+++ b/solution.py
@@ -42,10 +42,13 @@
     return jnp.stack(codes)[:, :, None], jnp.asarray(pick, jnp.bfloat16)
 
 
-def gram_kernel(row0_ref, *refs, npar, n_meta, per, picked, with_weighted):
+def gram_kernel(row0_ref, *refs, npar, n_meta, per, picked, with_weighted, with_init):
     metas = refs[:n_meta]
-    pick_ref, code_ref, gram_ref = refs[n_meta:n_meta + 3]
-    wt_refs = refs[n_meta + 3:-1] if with_weighted else ()
+    pick_ref, code_ref = refs[n_meta:n_meta + 2]
+    rest = refs[n_meta + 2:]
+    init_refs = rest[:1] if with_init else ()
+    gram_ref = rest[len(init_refs)]
+    wt_refs = rest[len(init_refs) + 1:-1] if with_weighted else ()
     oh_ref = refs[-1]
     step = pl.program_id(0)
     groups, _, width3 = oh_ref.shape
@@ -53,7 +56,7 @@
 
     @pl.when(step == 0)
     def _():
-        gram_ref[...] = jnp.zeros_like(gram_ref)
+        gram_ref[...] = init_refs[0][...] if with_init else jnp.zeros_like(gram_ref)
         lanes = lax.broadcasted_iota(jnp.int32, (1, width3), 1) % width
         for g in range(groups):
             oh_ref[g] = (code_ref[g] == lanes).astype(jnp.bfloat16)
@@ -93,7 +96,7 @@
         wt_refs[0][...] = (w * basis).astype(jnp.bfloat16)
 
 
-def gram_rows(metas, pick, codes, row0, picked, npar, with_weighted, block=1024):
+def gram_rows(metas, pick, codes, row0, picked, npar, with_weighted, block=1024, init=None):
     rows, samples = metas[0].shape
     per = samples // block
     n_meta = len(metas)
@@ -114,12 +117,13 @@
         in_specs=[pl.BlockSpec((rows, block), meta_map(k)) for k in range(n_meta)] + [
             pl.BlockSpec(pick.shape, lambda i, r: (0, 0, 0)),
             pl.BlockSpec(codes.shape, lambda i, r: (0, 0, 0)),
-        ],
+        ] + ([pl.BlockSpec((picked, terms), lambda i, r: (0, 0))] if init is not None else []),
         out_specs=out_specs,
         scratch_shapes=[pltpu.VMEM((groups, terms, width3), jnp.bfloat16)],
     )
     kernel = functools.partial(
-        gram_kernel, npar=npar, n_meta=n_meta, per=per, picked=picked, with_weighted=with_weighted
+        gram_kernel, npar=npar, n_meta=n_meta, per=per, picked=picked, with_weighted=with_weighted,
+        with_init=init is not None,
     )
     return pl.pallas_call(
         kernel,
@@ -128,7 +132,7 @@
         compiler_params=pltpu.CompilerParams(
             dimension_semantics=("arbitrary",), vmem_limit_bytes=48 * 1024 * 1024
         ),
-    )(row0, *metas, pick, codes)
+    )(row0, *metas, pick, codes, *([init] if init is not None else []))
 
 
 def moment_kernel(w_ref, *refs, scale):
@@ -228,10 +232,9 @@
             "grp", [(i, (i + 2 * k) % members) for i in range(members)])
         for k in range(1, pairs)
     ]
-    (gram_oth,) = gram_rows(others, pick, codes, row0, 2 * own_rows, npar, False)
+    (gram_chip,) = gram_rows(others, pick, codes, row0, 2 * own_rows, npar, False, init=gram_own)
     for block in arrived:
         moment_rows = moment_rows + block
-    gram_chip = gram_own + gram_oth
     keep = lax.dynamic_slice_in_dim(gram_chip, core * own_rows, own_rows, axis=0)
     send = lax.dynamic_slice_in_dim(gram_chip, (1 - core) * own_rows, own_rows, axis=0)
     recv = lax.ppermute(send, "grp", [(i, i ^ 1) for i in range(members)])

time: 128 us -> 130 us (1.016)
    unnamed x26 -> x24, local copies, waits for them, and re-layouts: 4.37 us -> 4.62 us
where the time goes in v9:
time: 130 us; the launch traced here: 129 us
  waiting for transfers between devices  46.1 us (35%)
  Pallas kernels  41 us (32%)
  starting transfers between devices  18.1 us (14%)
  local copies, waits for them, and re-layouts  10.7 us (8%)
  other arithmetic  7.56 us (6%)
  matrix products  4.92 us (4%)
    pallas_call x2, Pallas kernels, gram_rows(): pl.pallas_call(kernel, grid_spec=grid_spec, out_shape=out_shape, compiler...  35.8 us
    ppermute x3, waiting for transfers between devices, on_device(): lax.ppermute(lax.dynamic_index_in_dim(chip_sum, (chip + k) % pairs, axis=...  21.8 us
    ppermute x6, waiting for transfers between devices, exchange(): lax.ppermute(blocks[m], 'elem', [(i, i ^ m) for i in range(groups)])  20 us
    ppermute x6, starting transfers between devices, exchange(): lax.ppermute(blocks[m], 'elem', [(i, i ^ m) for i in range(groups)])  9.3 us
    ppermute x3, starting transfers between devices, on_device(): lax.ppermute(meta_r, 'grp', [(i, (i + 2 * k) % members) for i in range(me...  5.52 us
    pallas_call x1, Pallas kernels, moment_sums(): pl.pallas_call(functools.partial(moment_kernel, scale=scale), grid=(terms...  5.16 us
    unnamed x24, local copies, waits for them, and re-layouts  4.62 us
    ppermute x3, waiting for transfers between devices, on_device(): lax.ppermute(meta_r, 'grp', [(i, (i + 2 * k) % members) for i in range(me...  4.31 us
  transfers between devices with their start and end apart: 14, of which 7 were waited for; matrix products, arithmetic and copies ran while one was open for 7% of the time, Pallas kernels for 28%

profile of v9, /device:TPU:0, one launch (start us, length us, event | category | flops | bytes accessed | tf_op | source)
XLA Modules:
  0.0 129.2 jit_solution(14614681064885265334)
XLA Ops:
  0.7 1.3 %fusion.19 = f32[1024]{0:T(1024)S(1)} fusion(s32[1024]{0:T(1024)} %param.9, s32[4]{0:T(128)S(1)} %iota_xor_fusion), kind=kOutput, calls=%fused_computation.15 | convolution fusion | flops 9452544 | bytes 8208 | tf_op jit(solution)/shard_map/dot_general | solution.py:190
  3.1 2.3 %fusion.9 = bf16[4,512,512]{2,1,0:T(8,128)(2,1)S(1)} fusion(pred[512,1024]{1,0:T(8,128)(4,1)S(1)} %iota_compare_fusion.2, pred[4,1024]{1,0:T(4,128)(4,1)S(1)} %broadcast_compare_fusion, bf16[1024,512]{1,0:T(8,128)(2,1)S(1)} %copy-done), kind=kOutput, calls=%fused_computation.11 | convolution fusion | flops 2150629376 | bytes 3674112 | tf_op jit(solution)/shard_map/eis,sq->eiq/dot_general | solution.py:195
  5.5 1.4 %slice_bitcast_fusion = (bf16[512,512]{1,0:T(8,128)(2,1)}, bf16[512,512]{1,0:T(8,128)(2,1)}, bf16[512,512]{1,0:T(8,128)(2,1)}, bf16[512,512]{1,0:T(8,128)(2,1)}) fusion(bf16[4,512,512]{2,1,0:T(8,128)(2,1)S(1)} %fusion.9), kind=kLoop, calls=%fused_computation.19 | loop fusion | bytes 4194304 | tf_op jit(solution)/shard_map/squeeze | solution.py:170
  6.8 3.0 %collective-permute-start.7 = (bf16[512,512]{1,0:T(8,128)(2,1)}, bf16[512,512]{1,0:T(8,128)(2,1)}, u32[]{:S(2)}, u32[]{:S(2)}) collective-permute-start(bf16[512,512]{1,0:T(8,128)(2,1)} %get-tuple-element.8), channel_id=1, source_target_pairs={{0,8},{8,0},{16,24},{24,16},{1,9},{9,1},{17,25},{25,17},{2,10},{10... | collective-permute-start | bytes 1572872 | tf_op jit(solution)/shard_map/ppermute | solution.py:170
  9.8 1.5 %collective-permute-start.8 = (bf16[512,512]{1,0:T(8,128)(2,1)}, bf16[512,512]{1,0:T(8,128)(2,1)}, u32[]{:S(2)}, u32[]{:S(2)}) collective-permute-start(bf16[512,512]{1,0:T(8,128)(2,1)} %get-tuple-element.7), channel_id=1, source_target_pairs={{0,16},{8,24},{16,0},{24,8},{1,17},{9,25},{17,1},{25,9},{2,18},{10... | collective-permute-start | bytes 1572872 | tf_op jit(solution)/shard_map/ppermute | solution.py:170
  13.3 2.9 %collective-permute-start.2 = (bf16[16,512]{1,0:T(8,128)(2,1)S(1)}, bf16[16,512]{1,0:T(8,128)(2,1)S(1)}, u32[]{:S(2)}, u32[]{:S(2)}) collective-permute-start(bf16[16,512]{1,0:T(8,128)(2,1)S(1)} %get-tuple-element.18), channel_id=1, source_target_pairs={{0,24},{8,16},{16,8},{24,0},{1,25},{9,17},{17,9},{25,1},{2,26},{10... | collective-permute-start | bytes 49160 | tf_op jit(solution)/shard_map/ppermute | solution.py:170
  16.8 18.1 %collective-permute-done.2 = bf16[16,512]{1,0:T(8,128)(2,1)S(1)} collective-permute-done((bf16[16,512]{1,0:T(8,128)(2,1)S(1)}, bf16[16,512]{1,0:T(8,128)(2,1)S(1)}, u32[]{:S(2)}, u32[]{:S(2)}) %collective-permute-start.2) | collective-permute-done | bytes 16416 | tf_op jit(solution)/shard_map/ppermute | solution.py:170
  34.8 1.4 %collective-permute-start = (bf16[16,512]{1,0:T(8,128)(2,1)}, bf16[16,512]{1,0:T(8,128)(2,1)}, u32[]{:S(2)}, u32[]{:S(2)}) collective-permute-start(bf16[16,512]{1,0:T(8,128)(2,1)} %get-tuple-element.20), channel_id=1, source_target_pairs={{0,8},{8,0},{16,24},{24,16},{1,9},{9,1},{17,25},{25,17},{2,10},{10... | collective-permute-start | bytes 49160 | tf_op jit(solution)/shard_map/ppermute | solution.py:170
  37.0 1.9 %collective-permute-done = bf16[16,512]{1,0:T(8,128)(2,1)} collective-permute-done((bf16[16,512]{1,0:T(8,128)(2,1)}, bf16[16,512]{1,0:T(8,128)(2,1)}, u32[]{:S(2)}, u32[]{:S(2)}) %collective-permute-start) | collective-permute-done | bytes 16416 | tf_op jit(solution)/shard_map/ppermute | solution.py:170
  40.3 10.2 %shard_map.77 = (f32[256,1024]{1,0:T(8,128)S(1)}, bf16[1024,2048]{1,0:T(8,128)(2,1)}) custom-call(s32[1]{0:T(128)} %bitcast.row0_ref, bf16[16,2048]{1,0:T(8,128)(2,1)} %bitcast.30.refs_0_, bf16[3,256,192]{2,1,0:T(8,128)(2,1)S(1)} %copy-done.5, s32[4,1024,1]{2,1,0:T(8,128)S(1)} %copy.11.refs_2_.refs_4_), custom_call_target="tpu_custom_call" | custom-call | tf_op jit(solution)/shard_map/pallas_call | solution.py:128
  51.6 5.2 %shard_map.79 = f32[1024,512]{1,0:T(8,128)S(1)} custom-call(bf16[1024,2048]{1,0:T(8,128)(2,1)} %get-tuple-element.5.w_ref, bf16[512,512]{1,0:T(8,128)(2,1)S(1)} %copy-done.4, bf16[512,512]{1,0:T(8,128)(2,1)} %collective-permute-done.7.refs_1_, bf16[512,512]{1,0:T(8,128)(2,1)} %collective-permute-done.8.refs_2_, bf16[512,512]{1,0:T(8,128)(2,1)} %collective-permute-done.9.refs_3_), custom_call_target="tpu_custom_call" | custom-call | tf_op jit(solution)/shard_map/pallas_call | solution.py:151
  56.8 1.3 %copy-done.1 = f32[1024,512]{1,0:T(8,128)} copy-done((f32[1024,512]{1,0:T(8,128)}, f32[1024,512]{1,0:T(8,128)S(1)}, u32[]{:S(2)}) %copy-start.1) | copy-done | bytes 2097176
  59.1 1.6 %collective-permute-start.3 = (bf16[16,2048]{1,0:T(8,128)(2,1)}, bf16[16,2048]{1,0:T(8,128)(2,1)}, u32[]{:S(2)}, u32[]{:S(2)}) collective-permute-start(bf16[16,2048]{1,0:T(8,128)(2,1)} %bitcast.30.refs_0_), channel_id=1, source_target_pairs={{0,2},{1,3},{2,4},{3,5},{4,6},{5,7},{6,0},{7,1},{8,10},{9,11},{10,... | collective-permute-start | bytes 196616 | tf_op jit(solution)/shard_map/ppermute | solution.py:216
  60.7 2.6 %collective-permute-start.4 = (bf16[16,2048]{1,0:T(8,128)(2,1)}, bf16[16,2048]{1,0:T(8,128)(2,1)}, u32[]{:S(2)}, u32[]{:S(2)}) collective-permute-start(bf16[16,2048]{1,0:T(8,128)(2,1)} %bitcast.30.refs_0_), channel_id=1, source_target_pairs={{0,4},{1,5},{2,6},{3,7},{4,0},{5,1},{6,2},{7,3},{8,12},{9,13},{10,... | collective-permute-start | bytes 196616 | tf_op jit(solution)/shard_map/ppermute | solution.py:216
  63.3 1.3 %collective-permute-start.5 = (bf16[16,2048]{1,0:T(8,128)(2,1)}, bf16[16,2048]{1,0:T(8,128)(2,1)}, u32[]{:S(2)}, u32[]{:S(2)}) collective-permute-start(bf16[16,2048]{1,0:T(8,128)(2,1)} %bitcast.30.refs_0_), channel_id=1, source_target_pairs={{0,6},{1,7},{2,0},{3,1},{4,2},{5,3},{6,4},{7,5},{8,14},{9,15},{10,... | collective-permute-start | bytes 196616 | tf_op jit(solution)/shard_map/ppermute | solution.py:216
  64.7 1.3 %collective-permute-done.3.refs_0_ = bf16[16,2048]{1,0:T(8,128)(2,1)} collective-permute-done((bf16[16,2048]{1,0:T(8,128)(2,1)}, bf16[16,2048]{1,0:T(8,128)(2,1)}, u32[]{:S(2)}, u32[]{:S(2)}) %collective-permute-start.3) | collective-permute-done | bytes 65568 | tf_op jit(solution)/shard_map/ppermute | solution.py:216
  66.0 2.8 %collective-permute-done.4.refs_1_ = bf16[16,2048]{1,0:T(8,128)(2,1)} collective-permute-done((bf16[16,2048]{1,0:T(8,128)(2,1)}, bf16[16,2048]{1,0:T(8,128)(2,1)}, u32[]{:S(2)}, u32[]{:S(2)}) %collective-permute-start.4) | collective-permute-done | bytes 65568 | tf_op jit(solution)/shard_map/ppermute | solution.py:216
  70.2 25.6 %shard_map.78 = f32[256,1024]{1,0:T(8,128)S(1)} custom-call(s32[1]{0:T(128)} %bitcast.row0_ref, bf16[16,2048]{1,0:T(8,128)(2,1)} %collective-permute-done.3.refs_0_, bf16[16,2048]{1,0:T(8,128)(2,1)} %collective-permute-done.4.refs_1_, bf16[16,2048]{1,0:T(8,128)(2,1)} %collective-permute-done.5.refs_2_, bf16[3,256,192]{2,1,0:T(8,128)(2,1)S(1)} %copy-done.5, ...), custom_call_target="tpu_custom_call" | custom-call | tf_op jit(solution)/shard_map/pallas_call | solution.py:128
  97.6 1.8 %bitcast_add_fusion = f32[4,128,512]{2,1,0:T(8,128)S(1)} fusion(f32[4,128,512]{2,1,0:T(8,128)} %collective-permute-done.10, f32[4,2,128,512]{3,2,1,0:T(8,128)} %bitcast.64, s32[]{:T(128)S(6)} %select_n.58), kind=kLoop, calls=%fused_computation.16 | loop fusion | flops 262144 | bytes 3145732 | tf_op jit(solution)/shard_map/add | solution.py:227
  100.4 2.7 %collective-permute-start.13 = (f32[128,512]{1,0:T(8,128)}, f32[128,512]{1,0:T(8,128)}, u32[]{:S(2)}, u32[]{:S(2)}) collective-permute-start(f32[128,512]{1,0:T(8,128)} %get-tuple-element.11), channel_id=1, source_target_pairs={{0,6},{1,7},{2,0},{3,1},{4,2},{5,3},{6,4},{7,5},{8,14},{9,15},{10,... | collective-permute-start | bytes 786440 | tf_op jit(solution)/shard_map/ppermute | solution.py:230
  103.6 1.9 %multiply_bitcast_fusion = f32[1,128,1024]{2,1,0:T(8,128)} fusion(f32[128,1024]{1,0:T(8,128)} %collective-permute-done.6, f32[256,1024]{1,0:T(8,128)S(1)} %copy-done.3, s32[]{:T(128)S(6)} %select_n.56), kind=kLoop, calls=%fused_computation.23 | loop fusion | flops 262144 | bytes 1572868 | tf_op jit(solution)/shard_map/broadcast_in_dim | solution.py:242
  105.5 4.6 %collective-permute-done.13 = f32[128,512]{1,0:T(8,128)} collective-permute-done((f32[128,512]{1,0:T(8,128)}, f32[128,512]{1,0:T(8,128)}, u32[]{:S(2)}, u32[]{:S(2)}) %collective-permute-start.13) | collective-permute-done | bytes 262176 | tf_op jit(solution)/shard_map/ppermute | solution.py:230
  110.2 17.1 %collective-permute-done.12 = f32[128,512]{1,0:T(8,128)} collective-permute-done((f32[128,512]{1,0:T(8,128)}, f32[128,512]{1,0:T(8,128)}, u32[]{:S(2)}, u32[]{:S(2)}) %collective-permute-start.12) | collective-permute-done | bytes 262176 | tf_op jit(solution)/shard_map/ppermute | solution.py:230
  127.3 1.9 %fusion.23 = f32[1,128,512]{2,1,0:T(8,128)} fusion(f32[128,512]{1,0:T(8,128)} %collective-permute-done.13, f32[128,512]{1,0:T(8,128)} %collective-permute-done.12, f32[128,512]{1,0:T(8,128)} %collective-permute-done.11, f32[4,128,512]{2,1,0:T(8,128)S(1)} %bitcast_add_fusion, s32[]{:T(128)S(6)} %select_n.60), kind=kLoop, calls=%fused_computation.27 | loop fusion | flops 196608 | bytes 1310724 | tf_op jit(solution)/shard_map/broadcast_in_dim | solution.py:242
  (54 shorter events, 12.5 us)
Async XLA Ops:
  0.6 2.5 %copy-start = (bf16[1024,512]{1,0:T(8,128)(2,1)S(1)}, bf16[1024,512]{1,0:T(8,128)(2,1)}, u32[]{:S(2)}) copy-start(bf16[1024,512]{1,0:T(8,128)(2,1)} %param.7) | copy-start | bytes 3145732
  5.4 5.9 %copy-start.10 = (bf16[1024]{0:T(1024)(128)(2,1)S(1)}, bf16[1024]{0:T(1024)(128)(2,1)}, u32[]{:S(2)}) copy-start(bf16[1024]{0:T(1024)(128)(2,1)} %param.8) | copy-start | bytes 6148
  5.5 6.0 %copy-start.11 = (bf16[12,1024]{1,0:T(8,128)(2,1)S(1)}, bf16[12,1024]{1,0:T(8,128)(2,1)}, u32[]{:S(2)}) copy-start(bf16[12,1024]{1,0:T(8,128)(2,1)} %param.6) | copy-start | bytes 73732
  6.8 9.9 %copy-start.8 = (s32[1024,12]{0,1:T(8,128)S(1)}, s32[1024,12]{0,1:T(8,128)}, u32[]{:S(2)}) copy-start(s32[1024,12]{0,1:T(8,128)} %param.10) | copy-start | bytes 147460
  6.8 44.7 %collective-permute-start.7 = (bf16[512,512]{1,0:T(8,128)(2,1)}, bf16[512,512]{1,0:T(8,128)(2,1)}, u32[]{:S(2)}, u32[]{:S(2)}) collective-permute-start(bf16[512,512]{1,0:T(8,128)(2,1)} %get-tuple-element.8), channel_id=1, source_target_pairs={{0,8},{8,0},{16,24},{24,16},{1,9},{9,1},{17,25},{25,17},{2,10},{10... | collective-permute-start | bytes 1572872 | tf_op jit(solution)/shard_map/ppermute | solution.py:170
  9.8 41.8 %collective-permute-start.8 = (bf16[512,512]{1,0:T(8,128)(2,1)}, bf16[512,512]{1,0:T(8,128)(2,1)}, u32[]{:S(2)}, u32[]{:S(2)}) collective-permute-start(bf16[512,512]{1,0:T(8,128)(2,1)} %get-tuple-element.7), channel_id=1, source_target_pairs={{0,16},{8,24},{16,0},{24,8},{1,17},{9,25},{17,1},{25,9},{2,18},{10... | collective-permute-start | bytes 1572872 | tf_op jit(solution)/shard_map/ppermute | solution.py:170
  11.3 40.2 %collective-permute-start.9 = (bf16[512,512]{1,0:T(8,128)(2,1)}, bf16[512,512]{1,0:T(8,128)(2,1)}, u32[]{:S(2)}, u32[]{:S(2)}) collective-permute-start(bf16[512,512]{1,0:T(8,128)(2,1)} %get-tuple-element.6), channel_id=1, source_target_pairs={{0,24},{8,16},{16,8},{24,0},{1,25},{9,17},{17,9},{25,1},{2,26},{10... | collective-permute-start | bytes 1572872 | tf_op jit(solution)/shard_map/ppermute | solution.py:170
  12.7 27.6 %copy-start.5 = (bf16[3,256,192]{2,1,0:T(8,128)(2,1)S(1)}, bf16[3,256,192]{2,1,0:T(8,128)(2,1)}, u32[]{:S(2)}) copy-start(bf16[3,256,192]{2,1,0:T(8,128)(2,1)} %constant.84.clone.refs_1_.refs_3_) | copy-start | bytes 884740
  13.3 21.5 %collective-permute-start.2 = (bf16[16,512]{1,0:T(8,128)(2,1)S(1)}, bf16[16,512]{1,0:T(8,128)(2,1)S(1)}, u32[]{:S(2)}, u32[]{:S(2)}) collective-permute-start(bf16[16,512]{1,0:T(8,128)(2,1)S(1)} %get-tuple-element.18), channel_id=1, source_target_pairs={{0,24},{8,16},{16,8},{24,0},{1,25},{9,17},{17,9},{25,1},{2,26},{10... | collective-permute-start | bytes 49160 | tf_op jit(solution)/shard_map/ppermute | solution.py:170
  16.2 20.7 %collective-permute-start.1 = (bf16[16,512]{1,0:T(8,128)(2,1)}, bf16[16,512]{1,0:T(8,128)(2,1)}, u32[]{:S(2)}, u32[]{:S(2)}) collective-permute-start(bf16[16,512]{1,0:T(8,128)(2,1)} %get-tuple-element.19), channel_id=1, source_target_pairs={{0,16},{8,24},{16,0},{24,8},{1,17},{9,25},{17,1},{25,9},{2,18},{10... | collective-permute-start | bytes 49160 | tf_op jit(solution)/shard_map/ppermute | solution.py:170
  34.8 1.4 %copy-start.9 = (bf16[16,512]{1,0:T(8,128)(2,1)}, bf16[16,512]{1,0:T(8,128)(2,1)S(1)}, u32[]{:S(2)}) copy-start(bf16[16,512]{1,0:T(8,128)(2,1)S(1)} %collective-permute-done.2) | copy-start | bytes 49156
  34.8 4.1 %collective-permute-start = (bf16[16,512]{1,0:T(8,128)(2,1)}, bf16[16,512]{1,0:T(8,128)(2,1)}, u32[]{:S(2)}, u32[]{:S(2)}) collective-permute-start(bf16[16,512]{1,0:T(8,128)(2,1)} %get-tuple-element.20), channel_id=1, source_target_pairs={{0,8},{8,0},{16,24},{24,16},{1,9},{9,1},{17,25},{25,17},{2,10},{10... | collective-permute-start | bytes 49160 | tf_op jit(solution)/shard_map/ppermute | solution.py:170
  36.9 14.6 %copy-start.4 = (bf16[512,512]{1,0:T(8,128)(2,1)S(1)}, bf16[512,512]{1,0:T(8,128)(2,1)}, u32[]{:S(2)}) copy-start(bf16[512,512]{1,0:T(8,128)(2,1)} %get-tuple-element.9.refs_0_) | copy-start | bytes 1572868
  56.8 1.3 %copy-start.1 = (f32[1024,512]{1,0:T(8,128)}, f32[1024,512]{1,0:T(8,128)S(1)}, u32[]{:S(2)}) copy-start(f32[1024,512]{1,0:T(8,128)S(1)} %shard_map.79) | copy-start | bytes 6291460
  59.1 38.5 %collective-permute-start.10 = (f32[4,128,512]{2,1,0:T(8,128)}, f32[4,128,512]{2,1,0:T(8,128)}, u32[]{:S(2)}, u32[]{:S(2)}) collective-permute-start(f32[4,128,512]{2,1,0:T(8,128)} %dynamic-slice_bitcast_fusion), channel_id=1, source_target_pairs={{0,1},{1,0},{2,3},{3,2},{4,5},{5,4},{6,7},{7,6},{8,9},{9,8},{10,11... | collective-permute-start | bytes 3145736 | tf_op jit(solution)/shard_map/ppermute | solution.py:226
  59.1 6.8 %collective-permute-start.3 = (bf16[16,2048]{1,0:T(8,128)(2,1)}, bf16[16,2048]{1,0:T(8,128)(2,1)}, u32[]{:S(2)}, u32[]{:S(2)}) collective-permute-start(bf16[16,2048]{1,0:T(8,128)(2,1)} %bitcast.30.refs_0_), channel_id=1, source_target_pairs={{0,2},{1,3},{2,4},{3,5},{4,6},{5,7},{6,0},{7,1},{8,10},{9,11},{10,... | collective-permute-start | bytes 196616 | tf_op jit(solution)/shard_map/ppermute | solution.py:216
  60.7 8.0 %collective-permute-start.4 = (bf16[16,2048]{1,0:T(8,128)(2,1)}, bf16[16,2048]{1,0:T(8,128)(2,1)}, u32[]{:S(2)}, u32[]{:S(2)}) collective-permute-start(bf16[16,2048]{1,0:T(8,128)(2,1)} %bitcast.30.refs_0_), channel_id=1, source_target_pairs={{0,4},{1,5},{2,6},{3,7},{4,0},{5,1},{6,2},{7,3},{8,12},{9,13},{10,... | collective-permute-start | bytes 196616 | tf_op jit(solution)/shard_map/ppermute | solution.py:216
  63.3 5.7 %collective-permute-start.5 = (bf16[16,2048]{1,0:T(8,128)(2,1)}, bf16[16,2048]{1,0:T(8,128)(2,1)}, u32[]{:S(2)}, u32[]{:S(2)}) collective-permute-start(bf16[16,2048]{1,0:T(8,128)(2,1)} %bitcast.30.refs_0_), channel_id=1, source_target_pairs={{0,6},{1,7},{2,0},{3,1},{4,2},{5,3},{6,4},{7,5},{8,14},{9,15},{10,... | collective-permute-start | bytes 196616 | tf_op jit(solution)/shard_map/ppermute | solution.py:216
  69.0 1.2 copy-start.7
  97.6 6.0 %collective-permute-start.6 = (f32[128,1024]{1,0:T(8,128)}, f32[128,1024]{1,0:T(8,128)}, u32[]{:S(2)}, u32[]{:S(2)}) collective-permute-start(f32[128,1024]{1,0:T(8,128)} %constant_dynamic-slice_fusion), channel_id=1, source_target_pairs={{0,1},{1,0},{2,3},{3,2},{4,5},{5,4},{6,7},{7,6},{8,9},{9,8},{10,11... | collective-permute-start | bytes 1572872 | tf_op jit(solution)/shard_map/ppermute | solution.py:240
  97.6 6.0 %copy-start.3 = (f32[256,1024]{1,0:T(8,128)S(1)}, f32[256,1024]{1,0:T(8,128)}, u32[]{:S(2)}) copy-start(f32[256,1024]{1,0:T(8,128)} %copy-done.2) | copy-start | bytes 3145732
  100.4 9.8 %collective-permute-start.13 = (f32[128,512]{1,0:T(8,128)}, f32[128,512]{1,0:T(8,128)}, u32[]{:S(2)}, u32[]{:S(2)}) collective-permute-start(f32[128,512]{1,0:T(8,128)} %get-tuple-element.11), channel_id=1, source_target_pairs={{0,6},{1,7},{2,0},{3,1},{4,2},{5,3},{6,4},{7,5},{8,14},{9,15},{10,... | collective-permute-start | bytes 786440 | tf_op jit(solution)/shard_map/ppermute | solution.py:230
  103.1 24.2 %collective-permute-start.12 = (f32[128,512]{1,0:T(8,128)}, f32[128,512]{1,0:T(8,128)}, u32[]{:S(2)}, u32[]{:S(2)}) collective-permute-start(f32[128,512]{1,0:T(8,128)} %get-tuple-element.12), channel_id=1, source_target_pairs={{0,4},{1,5},{2,6},{3,7},{4,0},{5,1},{6,2},{7,3},{8,12},{9,13},{10,... | collective-permute-start | bytes 786440 | tf_op jit(solution)/shard_map/ppermute | solution.py:230
  103.5 23.8 %collective-permute-start.11 = (f32[128,512]{1,0:T(8,128)S(1)}, f32[128,512]{1,0:T(8,128)}, u32[]{:S(2)}, u32[]{:S(2)}) collective-permute-start(f32[128,512]{1,0:T(8,128)S(1)} %get-tuple-element.10), channel_id=1, source_target_pairs={{0,2},{1,3},{2,4},{3,5},{4,6},{5,7},{6,0},{7,1},{8,10},{9,11},{10,... | collective-permute-start | bytes 786440 | tf_op jit(solution)/shard_map/ppermute | solution.py:230
  (2 other events, 2.0 us)
